TPU v7x, 512 devices: a whole 4x8x8 slice. The times are simulated.
512 devices in a mesh: dp: 32 (over y, x), ctx: 16 (over z, core).
Axes of the slice: x: 4, y: 8, z: 8, core: 2. Of those that a mesh axis runs over, the one named last changes fastest.
Arguments:
- xbc: bfloat16 [65536, 3328], P(('dp', 'ctx')), parts along dimension 0, may hold values from -6 to 6
- dt_raw: float32 [65536, 48], P(('dp', 'ctx')), parts along dimension 0, may hold values from -3 to 3
- lengths: int32 [256], P('dp'), parts along dimension 0, may hold values from 1 to 1024, 2048 in all
- conv_weight: float32 [4, 3328], replicated, may hold values from -3 to 3
- conv_bias: float32 [3328], replicated, may hold values from -3 to 3
- dt_bias: float32 [48], replicated, may hold values from -1 to 1
- decay_rate: float32 [48], replicated, may hold values from 0.0001 to 0.08
- skip: float32 [48], replicated, may hold values from 0.5 to 4
- norm_gain: float32 [3072], replicated, may hold values from 0.5 to 1.5
Outputs:
- mixed: bfloat16 [65536, 3072], P(('dp', 'ctx')), parts along dimension 0
There are 32 independent parts, one for each index of `dp`. A program takes and returns all parts, laid end to end along the dimension named above; an argument that names none is the same for every part. Nothing has to cross between parts.
Inputs may be any that keep to these rules, and one draw needn't show every extreme that they name: Documents lie end to end in order and their lengths sum to 2048; the longest is exactly 1024.
All inputs are finite; a program needn't handle non-finite values.
Results may differ from a plain program's by a relative error of at most 0.0036.
Values may be sent and summed in bfloat16 or wider, within the bound.
No kernel may reach another device: no remote copies, remote signals or barrier semaphores. Data moves between devices by JAX's collectives and lax.ppermute only.
A program may use at most 128 MiB of HBM per device.

v0:
```python
import jax
import jax.numpy as jnp
from jax import lax
from jax.sharding import PartitionSpec as P


def shifted(block, axis, distance):
    devices = range(lax.axis_size(axis))
    route = [(i - distance, i) for i in devices if i - distance in devices]
    return lax.ppermute(block, axis, route)


def carried_in(shard, axis, combine, identity):
    size, position = (lax.axis_size(axis), lax.axis_index(axis))
    everything = jax.tree.map(lambda part: lax.all_gather(part, axis), shard)
    start = jax.tree.map(
        lambda part, zero: jnp.broadcast_to(jnp.asarray(zero, part.dtype), part.shape),
        shard,
        identity,
    )

    def turn(k, before):
        reached = k < position
        new = combine(before, jax.tree.map(lambda part: part[k], everything))
        return jax.tree.map(lambda a, b: jnp.where(reached, a, b), new, before)

    return lax.fori_loop(0, size, turn, start)


def combine(earlier, later):
    return (earlier[0] * later[0], later[0][:, None, None] * earlier[1] + later[1])


def body(xbc, dt_raw, lengths, conv_weight, conv_bias, dt_bias, decay_rate, skip, norm_gain):
    rows = xbc.shape[0]
    heads = dt_raw.shape[1]
    inner_width = norm_gain.shape[0]
    head_dim = inner_width // heads
    state_dim = (xbc.shape[1] - inner_width) // 2
    taps = conv_weight.shape[0]
    device = lax.axis_index("ctx")
    first = device * rows
    ends = jnp.cumsum(lengths)
    places = first - (taps - 1) + jnp.arange(rows + taps - 1, dtype=jnp.int32)
    counted = jnp.sum((places[:, None] >= ends[None, :]).astype(jnp.int32), axis=1)
    seg_wide = jnp.where(places < 0, -1, counted)
    seg = seg_wide[taps - 1 :]
    start = seg != seg_wide[taps - 2 : -1]
    rim = shifted(xbc[rows - (taps - 1) :], "ctx", 1)
    widened = jnp.concatenate([rim, xbc], axis=0)
    total = conv_bias[None, :] + conv_weight[taps - 1][None, :] * xbc.astype(jnp.float32)
    for lag in range(1, taps):
        moved = widened[taps - 1 - lag : taps - 1 - lag + rows].astype(jnp.float32)
        same = seg_wide[taps - 1 - lag : taps - 1 - lag + rows] == seg
        total = total + conv_weight[taps - 1 - lag][None, :] * jnp.where(same[:, None], moved, 0.0)
    act = jax.nn.silu(total).astype(jnp.bfloat16)
    xs = act[:, :inner_width].reshape(rows, heads, head_dim)
    bs = act[:, inner_width : inner_width + state_dim]
    cs = act[:, inner_width + state_dim :]
    step_size = jax.nn.softplus(dt_raw + dt_bias[None, :])
    cum = jnp.cumsum(-step_size * decay_rate[None, :], axis=0)
    alive = (jnp.cumsum(start.astype(jnp.int32)) == 0).astype(jnp.float32)
    same_end = (seg == seg[-1]).astype(jnp.float32)
    factor = jnp.exp(cum[-1][None, :] - cum) * same_end[:, None] * step_size
    scaled = (factor[:, :, None] * xs.astype(jnp.float32)).astype(jnp.bfloat16)
    local = jnp.einsum("shp,sn->hpn", scaled, bs, preferred_element_type=jnp.float32)
    block_decay = jnp.exp(cum[-1]) * alive[-1]
    scores = jnp.dot(cs, bs.T, preferred_element_type=jnp.float32)
    index = jnp.arange(rows, dtype=jnp.int32)
    mask = (index[:, None] >= index[None, :]) & (seg[:, None] == seg[None, :])
    group = 8
    pieces = []
    for part_start in range(0, heads, group):
        cum_part = cum[:, part_start : part_start + group].T
        diff = cum_part[:, :, None] - cum_part[:, None, :]
        decay = jnp.where(mask[None], jnp.exp(jnp.where(mask[None], diff, 0.0)), 0.0)
        weights = (
            scores[None] * decay * step_size[:, part_start : part_start + group].T[:, None, :]
        ).astype(jnp.bfloat16)
        pieces.append(
            jnp.einsum(
                "hts,shp->thp",
                weights,
                xs[:, part_start : part_start + group, :],
                preferred_element_type=jnp.float32,
            )
        )
    inner = jnp.concatenate(pieces, axis=1)
    element = (block_decay, local)
    identity = (jnp.ones_like(block_decay), jnp.zeros_like(local))
    carry = carried_in(element, "ctx", combine, identity)[1]
    carried = carry.astype(jnp.bfloat16)
    outer = (
        jnp.exp(cum)[:, :, None]
        * alive[:, None, None]
        * jnp.einsum("hpn,tn->thp", carried, cs, preferred_element_type=jnp.float32)
    )
    total_out = inner + outer + skip[None, :, None] * xs.astype(jnp.float32)
    normed = (
        total_out
        * lax.rsqrt(jnp.mean(total_out * total_out, axis=-1, keepdims=True) + 1e-05)
        * norm_gain.reshape(heads, head_dim)[None]
    )
    return normed.astype(jnp.bfloat16).reshape(rows, inner_width)


def solution(mesh):
    in_specs = (
        P(("dp", "ctx"), None),
        P(("dp", "ctx"), None),
        P("dp"),
        P(),
        P(),
        P(),
        P(),
        P(),
        P(),
    )
    out_specs = P(("dp", "ctx"), None)
    return jax.shard_map(body, mesh=mesh, in_specs=in_specs, out_specs=out_specs, check_vma=False)
```

profile of v0, /device:TPU:1, one launch (start us, length us, event | category | flops | bytes accessed | tf_op | source)
XLA Modules:
  0.0 206.8 jit_solution(6009375544493127728)
XLA Ops:
  7.4 5.4 %collective-permute-start = (bf16[3,3328]{1,0:T(4,128)(2,1)S(1)}, bf16[3,3328]{1,0:T(4,128)(2,1)S(1)}, u32[]{:S(2)}, u32[]{:S(2)}) collective-permute-start(bf16[3,3328]{1,0:T(4,128)(2,1)S(1)} %slice.116), channel_id=1, source_target_pairs={{0,1},{1,2},{2,3},{3,4},{4,5},{5,6},{6,7},{7,8},{8,9},{9,10},{10,1... | collective-permute-start | bytes 59912 | tf_op jit(solution)/shard_map/ppermute | solution.py:10
  17.8 1.2 slice_bitcast_fusion.12
  19.0 1.1 slice_reduce_fusion.3
  20.2 2.6 %multiply_convert_fusion = bf16[128,3328]{1,0:T(8,128)(2,1)S(1)} fusion(bf16[128,3328]{1,0:T(8,128)(2,1)S(1)} %copy-done, bf16[3,3328]{1,0:T(4,128)(2,1)S(1)} %collective-permute-done, f32[3328]{0:T(1024)S(1)} %get-tuple-element.120, f32[3328]{0:T(1024)S(1)} %get-tuple-element.121, f32[3328]{0:T(1024)S(1)} %get-tuple-element.119, ...), kind=kLoop, calls=%fused_computation.5 | loop fusion | flops 12353536 | bytes 1790848 | tf_op jit(solution)/shard_map/convert_element_type | solution.py:56
  23.3 1.6 fusion.11
  34.7 21.1 %all-gather.1 = f32[16,1,48]{2,1,0:T(1,128)S(1)} all-gather(f32[1,1,48]{2,1,0:T(1,128)} %get-tuple-element.137), channel_id=1, replica_groups=mesh['dp'=32,'ctx'=16] {'ctx'}, dimensions={0}, use_global_device_ids=true | all-gather | bytes 3264 | tf_op jit(solution)/shard_map/all_gather | solution.py:15
  56.8 1.8 fusion.8
  58.6 1.1 fusion.7
  59.6 1.1 fusion.6
  60.7 1.1 fusion.5
  61.8 1.1 fusion.4
  62.9 1.1 fusion.3
  63.9 103.2 %all-gather.4.cloned.1.call-done = f32[768,64,128]{2,1,0:T(8,128)} async-done(((f32[48,64,128]{2,1,0:T(8,128)}), f32[768,64,128]{2,1,0:T(8,128)}) %all-gather.4.cloned.1.call-update) | async-done | bytes 25165840 | tf_op jit(solution)/shard_map/all_gather | solution.py:15
  167.1 29.1 %while.14 = (s32[]{:T(128)}, f32[48,64,128]{2,1,0:T(8,128)S(1)}, s32[]{:T(128)}, f32[16,48]{1,0:T(8,128)S(1)}, f32[16,48,64,128]{3,2,1,0:T(8,128)}, /*index=5*/s32[]{:T(128)}, s32[]{:T(128)}) while((s32[]{:T(128)}, f32[48,64,128]{2,1,0:T(8,128)S(1)}, s32[]{:T(128)}, f32[16,48]{1,0:T(8,128)S(1)}, f32[16,48,64,128]{3,2,1,0:T(8,128)}, ...), condition=%wide.region_5.6_spmd.clone, body=%wide.region_4.5_spmd.clone.sunk | while | flops 1572868 | bytes 4719281 | solution.py:27
  167.1 1.8 fusion.74
  169.0 1.8 fusion.74
  170.8 1.8 fusion.74
  172.6 1.8 fusion.74
  174.4 1.8 fusion.74
  176.2 1.8 fusion.74
  178.1 1.8 fusion.74
  179.9 1.8 fusion.74
  181.7 1.8 fusion.74
  183.5 1.8 fusion.74
  185.3 1.8 fusion.74
  187.1 1.8 fusion.74
  189.0 1.8 fusion.74
  190.8 1.8 fusion.74
  192.6 1.8 fusion.74
  194.4 1.8 fusion.74
  196.2 2.0 multiply_reduce_fusion
  198.8 1.2 copy.105
  (72 shorter events, 17.8 us)
Async XLA Ops:
  6.5 13.7 %copy-start = (bf16[128,3328]{1,0:T(8,128)(2,1)S(1)}, bf16[128,3328]{1,0:T(8,128)(2,1)}, u32[]{:S(2)}) copy-start(bf16[128,3328]{1,0:T(8,128)(2,1)} %param.11) | copy-start | bytes 2555908
  6.5 160.6 %all-gather.4.cloned.1.call-start = ((), (), s32[]{:S(2)}) async-start(), calls=%async_computation | async-start | bytes 26738688 | tf_op jit(solution)/shard_map/all_gather | solution.py:15
  7.4 12.8 %collective-permute-start = (bf16[3,3328]{1,0:T(4,128)(2,1)S(1)}, bf16[3,3328]{1,0:T(4,128)(2,1)S(1)}, u32[]{:S(2)}, u32[]{:S(2)}) collective-permute-start(bf16[3,3328]{1,0:T(4,128)(2,1)S(1)} %slice.116), channel_id=1, source_target_pairs={{0,1},{1,2},{2,3},{3,4},{4,5},{5,6},{6,7},{7,8},{8,9},{9,10},{10,1... | collective-permute-start | bytes 59912 | tf_op jit(solution)/shard_map/ppermute | solution.py:10
  23.3 2.3 %copy-start.3 = (f32[3072]{0:T(1024)S(1)}, f32[3072]{0:T(1024)}, u32[]{:S(2)}) copy-start(f32[3072]{0:T(1024)} %param.19) | copy-start | bytes 36868
  32.6 26.0 %copy-start.4 = (f32[8,128]{1,0:T(8,128)S(1)}, f32[8,128]{1,0:T(8,128)}, u32[]{:S(2)}) copy-start(f32[8,128]{1,0:T(8,128)} %copy.89) | copy-start | bytes 12292
  167.1 29.1 %copy-start.2 = (f32[128,48]{0,1:T(8,128)S(1)}, f32[128,48]{0,1:T(8,128)}, u32[]{:S(2)}) copy-start(f32[128,48]{0,1:T(8,128)} %copy.103) | copy-start | bytes 73732
  167.1 29.1 %copy-start.5 = (f32[48]{0:T(128)S(1)}, f32[48]{0:T(128)}, u32[]{:S(2)}) copy-start(f32[48]{0:T(128)} %param.18) | copy-start | bytes 580
  196.2 2.0 copy-start.1
Sparse Core Ops, SparseCore 0:
  25.0 142.0 all-gather.3
where the time goes:
time: 208 us; the launch traced here: 207 us
  waiting for transfers between devices  103 us (50%)
  other arithmetic  36.4 us (18%)
  blocking collectives  21.1 us (10%)
  local copies, waits for them, and re-layouts  15.6 us (8%)
  between operations  13.6 us (7%)
  matrix products  10.9 us (5%)
  starting transfers between devices  5.39 us (3%)
    all_gather x1, waiting for transfers between devices, carried_in(): everything = jax.tree.map(lambda part: lax.all_gather(part, axis), shard)  103 us
    select_n x16, other arithmetic, turn(): return jax.tree.map(lambda a, b: jnp.where(reached, a, b), new, before)  28.3 us
    all_gather x1, blocking collectives, carried_in(): everything = jax.tree.map(lambda part: lax.all_gather(part, axis), shard)  21.1 us
    dot_general x6, matrix products, body(): jnp.einsum('hts,shp->thp', weights, xs[:, part_start:part_start + group,...  7.13 us
    ppermute x1, starting transfers between devices, shifted(): return lax.ppermute(block, axis, route)  5.39 us
    transpose x7, local copies, waits for them, and re-layouts, body(): step_size[:, part_start:part_start + group].T[:, None, :]  4.89 us
  transfers between devices with their start and end apart: 2, of which 1 were waited for; matrix products, arithmetic and copies ran while one was open for 12% of the time, Pallas kernels for 0%

commit v1 on v0

--- a/solution.py
+++ b/solution.py
@@ -10,25 +10,33 @@
     return lax.ppermute(block, axis, route)
 
 
-def carried_in(shard, axis, combine, identity):
-    size, position = (lax.axis_size(axis), lax.axis_index(axis))
-    everything = jax.tree.map(lambda part: lax.all_gather(part, axis), shard)
-    start = jax.tree.map(
-        lambda part, zero: jnp.broadcast_to(jnp.asarray(zero, part.dtype), part.shape),
-        shard,
-        identity,
-    )
-
-    def turn(k, before):
-        reached = k < position
-        new = combine(before, jax.tree.map(lambda part: part[k], everything))
-        return jax.tree.map(lambda a, b: jnp.where(reached, a, b), new, before)
-
-    return lax.fori_loop(0, size, turn, start)
-
-
-def combine(earlier, later):
-    return (earlier[0] * later[0], later[0][:, None, None] * earlier[1] + later[1])
+def chain_carry(decay, local, chunks):
+    size, position = (lax.axis_size("ctx"), lax.axis_index("ctx"))
+    chips = size // 2
+    chip = position // 2
+    heads = decay.shape[0]
+    width = heads // chunks
+    up = [(2 * i, 2 * i + 1) for i in range(chips)]
+    down = [(2 * i + 1, 2 * i) for i in range(chips)]
+    ahead = [(2 * i + 1, 2 * i + 3) for i in range(chips - 1)]
+    decay_low, local_low = lax.ppermute((decay, local), "ctx", up)
+    chip_decay = decay * decay_low
+    chip_local = decay[:, None, None] * local_low + local
+    received = jnp.zeros((width,) + local.shape[1:], local.dtype)
+    carry = jnp.zeros_like(local)
+    for step in range(chunks + chips - 1):
+        k = step - chip
+        valid = (k >= 0) & (k < chunks)
+        at = jnp.clip(k, 0, chunks - 1) * width
+        old = lax.dynamic_slice_in_dim(carry, at, width, 0)
+        carry = lax.dynamic_update_slice_in_dim(carry, jnp.where(valid, received, old), at, 0)
+        if step < chunks + chips - 2:
+            d = lax.dynamic_slice_in_dim(chip_decay, at, width, 0)
+            l = lax.dynamic_slice_in_dim(chip_local, at, width, 0)
+            received = lax.ppermute(d[:, None, None] * received + l, "ctx", ahead)
+    lowered = lax.ppermute(carry, "ctx", down)
+    own = decay_low[:, None, None] * carry + local_low
+    return jnp.where(position % 2 == 0, lowered, own)
 
 
 def body(xbc, dt_raw, lengths, conv_weight, conv_bias, dt_bias, decay_rate, skip, norm_gain):
@@ -86,9 +94,7 @@
             )
         )
     inner = jnp.concatenate(pieces, axis=1)
-    element = (block_decay, local)
-    identity = (jnp.ones_like(block_decay), jnp.zeros_like(local))
-    carry = carried_in(element, "ctx", combine, identity)[1]
+    carry = chain_carry(block_decay, local, 4)
     carried = carry.astype(jnp.bfloat16)
     outer = (
         jnp.exp(cum)[:, :, None]

time: 208 us -> 154 us (0.74)
  the two profiles are of different devices: /device:TPU:1 before, /device:TPU:127 now
where the time goes in v1:
time: 154 us; the launch traced here: 153 us
  starting transfers between devices  56 us (36%)
  waiting for transfers between devices  45 us (29%)
  other arithmetic  26.6 us (17%)
  local copies, waits for them, and re-layouts  18.7 us (12%)
  matrix products  5.63 us (4%)
    ppermute x10, starting transfers between devices, chain_carry(): received = lax.ppermute(d[:, None, None] * received + l, 'ctx', ahead)  47.5 us
    ppermute x10, waiting for transfers between devices, chain_carry(): received = lax.ppermute(d[:, None, None] * received + l, 'ctx', ahead)  41.8 us
    add x10, other arithmetic, chain_carry(): received = lax.ppermute(d[:, None, None] * received + l, 'ctx', ahead)  15.7 us
    transpose x7, local copies, waits for them, and re-layouts, body(): step_size[:, part_start:part_start + group].T[:, None, :]  6.65 us
    ppermute x1, starting transfers between devices, shifted(): return lax.ppermute(block, axis, route)  4.56 us
    transpose x7, local copies, waits for them, and re-layouts, body(): cum_part = cum[:, part_start:part_start + group].T  3.96 us
  transfers between devices with their start and end apart: 14, of which 11 were waited for; matrix products, arithmetic and copies ran while one was open for 16% of the time, Pallas kernels for 0%

profile of v1, /device:TPU:127, one launch (start us, length us, event | category | flops | bytes accessed | tf_op | source)
XLA Modules:
  0.0 152.6 jit_solution(5931358091945540497)
XLA Ops:
  0.9 4.6 %collective-permute-start = (bf16[3,3328]{1,0:T(4,128)(2,1)S(1)}, bf16[3,3328]{1,0:T(4,128)(2,1)S(1)}, u32[]{:S(2)}, u32[]{:S(2)}) collective-permute-start(bf16[3,3328]{1,0:T(4,128)(2,1)S(1)} %slice.116), channel_id=1, source_target_pairs={{0,1},{1,2},{2,3},{3,4},{4,5},{5,6},{6,7},{7,8},{8,9},{9,10},{10,1... | collective-permute-start | bytes 59912 | tf_op jit(solution)/shard_map/ppermute | solution.py:10
  11.8 2.6 %multiply_convert_fusion = bf16[128,3328]{1,0:T(8,128)(2,1)S(1)} fusion(bf16[128,3328]{1,0:T(8,128)(2,1)S(1)} %copy-done.4, bf16[3,3328]{1,0:T(4,128)(2,1)S(1)} %collective-permute-done, f32[3328]{0:T(1024)S(1)} %get-tuple-element.7, f32[3328]{0:T(1024)S(1)} %get-tuple-element.8, f32[3328]{0:T(1024)S(1)} %get-tuple-element.6, f32[3328]{0:T(1024)S(1)} %get-tuple-element.5, ...), kind=kLoop, calls=%fused_computation.2 | loop fusion | flops 12353536 | bytes 1790848 | tf_op jit(solution)/shard_map/convert_element_type | solution.py:64
  19.1 2.8 %collective-permute-done.1 = f32[48]{0:T(128)S(1)} collective-permute-done((f32[48]{0:T(128)S(1)}, f32[48]{0:T(128)S(1)}, u32[]{:S(2)}, u32[]{:S(2)}) %collective-permute-start.1) | collective-permute-done | bytes 224 | tf_op jit(solution)/shard_map/ppermute | solution.py:22
  23.7 2.1 %multiply_add_fusion = f32[48,64,128]{2,1,0:T(8,128)S(1)} fusion(f32[48,64,128]{2,1,0:T(8,128)} %copy-done.2, f32[48,64,128]{2,1,0:T(8,128)} %collective-permute-done.2, f32[48]{0:T(128)S(1)} %exponential_multiply_fusion.1), kind=kLoop, calls=%fused_computation.8 | loop fusion | flops 786432 | bytes 4718784 | tf_op jit(solution)/shard_map/add | solution.py:24
  26.6 4.0 %collective-permute-start.3 = (f32[12,64,128]{2,1,0:T(8,128)}, f32[12,64,128]{2,1,0:T(8,128)}, u32[]{:S(2)}, u32[]{:S(2)}) collective-permute-start(f32[12,64,128]{2,1,0:T(8,128)} %dynamic-slice_add_fusion.9), channel_id=1, source_target_pairs={{1,3},{3,5},{5,7},{7,9},{9,11},{11,13},{13,15},{17,19},{19,21},{21... | collective-permute-start | bytes 1179656 | tf_op jit(solution)/shard_map/ppermute | solution.py:36
  30.9 4.8 %collective-permute-done.3 = f32[12,64,128]{2,1,0:T(8,128)} collective-permute-done((f32[12,64,128]{2,1,0:T(8,128)}, f32[12,64,128]{2,1,0:T(8,128)}, u32[]{:S(2)}, u32[]{:S(2)}) %collective-permute-start.3) | collective-permute-done | bytes 393248 | tf_op jit(solution)/shard_map/ppermute | solution.py:36
  35.7 1.8 %dynamic-slice_add_fusion.8 = (f32[12,64,128]{2,1,0:T(8,128)}, f32[48,64,128]{2,1,0:T(8,128)S(1)}) fusion(f32[48,64,128]{2,1,0:T(8,128)S(1)} %multiply_add_fusion, s32[]{:T(128)S(6)} %select_n.230, f32[12,64,128]{2,1,0:T(8,128)} %collective-permute-done.3, f32[12]{0:T(128)S(1)} %get-tuple-element.56, ...), kind=kLoop, calls=%fused_computation.53 | loop fusion | flops 294912 | bytes 1966597 | tf_op jit(solution)/shard_map/add | solution.py:36
  37.5 5.2 %collective-permute-start.4 = (f32[12,64,128]{2,1,0:T(8,128)}, f32[12,64,128]{2,1,0:T(8,128)}, u32[]{:S(2)}, u32[]{:S(2)}) collective-permute-start(f32[12,64,128]{2,1,0:T(8,128)} %get-tuple-element.27), channel_id=1, source_target_pairs={{1,3},{3,5},{5,7},{7,9},{9,11},{11,13},{13,15},{17,19},{19,21},{21... | collective-permute-start | bytes 1179656 | tf_op jit(solution)/shard_map/ppermute | solution.py:36
  42.7 5.0 %collective-permute-done.4 = f32[12,64,128]{2,1,0:T(8,128)} collective-permute-done((f32[12,64,128]{2,1,0:T(8,128)}, f32[12,64,128]{2,1,0:T(8,128)}, u32[]{:S(2)}, u32[]{:S(2)}) %collective-permute-start.4) | collective-permute-done | bytes 393248 | tf_op jit(solution)/shard_map/ppermute | solution.py:36
  47.7 1.8 %dynamic-slice_add_fusion.7 = (f32[12,64,128]{2,1,0:T(8,128)}, f32[48,64,128]{2,1,0:T(8,128)S(1)}) fusion(f32[48,64,128]{2,1,0:T(8,128)S(1)} %multiply_add_fusion, s32[]{:T(128)S(6)} %select_n.233, f32[12,64,128]{2,1,0:T(8,128)} %collective-permute-done.4, f32[12]{0:T(128)S(1)} %get-tuple-element.55, f32[48,64,128]{2,1,0:T(8,128)S(1)} %get-tuple-element.28, ...), kind=kLoop, calls=%fused_computation.51 | loop fusion | flops 294912 | bytes 1966597 | tf_op jit(solution)/shard_map/add | solution.py:36
  49.6 3.8 %collective-permute-start.5 = (f32[12,64,128]{2,1,0:T(8,128)}, f32[12,64,128]{2,1,0:T(8,128)}, u32[]{:S(2)}, u32[]{:S(2)}) collective-permute-start(f32[12,64,128]{2,1,0:T(8,128)} %get-tuple-element.25), channel_id=1, source_target_pairs={{1,3},{3,5},{5,7},{7,9},{9,11},{11,13},{13,15},{17,19},{19,21},{21... | collective-permute-start | bytes 1179656 | tf_op jit(solution)/shard_map/ppermute | solution.py:36
  53.4 5.0 %collective-permute-done.5 = f32[12,64,128]{2,1,0:T(8,128)} collective-permute-done((f32[12,64,128]{2,1,0:T(8,128)}, f32[12,64,128]{2,1,0:T(8,128)}, u32[]{:S(2)}, u32[]{:S(2)}) %collective-permute-start.5) | collective-permute-done | bytes 393248 | tf_op jit(solution)/shard_map/ppermute | solution.py:36
  58.4 1.8 %dynamic-slice_add_fusion.6 = (f32[12,64,128]{2,1,0:T(8,128)}, f32[48,64,128]{2,1,0:T(8,128)S(1)}) fusion(f32[48,64,128]{2,1,0:T(8,128)S(1)} %multiply_add_fusion, s32[]{:T(128)S(6)} %select_n.236, f32[12,64,128]{2,1,0:T(8,128)} %collective-permute-done.5, f32[12]{0:T(128)S(1)} %get-tuple-element.54, f32[48,64,128]{2,1,0:T(8,128)S(1)} %get-tuple-element.26, ...), kind=kLoop, calls=%fused_computation.49 | loop fusion | flops 294912 | bytes 1966597 | tf_op jit(solution)/shard_map/add | solution.py:36
  60.2 4.3 %collective-permute-start.6 = (f32[12,64,128]{2,1,0:T(8,128)}, f32[12,64,128]{2,1,0:T(8,128)}, u32[]{:S(2)}, u32[]{:S(2)}) collective-permute-start(f32[12,64,128]{2,1,0:T(8,128)} %get-tuple-element.23), channel_id=1, source_target_pairs={{1,3},{3,5},{5,7},{7,9},{9,11},{11,13},{13,15},{17,19},{19,21},{21... | collective-permute-start | bytes 1179656 | tf_op jit(solution)/shard_map/ppermute | solution.py:36
  64.6 5.0 %collective-permute-done.6 = f32[12,64,128]{2,1,0:T(8,128)} collective-permute-done((f32[12,64,128]{2,1,0:T(8,128)}, f32[12,64,128]{2,1,0:T(8,128)}, u32[]{:S(2)}, u32[]{:S(2)}) %collective-permute-start.6) | collective-permute-done | bytes 393248 | tf_op jit(solution)/shard_map/ppermute | solution.py:36
  69.6 1.8 %dynamic-slice_add_fusion.5 = (f32[12,64,128]{2,1,0:T(8,128)}, f32[48,64,128]{2,1,0:T(8,128)S(1)}) fusion(f32[48,64,128]{2,1,0:T(8,128)S(1)} %multiply_add_fusion, s32[]{:T(128)S(6)} %select_n.239, f32[12,64,128]{2,1,0:T(8,128)} %collective-permute-done.6, f32[12]{0:T(128)S(1)} %get-tuple-element.53, f32[48,64,128]{2,1,0:T(8,128)S(1)} %get-tuple-element.24, ...), kind=kLoop, calls=%fused_computation.47 | loop fusion | flops 294912 | bytes 1966597 | tf_op jit(solution)/shard_map/add | solution.py:36
  71.4 5.0 %collective-permute-start.7 = (f32[12,64,128]{2,1,0:T(8,128)}, f32[12,64,128]{2,1,0:T(8,128)}, u32[]{:S(2)}, u32[]{:S(2)}) collective-permute-start(f32[12,64,128]{2,1,0:T(8,128)} %get-tuple-element.21), channel_id=1, source_target_pairs={{1,3},{3,5},{5,7},{7,9},{9,11},{11,13},{13,15},{17,19},{19,21},{21... | collective-permute-start | bytes 1179656 | tf_op jit(solution)/shard_map/ppermute | solution.py:36
  76.4 5.0 %collective-permute-done.7 = f32[12,64,128]{2,1,0:T(8,128)} collective-permute-done((f32[12,64,128]{2,1,0:T(8,128)}, f32[12,64,128]{2,1,0:T(8,128)}, u32[]{:S(2)}, u32[]{:S(2)}) %collective-permute-start.7) | collective-permute-done | bytes 393248 | tf_op jit(solution)/shard_map/ppermute | solution.py:36
  81.4 1.8 %dynamic-slice_add_fusion.4 = (f32[12,64,128]{2,1,0:T(8,128)}, f32[48,64,128]{2,1,0:T(8,128)S(1)}) fusion(f32[48,64,128]{2,1,0:T(8,128)S(1)} %multiply_add_fusion, s32[]{:T(128)S(6)} %select_n.242, f32[12,64,128]{2,1,0:T(8,128)} %collective-permute-done.7, f32[12]{0:T(128)S(1)} %get-tuple-element.52, f32[48,64,128]{2,1,0:T(8,128)S(1)} %get-tuple-element.22, ...), kind=kLoop, calls=%fused_computation.45 | loop fusion | flops 294912 | bytes 1966597 | tf_op jit(solution)/shard_map/add | solution.py:36
  83.3 5.0 %collective-permute-start.8 = (f32[12,64,128]{2,1,0:T(8,128)}, f32[12,64,128]{2,1,0:T(8,128)}, u32[]{:S(2)}, u32[]{:S(2)}) collective-permute-start(f32[12,64,128]{2,1,0:T(8,128)} %get-tuple-element.19), channel_id=1, source_target_pairs={{1,3},{3,5},{5,7},{7,9},{9,11},{11,13},{13,15},{17,19},{19,21},{21... | collective-permute-start | bytes 1179656 | tf_op jit(solution)/shard_map/ppermute | solution.py:36
  88.3 5.0 %collective-permute-done.8 = f32[12,64,128]{2,1,0:T(8,128)} collective-permute-done((f32[12,64,128]{2,1,0:T(8,128)}, f32[12,64,128]{2,1,0:T(8,128)}, u32[]{:S(2)}, u32[]{:S(2)}) %collective-permute-start.8) | collective-permute-done | bytes 393248 | tf_op jit(solution)/shard_map/ppermute | solution.py:36
  93.3 1.8 %dynamic-slice_add_fusion.3 = (f32[12,64,128]{2,1,0:T(8,128)}, f32[48,64,128]{2,1,0:T(8,128)S(1)}) fusion(f32[48,64,128]{2,1,0:T(8,128)S(1)} %multiply_add_fusion, s32[]{:T(128)S(6)} %select_n.245, f32[12,64,128]{2,1,0:T(8,128)} %collective-permute-done.8, f32[12]{0:T(128)S(1)} %get-tuple-element.51, f32[48,64,128]{2,1,0:T(8,128)S(1)} %get-tuple-element.20, ...), kind=kLoop, calls=%fused_computation.43 | loop fusion | flops 294912 | bytes 1966597 | tf_op jit(solution)/shard_map/add | solution.py:36
  95.2 5.0 %collective-permute-start.9 = (f32[12,64,128]{2,1,0:T(8,128)}, f32[12,64,128]{2,1,0:T(8,128)}, u32[]{:S(2)}, u32[]{:S(2)}) collective-permute-start(f32[12,64,128]{2,1,0:T(8,128)} %get-tuple-element.17), channel_id=1, source_target_pairs={{1,3},{3,5},{5,7},{7,9},{9,11},{11,13},{13,15},{17,19},{19,21},{21... | collective-permute-start | bytes 1179656 | tf_op jit(solution)/shard_map/ppermute | solution.py:36
  100.8 4.4 %collective-permute-done.9 = f32[12,64,128]{2,1,0:T(8,128)} collective-permute-done((f32[12,64,128]{2,1,0:T(8,128)}, f32[12,64,128]{2,1,0:T(8,128)}, u32[]{:S(2)}, u32[]{:S(2)}) %collective-permute-start.9) | collective-permute-done | bytes 393248 | tf_op jit(solution)/shard_map/ppermute | solution.py:36
  105.2 1.8 %dynamic-slice_add_fusion.2 = (f32[12,64,128]{2,1,0:T(8,128)}, f32[48,64,128]{2,1,0:T(8,128)S(1)}) fusion(f32[48,64,128]{2,1,0:T(8,128)S(1)} %multiply_add_fusion, s32[]{:T(128)S(6)} %select_n.248, f32[12,64,128]{2,1,0:T(8,128)} %collective-permute-done.9, f32[12]{0:T(128)S(1)} %get-tuple-element.50, f32[48,64,128]{2,1,0:T(8,128)S(1)} %get-tuple-element.18, ...), kind=kLoop, calls=%fused_computation.41 | loop fusion | flops 294912 | bytes 1966597 | tf_op jit(solution)/shard_map/add | solution.py:36
  107.1 5.1 %collective-permute-start.10 = (f32[12,64,128]{2,1,0:T(8,128)}, f32[12,64,128]{2,1,0:T(8,128)}, u32[]{:S(2)}, u32[]{:S(2)}) collective-permute-start(f32[12,64,128]{2,1,0:T(8,128)} %get-tuple-element.15), channel_id=1, source_target_pairs={{1,3},{3,5},{5,7},{7,9},{9,11},{11,13},{13,15},{17,19},{19,21},{21... | collective-permute-start | bytes 1179656 | tf_op jit(solution)/shard_map/ppermute | solution.py:36
  115.3 1.5 copy.62
  125.1 5.0 %collective-permute-start.11 = (f32[12,64,128]{2,1,0:T(8,128)S(1)}, f32[12,64,128]{2,1,0:T(8,128)S(1)}, u32[]{:S(2)}, u32[]{:S(2)}) collective-permute-start(f32[12,64,128]{2,1,0:T(8,128)S(1)} %get-tuple-element.13), channel_id=1, source_target_pairs={{1,3},{3,5},{5,7},{7,9},{9,11},{11,13},{13,15},{17,19},{19,21},{21... | collective-permute-start | bytes 1179656 | tf_op jit(solution)/shard_map/ppermute | solution.py:36
  131.1 3.7 %collective-permute-done.11 = f32[12,64,128]{2,1,0:T(8,128)S(1)} collective-permute-done((f32[12,64,128]{2,1,0:T(8,128)S(1)}, f32[12,64,128]{2,1,0:T(8,128)S(1)}, u32[]{:S(2)}, u32[]{:S(2)}) %collective-permute-start.11) | collective-permute-done | bytes 393248 | tf_op jit(solution)/shard_map/ppermute | solution.py:36
  135.5 5.0 %collective-permute-start.12 = (f32[12,64,128]{2,1,0:T(8,128)S(1)}, f32[12,64,128]{2,1,0:T(8,128)S(1)}, u32[]{:S(2)}, u32[]{:S(2)}) collective-permute-start(f32[12,64,128]{2,1,0:T(8,128)S(1)} %get-tuple-element.11), channel_id=1, source_target_pairs={{1,3},{3,5},{5,7},{7,9},{9,11},{11,13},{13,15},{17,19},{19,21},{21... | collective-permute-start | bytes 1179656 | tf_op jit(solution)/shard_map/ppermute | solution.py:36
  141.3 3.9 %collective-permute-done.12 = f32[12,64,128]{2,1,0:T(8,128)S(1)} collective-permute-done((f32[12,64,128]{2,1,0:T(8,128)S(1)}, f32[12,64,128]{2,1,0:T(8,128)S(1)}, u32[]{:S(2)}, u32[]{:S(2)}) %collective-permute-start.12) | collective-permute-done | bytes 393248 | tf_op jit(solution)/shard_map/ppermute | solution.py:36
  148.7 2.2 %multiply_reduce_fusion = (f32[128,48]{0,1:T(8,128)S(1)}, f32[128,48,64]{0,2,1:T(8,128)S(1)}) fusion(bf16[128,48,64]{0,2,1:T(8,128)(2,1)S(1)} %bitcast.83, f32[48]{0:T(128)S(1)} %copy-done.13, f32[128,48,64]{0,2,1:T(8,128)S(1)} %fusion.2, bf16[48,64,128]{2,1,0:T(8,128)(2,1)S(1)} %collective-permute-done.13, f32[48,64,128]{2,1,0:T(8,128)} %collective-permute-done.2, ...), kind=kOutput, calls=%fused_computation.6 | convolution fusion | flops 104589312 | bytes 7946625 | tf_op jit(solution)/shard_map/hpn,tn->thp/dot_general | solution.py:102
  (94 shorter events, 33.9 us)
Async XLA Ops:
  0.0 11.8 %copy-start.4 = (bf16[128,3328]{1,0:T(8,128)(2,1)S(1)}, bf16[128,3328]{1,0:T(8,128)(2,1)}, u32[]{:S(2)}) copy-start(bf16[128,3328]{1,0:T(8,128)(2,1)} %param.9) | copy-start | bytes 2555908
  0.9 10.8 %collective-permute-start = (bf16[3,3328]{1,0:T(4,128)(2,1)S(1)}, bf16[3,3328]{1,0:T(4,128)(2,1)S(1)}, u32[]{:S(2)}, u32[]{:S(2)}) collective-permute-start(bf16[3,3328]{1,0:T(4,128)(2,1)S(1)} %slice.116), channel_id=1, source_target_pairs={{0,1},{1,2},{2,3},{3,4},{4,5},{5,6},{6,7},{7,8},{8,9},{9,10},{10,1... | collective-permute-start | bytes 59912 | tf_op jit(solution)/shard_map/ppermute | solution.py:10
  14.4 9.3 %copy-start.3 = (bf16[128,3328]{1,0:T(8,128)(2,1)}, bf16[128,3328]{1,0:T(8,128)(2,1)S(1)}, u32[]{:S(2)}) copy-start(bf16[128,3328]{1,0:T(8,128)(2,1)S(1)} %multiply_convert_fusion) | copy-start | bytes 2555908
  14.9 10.9 %copy-start = (bf16[128,3072]{0,1:T(8,128)(2,1)}, bf16[128,3072]{0,1:T(8,128)(2,1)S(1)}, u32[]{:S(2)}) copy-start(bf16[128,3072]{0,1:T(8,128)(2,1)S(1)} %copy.58) | copy-start | bytes 2359300
  15.2 8.5 %copy-start.2 = (f32[48,64,128]{2,1,0:T(8,128)}, f32[48,64,128]{2,1,0:T(8,128)S(1)}, u32[]{:S(2)}) copy-start(f32[48,64,128]{2,1,0:T(8,128)S(1)} %fusion.10) | copy-start | bytes 4718596
  15.2 8.4 %collective-permute-start.2 = (f32[48,64,128]{2,1,0:T(8,128)S(1)}, f32[48,64,128]{2,1,0:T(8,128)}, u32[]{:S(2)}, u32[]{:S(2)}) collective-permute-start(f32[48,64,128]{2,1,0:T(8,128)S(1)} %fusion.10), channel_id=1, source_target_pairs={{0,1},{2,3},{4,5},{6,7},{8,9},{10,11},{12,13},{14,15},{16,17},{18,... | collective-permute-start | bytes 4718600 | tf_op jit(solution)/shard_map/ppermute | solution.py:22
  17.7 4.2 %collective-permute-start.1 = (f32[48]{0:T(128)S(1)}, f32[48]{0:T(128)S(1)}, u32[]{:S(2)}, u32[]{:S(2)}) collective-permute-start(f32[48]{0:T(128)S(1)} %exponential_multiply_fusion.1), channel_id=1, source_target_pairs={{0,1},{2,3},{4,5},{6,7},{8,9},{10,11},{12,13},{14,15},{16,17},{18,... | collective-permute-start | bytes 584 | tf_op jit(solution)/shard_map/ppermute | solution.py:22
  21.9 0.5 copy-start.10
  26.6 9.0 %collective-permute-start.3 = (f32[12,64,128]{2,1,0:T(8,128)}, f32[12,64,128]{2,1,0:T(8,128)}, u32[]{:S(2)}, u32[]{:S(2)}) collective-permute-start(f32[12,64,128]{2,1,0:T(8,128)} %dynamic-slice_add_fusion.9), channel_id=1, source_target_pairs={{1,3},{3,5},{5,7},{7,9},{9,11},{11,13},{13,15},{17,19},{19,21},{21... | collective-permute-start | bytes 1179656 | tf_op jit(solution)/shard_map/ppermute | solution.py:36
  37.5 10.2 %collective-permute-start.4 = (f32[12,64,128]{2,1,0:T(8,128)}, f32[12,64,128]{2,1,0:T(8,128)}, u32[]{:S(2)}, u32[]{:S(2)}) collective-permute-start(f32[12,64,128]{2,1,0:T(8,128)} %get-tuple-element.27), channel_id=1, source_target_pairs={{1,3},{3,5},{5,7},{7,9},{9,11},{11,13},{13,15},{17,19},{19,21},{21... | collective-permute-start | bytes 1179656 | tf_op jit(solution)/shard_map/ppermute | solution.py:36
  49.6 8.8 %collective-permute-start.5 = (f32[12,64,128]{2,1,0:T(8,128)}, f32[12,64,128]{2,1,0:T(8,128)}, u32[]{:S(2)}, u32[]{:S(2)}) collective-permute-start(f32[12,64,128]{2,1,0:T(8,128)} %get-tuple-element.25), channel_id=1, source_target_pairs={{1,3},{3,5},{5,7},{7,9},{9,11},{11,13},{13,15},{17,19},{19,21},{21... | collective-permute-start | bytes 1179656 | tf_op jit(solution)/shard_map/ppermute | solution.py:36
  60.2 9.3 %collective-permute-start.6 = (f32[12,64,128]{2,1,0:T(8,128)}, f32[12,64,128]{2,1,0:T(8,128)}, u32[]{:S(2)}, u32[]{:S(2)}) collective-permute-start(f32[12,64,128]{2,1,0:T(8,128)} %get-tuple-element.23), channel_id=1, source_target_pairs={{1,3},{3,5},{5,7},{7,9},{9,11},{11,13},{13,15},{17,19},{19,21},{21... | collective-permute-start | bytes 1179656 | tf_op jit(solution)/shard_map/ppermute | solution.py:36
  71.4 10.0 %collective-permute-start.7 = (f32[12,64,128]{2,1,0:T(8,128)}, f32[12,64,128]{2,1,0:T(8,128)}, u32[]{:S(2)}, u32[]{:S(2)}) collective-permute-start(f32[12,64,128]{2,1,0:T(8,128)} %get-tuple-element.21), channel_id=1, source_target_pairs={{1,3},{3,5},{5,7},{7,9},{9,11},{11,13},{13,15},{17,19},{19,21},{21... | collective-permute-start | bytes 1179656 | tf_op jit(solution)/shard_map/ppermute | solution.py:36
  83.3 10.0 %collective-permute-start.8 = (f32[12,64,128]{2,1,0:T(8,128)}, f32[12,64,128]{2,1,0:T(8,128)}, u32[]{:S(2)}, u32[]{:S(2)}) collective-permute-start(f32[12,64,128]{2,1,0:T(8,128)} %get-tuple-element.19), channel_id=1, source_target_pairs={{1,3},{3,5},{5,7},{7,9},{9,11},{11,13},{13,15},{17,19},{19,21},{21... | collective-permute-start | bytes 1179656 | tf_op jit(solution)/shard_map/ppermute | solution.py:36
  95.2 10.0 %collective-permute-start.9 = (f32[12,64,128]{2,1,0:T(8,128)}, f32[12,64,128]{2,1,0:T(8,128)}, u32[]{:S(2)}, u32[]{:S(2)}) collective-permute-start(f32[12,64,128]{2,1,0:T(8,128)} %get-tuple-element.17), channel_id=1, source_target_pairs={{1,3},{3,5},{5,7},{7,9},{9,11},{11,13},{13,15},{17,19},{19,21},{21... | collective-permute-start | bytes 1179656 | tf_op jit(solution)/shard_map/ppermute | solution.py:36
  107.1 16.7 %copy-start.5 = (f32[3072]{0:T(1024)S(1)}, f32[3072]{0:T(1024)}, u32[]{:S(2)}) copy-start(f32[3072]{0:T(1024)} %param.17) | copy-start | bytes 36868
  107.1 16.8 %collective-permute-start.10 = (f32[12,64,128]{2,1,0:T(8,128)}, f32[12,64,128]{2,1,0:T(8,128)}, u32[]{:S(2)}, u32[]{:S(2)}) collective-permute-start(f32[12,64,128]{2,1,0:T(8,128)} %get-tuple-element.15), channel_id=1, source_target_pairs={{1,3},{3,5},{5,7},{7,9},{9,11},{11,13},{13,15},{17,19},{19,21},{21... | collective-permute-start | bytes 1179656 | tf_op jit(solution)/shard_map/ppermute | solution.py:36
  115.3 14.8 %copy-start.12 = (s32[128]{0:T(128)S(1)}, s32[128]{0:T(128)}, u32[]{:S(2)}) copy-start(s32[128]{0:T(128)} %slice.115) | copy-start | bytes 1540
  123.8 16.7 %copy-start.1 = (bf16[128,3072]{0,1:T(8,128)(2,1)S(1)}, bf16[128,3072]{0,1:T(8,128)(2,1)}, u32[]{:S(2)}) copy-start(bf16[128,3072]{0,1:T(8,128)(2,1)} %copy-done) | copy-start | bytes 2359300
  123.9 16.7 %copy-start.6 = (f32[8,128]{1,0:T(8,128)S(1)}, f32[8,128]{1,0:T(8,128)}, u32[]{:S(2)}) copy-start(f32[8,128]{1,0:T(8,128)} %copy.60) | copy-start | bytes 12292
  123.9 16.7 %copy-start.7 = (f32[8,128]{1,0:T(8,128)S(1)}, f32[8,128]{1,0:T(8,128)}, u32[]{:S(2)}) copy-start(f32[8,128]{1,0:T(8,128)} %copy.62) | copy-start | bytes 12292
  125.1 9.7 %collective-permute-start.11 = (f32[12,64,128]{2,1,0:T(8,128)S(1)}, f32[12,64,128]{2,1,0:T(8,128)S(1)}, u32[]{:S(2)}, u32[]{:S(2)}) collective-permute-start(f32[12,64,128]{2,1,0:T(8,128)S(1)} %get-tuple-element.13), channel_id=1, source_target_pairs={{1,3},{3,5},{5,7},{7,9},{9,11},{11,13},{13,15},{17,19},{19,21},{21... | collective-permute-start | bytes 1179656 | tf_op jit(solution)/shard_map/ppermute | solution.py:36
  134.8 6.2 %copy-start.8 = (f32[8,128]{1,0:T(8,128)S(1)}, f32[8,128]{1,0:T(8,128)}, u32[]{:S(2)}) copy-start(f32[8,128]{1,0:T(8,128)} %copy.63) | copy-start | bytes 12292
  134.8 6.2 %copy-start.9 = (f32[8,128]{1,0:T(8,128)S(1)}, f32[8,128]{1,0:T(8,128)}, u32[]{:S(2)}) copy-start(f32[8,128]{1,0:T(8,128)} %copy.65) | copy-start | bytes 12292
  135.5 9.7 %collective-permute-start.12 = (f32[12,64,128]{2,1,0:T(8,128)S(1)}, f32[12,64,128]{2,1,0:T(8,128)S(1)}, u32[]{:S(2)}, u32[]{:S(2)}) collective-permute-start(f32[12,64,128]{2,1,0:T(8,128)S(1)} %get-tuple-element.11), channel_id=1, source_target_pairs={{1,3},{3,5},{5,7},{7,9},{9,11},{11,13},{13,15},{17,19},{19,21},{21... | collective-permute-start | bytes 1179656 | tf_op jit(solution)/shard_map/ppermute | solution.py:36
  145.5 3.2 %collective-permute-start.13 = (bf16[48,64,128]{2,1,0:T(8,128)(2,1)S(1)}, bf16[48,64,128]{2,1,0:T(8,128)(2,1)S(1)}, u32[]{:S(2)}, u32[]{:S(2)}) collective-permute-start(bf16[48,64,128]{2,1,0:T(8,128)(2,1)S(1)} %convert.8), channel_id=1, source_target_pairs={{1,0},{3,2},{5,4},{7,6},{9,8},{11,10},{13,12},{15,14},{17,16},{19,... | collective-permute-start | bytes 2359304 | tf_op jit(solution)/shard_map/ppermute | solution.py:37
  147.5 1.1 copy-start.11
  147.6 1.1 copy-start.13

commit v2 on v1

--- a/solution.py
+++ b/solution.py
@@ -14,29 +14,43 @@
     size, position = (lax.axis_size("ctx"), lax.axis_index("ctx"))
     chips = size // 2
     chip = position // 2
+    core = position % 2
+    low = core == 0
     heads = decay.shape[0]
-    width = heads // chunks
-    up = [(2 * i, 2 * i + 1) for i in range(chips)]
-    down = [(2 * i + 1, 2 * i) for i in range(chips)]
-    ahead = [(2 * i + 1, 2 * i + 3) for i in range(chips - 1)]
-    decay_low, local_low = lax.ppermute((decay, local), "ctx", up)
-    chip_decay = decay * decay_low
-    chip_local = decay[:, None, None] * local_low + local
-    received = jnp.zeros((width,) + local.shape[1:], local.dtype)
-    carry = jnp.zeros_like(local)
+    half = heads // 2
+    width = half // chunks
+    rest = local.shape[1:]
+    swap = [(2 * i + j, 2 * i + 1 - j) for i in range(chips) for j in range(2)]
+    ahead = [(i, i + 2) for i in range(size - 2)]
+    mine = lax.dynamic_slice_in_dim(local, core * half, half, 0)
+    theirs = lax.dynamic_slice_in_dim(local, (1 - core) * half, half, 0)
+    got_local = lax.ppermute(theirs, "ctx", swap)
+    got_decay = lax.ppermute(decay, "ctx", swap)
+    decay_hi = lax.dynamic_slice_in_dim(jnp.where(low, got_decay, decay), core * half, half, 0)
+    decay_lo = lax.dynamic_slice_in_dim(jnp.where(low, decay, got_decay), core * half, half, 0)
+    local_lo = jnp.where(low, mine, got_local)
+    local_hi = jnp.where(low, got_local, mine)
+    chip_decay = jnp.roll((decay_hi * decay_lo).reshape(chunks, width), chip, axis=0)
+    chip_local = jnp.roll(
+        (decay_hi[:, None, None] * local_lo + local_hi).reshape((chunks, width) + rest), chip, axis=0
+    )
+    received = jnp.zeros((width,) + rest, local.dtype)
+    slots = [received] * chunks
     for step in range(chunks + chips - 1):
         k = step - chip
         valid = (k >= 0) & (k < chunks)
-        at = jnp.clip(k, 0, chunks - 1) * width
-        old = lax.dynamic_slice_in_dim(carry, at, width, 0)
-        carry = lax.dynamic_update_slice_in_dim(carry, jnp.where(valid, received, old), at, 0)
+        j = step % chunks
+        slots[j] = jnp.where(valid, received, slots[j])
         if step < chunks + chips - 2:
-            d = lax.dynamic_slice_in_dim(chip_decay, at, width, 0)
-            l = lax.dynamic_slice_in_dim(chip_local, at, width, 0)
-            received = lax.ppermute(d[:, None, None] * received + l, "ctx", ahead)
-    lowered = lax.ppermute(carry, "ctx", down)
-    own = decay_low[:, None, None] * carry + local_low
-    return jnp.where(position % 2 == 0, lowered, own)
+            received = lax.ppermute(
+                chip_decay[j][:, None, None] * received + chip_local[j], "ctx", ahead
+            )
+    carry_half = jnp.roll(jnp.stack(slots), -chip, axis=0).reshape((half,) + rest)
+    onward = decay_lo[:, None, None] * carry_half + local_lo
+    got_end = lax.ppermute(jnp.where(low, onward, carry_half), "ctx", swap)
+    first = jnp.where(low, carry_half, got_end)
+    second = jnp.where(low, got_end, onward)
+    return jnp.concatenate([first, second], axis=0)
 
 
 def body(xbc, dt_raw, lengths, conv_weight, conv_bias, dt_bias, decay_rate, skip, norm_gain):

time: 154 us -> 136 us (0.88)
  the two profiles are of different devices: /device:TPU:127 before, /device:TPU:1 now
where the time goes in v2:
time: 136 us; the launch traced here: 135 us
  starting transfers between devices  64.5 us (47%)
  local copies, waits for them, and re-layouts  26.7 us (20%)
  waiting for transfers between devices  19.4 us (14%)
  other arithmetic  18.1 us (13%)
  matrix products  5.47 us (4%)
    ppermute x10, starting transfers between devices, chain_carry(): lax.ppermute(chip_decay[j][:, None, None] * received + chip_local[j], 'ct...  41.7 us
    ppermute x10, waiting for transfers between devices, chain_carry(): lax.ppermute(chip_decay[j][:, None, None] * received + chip_local[j], 'ct...  17.8 us
    ppermute x1, starting transfers between devices, chain_carry(): got_end = lax.ppermute(jnp.where(low, onward, carry_half), 'ctx', swap)  10.8 us
    transpose x7, local copies, waits for them, and re-layouts, body(): step_size[:, part_start:part_start + group].T[:, None, :]  8.96 us
    transpose x7, local copies, waits for them, and re-layouts, body(): cum_part = cum[:, part_start:part_start + group].T  7.53 us
    add x9, other arithmetic, chain_carry(): chip_decay[j][:, None, None] * received + chip_local[j]  5.6 us
    ppermute x1, starting transfers between devices, shifted(): return lax.ppermute(block, axis, route)  5.39 us
    ppermute x1, starting transfers between devices, chain_carry(): got_local = lax.ppermute(theirs, 'ctx', swap)  4.68 us
  transfers between devices with their start and end apart: 14, of which 10 were waited for; matrix products, arithmetic and copies ran while one was open for 24% of the time, Pallas kernels for 0%

profile of v2, /device:TPU:1, one launch (start us, length us, event | category | flops | bytes accessed | tf_op | source)
XLA Modules:
  0.0 134.8 jit_solution(7228757854028755946)
XLA Ops:
  0.9 5.4 %collective-permute-start = (bf16[3,3328]{1,0:T(4,128)(2,1)S(1)}, bf16[3,3328]{1,0:T(4,128)(2,1)S(1)}, u32[]{:S(2)}, u32[]{:S(2)}) collective-permute-start(bf16[3,3328]{1,0:T(4,128)(2,1)S(1)} %slice.152), channel_id=1, source_target_pairs={{0,1},{1,2},{2,3},{3,4},{4,5},{5,6},{6,7},{7,8},{8,9},{9,10},{10,1... | collective-permute-start | bytes 59912 | tf_op jit(solution)/shard_map/ppermute | solution.py:10
  13.7 2.6 %multiply_convert_fusion = bf16[128,3328]{1,0:T(8,128)(2,1)S(1)} fusion(bf16[128,3328]{1,0:T(8,128)(2,1)S(1)} %copy-done.3, bf16[3,3328]{1,0:T(4,128)(2,1)S(1)} %collective-permute-done, f32[3328]{0:T(1024)S(1)} %get-tuple-element.8, f32[3328]{0:T(1024)S(1)} %get-tuple-element.9, f32[3328]{0:T(1024)S(1)} %get-tuple-element.7, f32[3328]{0:T(1024)S(1)} %get-tuple-element.6, ...), kind=kLoop, calls=%fused_computation.2 | loop fusion | flops 12353536 | bytes 1790848 | tf_op jit(solution)/shard_map/convert_element_type | solution.py:78
  18.2 4.7 %collective-permute-start.2 = (f32[24,64,128]{2,1,0:T(8,128)}, f32[24,64,128]{2,1,0:T(8,128)S(1)}, u32[]{:S(2)}, u32[]{:S(2)}) collective-permute-start(f32[24,64,128]{2,1,0:T(8,128)} %constant_dynamic-slice_fusion), channel_id=1, source_target_pairs={{0,1},{1,0},{2,3},{3,2},{4,5},{5,4},{6,7},{7,6},{8,9},{9,8},{10,11... | collective-permute-start | bytes 2359304 | tf_op jit(solution)/shard_map/ppermute | solution.py:27
  22.9 1.9 %collective-permute-start.1 = (f32[48]{0:T(128)S(1)}, f32[48]{0:T(128)S(1)}, u32[]{:S(2)}, u32[]{:S(2)}) collective-permute-start(f32[48]{0:T(128)S(1)} %copy-done.24), channel_id=1, source_target_pairs={{0,1},{1,0},{2,3},{3,2},{4,5},{5,4},{6,7},{7,6},{8,9},{9,8},{10,11... | collective-permute-start | bytes 584 | tf_op jit(solution)/shard_map/ppermute | solution.py:28
  30.4 3.4 %collective-permute-done.3 = f32[6,64,128]{2,1,0:T(8,128)S(1)} collective-permute-done((f32[6,64,128]{2,1,0:T(8,128)S(1)}, f32[6,64,128]{2,1,0:T(8,128)S(1)}, u32[]{:S(2)}, u32[]{:S(2)}) %collective-permute-start.3) | collective-permute-done | bytes 196640 | tf_op jit(solution)/shard_map/ppermute | solution.py:45
  34.5 4.8 %collective-permute-start.4 = (f32[6,64,128]{2,1,0:T(8,128)}, f32[6,64,128]{2,1,0:T(8,128)}, u32[]{:S(2)}, u32[]{:S(2)}) collective-permute-start(f32[6,64,128]{2,1,0:T(8,128)} %multiply_add_fusion.8), channel_id=1, source_target_pairs={{0,2},{1,3},{2,4},{3,5},{4,6},{5,7},{6,8},{7,9},{8,10},{9,11},{10,... | collective-permute-start | bytes 589832 | tf_op jit(solution)/shard_map/ppermute | solution.py:45
  42.0 1.7 %multiply_add_fusion.7 = f32[6,64,128]{2,1,0:T(8,128)} fusion(f32[6,64,128]{2,1,0:T(8,128)} %collective-permute-done.4, f32[4,6,64,128]{3,2,1,0:T(8,128)S(1)} %fusion.17, f32[6]{0:T(128)} %get-tuple-element.39), kind=kLoop, calls=%fused_computation.112 | loop fusion | flops 98304 | bytes 589848 | tf_op jit(solution)/shard_map/add | solution.py:46
  43.7 5.9 %collective-permute-start.5 = (f32[6,64,128]{2,1,0:T(8,128)}, f32[6,64,128]{2,1,0:T(8,128)}, u32[]{:S(2)}, u32[]{:S(2)}) collective-permute-start(f32[6,64,128]{2,1,0:T(8,128)} %multiply_add_fusion.7), channel_id=1, source_target_pairs={{0,2},{1,3},{2,4},{3,5},{4,6},{5,7},{6,8},{7,9},{8,10},{9,11},{10,... | collective-permute-start | bytes 589832 | tf_op jit(solution)/shard_map/ppermute | solution.py:45
  50.4 1.5 %copy.77 = f32[8,128]{1,0:T(8,128)} copy(f32[8,128]{0,1:T(8,128)} %get-tuple-element.31) | data formatting | bytes 8192 | tf_op jit(solution)/shard_map/transpose | solution.py:100
  51.9 1.5 %copy.74 = f32[8,128]{1,0:T(8,128)} copy(f32[8,128]{0,1:T(8,128)} %get-tuple-element.32) | data formatting | bytes 8192 | tf_op jit(solution)/shard_map/transpose | solution.py:100
  53.4 1.5 %copy.71 = f32[8,128]{1,0:T(8,128)} copy(f32[8,128]{0,1:T(8,128)} %get-tuple-element.33) | data formatting | bytes 8192 | tf_op jit(solution)/shard_map/transpose | solution.py:100
  54.9 1.5 %copy.68 = f32[8,128]{1,0:T(8,128)} copy(f32[8,128]{0,1:T(8,128)} %get-tuple-element.34) | data formatting | bytes 8192 | tf_op jit(solution)/shard_map/transpose | solution.py:100
  56.4 1.5 %copy.65 = f32[8,128]{1,0:T(8,128)} copy(f32[8,128]{0,1:T(8,128)} %get-tuple-element.35) | data formatting | bytes 8192 | tf_op jit(solution)/shard_map/transpose | solution.py:100
  58.6 1.7 %multiply_add_fusion.6 = f32[6,64,128]{2,1,0:T(8,128)} fusion(f32[6,64,128]{2,1,0:T(8,128)} %collective-permute-done.5, f32[4,6,64,128]{3,2,1,0:T(8,128)S(1)} %fusion.17, f32[6]{0:T(128)S(1)} %copy-done.10), kind=kLoop, calls=%fused_computation.111 | loop fusion | flops 98304 | bytes 589848 | tf_op jit(solution)/shard_map/add | solution.py:46
  60.2 4.1 %collective-permute-start.6 = (f32[6,64,128]{2,1,0:T(8,128)}, f32[6,64,128]{2,1,0:T(8,128)}, u32[]{:S(2)}, u32[]{:S(2)}) collective-permute-start(f32[6,64,128]{2,1,0:T(8,128)} %multiply_add_fusion.6), channel_id=1, source_target_pairs={{0,2},{1,3},{2,4},{3,5},{4,6},{5,7},{6,8},{7,9},{8,10},{9,11},{10,... | collective-permute-start | bytes 589832 | tf_op jit(solution)/shard_map/ppermute | solution.py:45
  65.2 1.5 %copy.75 = f32[8,128]{1,0:T(8,128)} copy(f32[8,128]{0,1:T(8,128)} %get-tuple-element.25) | data formatting | bytes 8192 | tf_op jit(solution)/shard_map/transpose | solution.py:96
  66.7 1.5 %copy.72 = f32[8,128]{1,0:T(8,128)} copy(f32[8,128]{0,1:T(8,128)} %get-tuple-element.26) | data formatting | bytes 8192 | tf_op jit(solution)/shard_map/transpose | solution.py:96
  68.2 1.5 %copy.69 = f32[8,128]{1,0:T(8,128)} copy(f32[8,128]{0,1:T(8,128)} %get-tuple-element.27) | data formatting | bytes 8192 | tf_op jit(solution)/shard_map/transpose | solution.py:96
  69.7 1.5 %copy.66 = f32[8,128]{1,0:T(8,128)} copy(f32[8,128]{0,1:T(8,128)} %get-tuple-element.28) | data formatting | bytes 8192 | tf_op jit(solution)/shard_map/transpose | solution.py:96
  73.0 3.7 %collective-permute-start.7 = (f32[6,64,128]{2,1,0:T(8,128)S(1)}, f32[6,64,128]{2,1,0:T(8,128)S(1)}, u32[]{:S(2)}, u32[]{:S(2)}) collective-permute-start(f32[6,64,128]{2,1,0:T(8,128)S(1)} %multiply_add_fusion.5), channel_id=1, source_target_pairs={{0,2},{1,3},{2,4},{3,5},{4,6},{5,7},{6,8},{7,9},{8,10},{9,11},{10,... | collective-permute-start | bytes 589832 | tf_op jit(solution)/shard_map/ppermute | solution.py:45
  77.4 1.8 %collective-permute-done.7 = f32[6,64,128]{2,1,0:T(8,128)S(1)} collective-permute-done((f32[6,64,128]{2,1,0:T(8,128)S(1)}, f32[6,64,128]{2,1,0:T(8,128)S(1)}, u32[]{:S(2)}, u32[]{:S(2)}) %collective-permute-start.7) | collective-permute-done | bytes 196640 | tf_op jit(solution)/shard_map/ppermute | solution.py:45
  79.3 5.3 %collective-permute-start.8 = (f32[6,64,128]{2,1,0:T(8,128)S(1)}, f32[6,64,128]{2,1,0:T(8,128)S(1)}, u32[]{:S(2)}, u32[]{:S(2)}) collective-permute-start(f32[6,64,128]{2,1,0:T(8,128)S(1)} %multiply_add_fusion.4), channel_id=1, source_target_pairs={{0,2},{1,3},{2,4},{3,5},{4,6},{5,7},{6,8},{7,9},{8,10},{9,11},{10,... | collective-permute-start | bytes 589832 | tf_op jit(solution)/shard_map/ppermute | solution.py:45
  85.6 1.6 %collective-permute-done.8 = f32[6,64,128]{2,1,0:T(8,128)S(1)} collective-permute-done((f32[6,64,128]{2,1,0:T(8,128)S(1)}, f32[6,64,128]{2,1,0:T(8,128)S(1)}, u32[]{:S(2)}, u32[]{:S(2)}) %collective-permute-start.8) | collective-permute-done | bytes 196640 | tf_op jit(solution)/shard_map/ppermute | solution.py:45
  87.3 3.8 %collective-permute-start.9 = (f32[6,64,128]{2,1,0:T(8,128)S(1)}, f32[6,64,128]{2,1,0:T(8,128)S(1)}, u32[]{:S(2)}, u32[]{:S(2)}) collective-permute-start(f32[6,64,128]{2,1,0:T(8,128)S(1)} %multiply_add_fusion.3), channel_id=1, source_target_pairs={{0,2},{1,3},{2,4},{3,5},{4,6},{5,7},{6,8},{7,9},{8,10},{9,11},{10,... | collective-permute-start | bytes 589832 | tf_op jit(solution)/shard_map/ppermute | solution.py:45
  92.2 1.5 %collective-permute-done.9 = f32[6,64,128]{2,1,0:T(8,128)S(1)} collective-permute-done((f32[6,64,128]{2,1,0:T(8,128)S(1)}, f32[6,64,128]{2,1,0:T(8,128)S(1)}, u32[]{:S(2)}, u32[]{:S(2)}) %collective-permute-start.9) | collective-permute-done | bytes 196640 | tf_op jit(solution)/shard_map/ppermute | solution.py:45
  94.8 3.8 %collective-permute-start.10 = (f32[6,64,128]{2,1,0:T(8,128)S(1)}, f32[6,64,128]{2,1,0:T(8,128)S(1)}, u32[]{:S(2)}, u32[]{:S(2)}) collective-permute-start(f32[6,64,128]{2,1,0:T(8,128)S(1)} %get-tuple-element.18), channel_id=1, source_target_pairs={{0,2},{1,3},{2,4},{3,5},{4,6},{5,7},{6,8},{7,9},{8,10},{9,11},{10,... | collective-permute-start | bytes 589832 | tf_op jit(solution)/shard_map/ppermute | solution.py:45
  99.0 2.2 %collective-permute-done.10 = f32[6,64,128]{2,1,0:T(8,128)S(1)} collective-permute-done((f32[6,64,128]{2,1,0:T(8,128)S(1)}, f32[6,64,128]{2,1,0:T(8,128)S(1)}, u32[]{:S(2)}, u32[]{:S(2)}) %collective-permute-start.10) | collective-permute-done | bytes 196640 | tf_op jit(solution)/shard_map/ppermute | solution.py:45
  101.3 4.8 %collective-permute-start.11 = (f32[6,64,128]{2,1,0:T(8,128)S(1)}, f32[6,64,128]{2,1,0:T(8,128)S(1)}, u32[]{:S(2)}, u32[]{:S(2)}) collective-permute-start(f32[6,64,128]{2,1,0:T(8,128)S(1)} %get-tuple-element.21), channel_id=1, source_target_pairs={{0,2},{1,3},{2,4},{3,5},{4,6},{5,7},{6,8},{7,9},{8,10},{9,11},{10,... | collective-permute-start | bytes 589832 | tf_op jit(solution)/shard_map/ppermute | solution.py:45
  106.5 3.1 %collective-permute-done.11 = f32[6,64,128]{2,1,0:T(8,128)S(1)} collective-permute-done((f32[6,64,128]{2,1,0:T(8,128)S(1)}, f32[6,64,128]{2,1,0:T(8,128)S(1)}, u32[]{:S(2)}, u32[]{:S(2)}) %collective-permute-start.11) | collective-permute-done | bytes 196640 | tf_op jit(solution)/shard_map/ppermute | solution.py:45
  109.6 4.1 %collective-permute-start.12 = (f32[6,64,128]{2,1,0:T(8,128)S(1)}, f32[6,64,128]{2,1,0:T(8,128)S(1)}, u32[]{:S(2)}, u32[]{:S(2)}) collective-permute-start(f32[6,64,128]{2,1,0:T(8,128)S(1)} %get-tuple-element.19), channel_id=1, source_target_pairs={{0,2},{1,3},{2,4},{3,5},{4,6},{5,7},{6,8},{7,9},{8,10},{9,11},{10,... | collective-permute-start | bytes 589832 | tf_op jit(solution)/shard_map/ppermute | solution.py:45
  114.1 3.5 %collective-permute-done.12 = f32[6,64,128]{2,1,0:T(8,128)S(1)} collective-permute-done((f32[6,64,128]{2,1,0:T(8,128)S(1)}, f32[6,64,128]{2,1,0:T(8,128)S(1)}, u32[]{:S(2)}, u32[]{:S(2)}) %collective-permute-start.12) | collective-permute-done | bytes 196640 | tf_op jit(solution)/shard_map/ppermute | solution.py:45
  119.3 10.8 %collective-permute-start.13 = (bf16[24,64,128]{2,1,0:T(8,128)(2,1)S(1)}, bf16[24,64,128]{2,1,0:T(8,128)(2,1)S(1)}, u32[]{:S(2)}, u32[]{:S(2)}) collective-permute-start(bf16[24,64,128]{2,1,0:T(8,128)(2,1)S(1)} %bitcast_select_fusion.1), channel_id=1, source_target_pairs={{0,1},{1,0},{2,3},{3,2},{4,5},{5,4},{6,7},{7,6},{8,9},{9,8},{10,11... | collective-permute-start | bytes 1179656 | tf_op jit(solution)/shard_map/ppermute | solution.py:50
  (123 shorter events, 34.5 us)
Async XLA Ops:
  0.0 13.7 %copy-start.3 = (bf16[128,3328]{1,0:T(8,128)(2,1)S(1)}, bf16[128,3328]{1,0:T(8,128)(2,1)}, u32[]{:S(2)}) copy-start(bf16[128,3328]{1,0:T(8,128)(2,1)} %param.11) | copy-start | bytes 2555908
  0.9 12.8 %collective-permute-start = (bf16[3,3328]{1,0:T(4,128)(2,1)S(1)}, bf16[3,3328]{1,0:T(4,128)(2,1)S(1)}, u32[]{:S(2)}, u32[]{:S(2)}) collective-permute-start(bf16[3,3328]{1,0:T(4,128)(2,1)S(1)} %slice.152), channel_id=1, source_target_pairs={{0,1},{1,2},{2,3},{3,4},{4,5},{5,6},{6,7},{7,8},{8,9},{9,10},{10,1... | collective-permute-start | bytes 59912 | tf_op jit(solution)/shard_map/ppermute | solution.py:10
  16.8 6.1 %copy-start.24 = (f32[48]{0:T(128)S(1)}, f32[48]{0:T(128)}, u32[]{:S(2)}) copy-start(f32[48]{0:T(128)} %exponential_multiply_fusion.1) | copy-start | bytes 580
  18.2 9.0 %collective-permute-start.2 = (f32[24,64,128]{2,1,0:T(8,128)}, f32[24,64,128]{2,1,0:T(8,128)S(1)}, u32[]{:S(2)}, u32[]{:S(2)}) collective-permute-start(f32[24,64,128]{2,1,0:T(8,128)} %constant_dynamic-slice_fusion), channel_id=1, source_target_pairs={{0,1},{1,0},{2,3},{3,2},{4,5},{5,4},{6,7},{7,6},{8,9},{9,8},{10,11... | collective-permute-start | bytes 2359304 | tf_op jit(solution)/shard_map/ppermute | solution.py:27
  22.9 3.0 %collective-permute-start.1 = (f32[48]{0:T(128)S(1)}, f32[48]{0:T(128)S(1)}, u32[]{:S(2)}, u32[]{:S(2)}) collective-permute-start(f32[48]{0:T(128)S(1)} %copy-done.24), channel_id=1, source_target_pairs={{0,1},{1,0},{2,3},{3,2},{4,5},{5,4},{6,7},{7,6},{8,9},{9,8},{10,11... | collective-permute-start | bytes 584 | tf_op jit(solution)/shard_map/ppermute | solution.py:28
  28.1 11.8 %copy-start.6 = (f32[3072]{0:T(1024)S(1)}, f32[3072]{0:T(1024)}, u32[]{:S(2)}) copy-start(f32[3072]{0:T(1024)} %param.19) | copy-start | bytes 36868
  28.3 5.4 %collective-permute-start.3 = (f32[6,64,128]{2,1,0:T(8,128)S(1)}, f32[6,64,128]{2,1,0:T(8,128)S(1)}, u32[]{:S(2)}, u32[]{:S(2)}) collective-permute-start(f32[6,64,128]{2,1,0:T(8,128)S(1)} %fusion.62), channel_id=1, source_target_pairs={{0,2},{1,3},{2,4},{3,5},{4,6},{5,7},{6,8},{7,9},{8,10},{9,11},{10,... | collective-permute-start | bytes 589832 | tf_op jit(solution)/shard_map/ppermute | solution.py:45
  34.5 7.5 %collective-permute-start.4 = (f32[6,64,128]{2,1,0:T(8,128)}, f32[6,64,128]{2,1,0:T(8,128)}, u32[]{:S(2)}, u32[]{:S(2)}) collective-permute-start(f32[6,64,128]{2,1,0:T(8,128)} %multiply_add_fusion.8), channel_id=1, source_target_pairs={{0,2},{1,3},{2,4},{3,5},{4,6},{5,7},{6,8},{7,9},{8,10},{9,11},{10,... | collective-permute-start | bytes 589832 | tf_op jit(solution)/shard_map/ppermute | solution.py:45
  39.9 18.7 %copy-start.10 = (f32[6]{0:T(128)S(1)}, f32[6]{0:T(128)}, u32[]{:S(2)}) copy-start(f32[6]{0:T(128)} %get-tuple-element.40) | copy-start | bytes 76
  43.7 28.3 %copy-start.9 = (f32[6]{0:T(128)S(1)}, f32[6]{0:T(128)}, u32[]{:S(2)}) copy-start(f32[6]{0:T(128)} %get-tuple-element.37) | copy-start | bytes 76
  43.7 14.9 %collective-permute-start.5 = (f32[6,64,128]{2,1,0:T(8,128)}, f32[6,64,128]{2,1,0:T(8,128)}, u32[]{:S(2)}, u32[]{:S(2)}) collective-permute-start(f32[6,64,128]{2,1,0:T(8,128)} %multiply_add_fusion.7), channel_id=1, source_target_pairs={{0,2},{1,3},{2,4},{3,5},{4,6},{5,7},{6,8},{7,9},{8,10},{9,11},{10,... | collective-permute-start | bytes 589832 | tf_op jit(solution)/shard_map/ppermute | solution.py:45
  50.4 28.8 %copy-start.8 = (f32[6]{0:T(128)S(1)}, f32[6]{0:T(128)}, u32[]{:S(2)}) copy-start(f32[6]{0:T(128)} %copy-done.7) | copy-start | bytes 76
  58.5 28.7 %copy-start.11 = (f32[6]{0:T(128)S(1)}, f32[6]{0:T(128)}, u32[]{:S(2)}) copy-start(f32[6]{0:T(128)} %get-tuple-element.39) | copy-start | bytes 76
  60.2 11.7 %collective-permute-start.6 = (f32[6,64,128]{2,1,0:T(8,128)}, f32[6,64,128]{2,1,0:T(8,128)}, u32[]{:S(2)}, u32[]{:S(2)}) collective-permute-start(f32[6,64,128]{2,1,0:T(8,128)} %multiply_add_fusion.6), channel_id=1, source_target_pairs={{0,2},{1,3},{2,4},{3,5},{4,6},{5,7},{6,8},{7,9},{8,10},{9,11},{10,... | collective-permute-start | bytes 589832 | tf_op jit(solution)/shard_map/ppermute | solution.py:45
  73.0 6.2 %collective-permute-start.7 = (f32[6,64,128]{2,1,0:T(8,128)S(1)}, f32[6,64,128]{2,1,0:T(8,128)S(1)}, u32[]{:S(2)}, u32[]{:S(2)}) collective-permute-start(f32[6,64,128]{2,1,0:T(8,128)S(1)} %multiply_add_fusion.5), channel_id=1, source_target_pairs={{0,2},{1,3},{2,4},{3,5},{4,6},{5,7},{6,8},{7,9},{8,10},{9,11},{10,... | collective-permute-start | bytes 589832 | tf_op jit(solution)/shard_map/ppermute | solution.py:45
  79.3 7.9 %collective-permute-start.8 = (f32[6,64,128]{2,1,0:T(8,128)S(1)}, f32[6,64,128]{2,1,0:T(8,128)S(1)}, u32[]{:S(2)}, u32[]{:S(2)}) collective-permute-start(f32[6,64,128]{2,1,0:T(8,128)S(1)} %multiply_add_fusion.4), channel_id=1, source_target_pairs={{0,2},{1,3},{2,4},{3,5},{4,6},{5,7},{6,8},{7,9},{8,10},{9,11},{10,... | collective-permute-start | bytes 589832 | tf_op jit(solution)/shard_map/ppermute | solution.py:45
  85.6 13.0 %copy-start.20 = (f32[8,128]{1,0:T(8,128)S(1)}, f32[8,128]{1,0:T(8,128)}, u32[]{:S(2)}) copy-start(f32[8,128]{1,0:T(8,128)} %copy.65) | copy-start | bytes 12292
  85.6 13.0 %copy-start.22 = (f32[8,128]{1,0:T(8,128)S(1)}, f32[8,128]{1,0:T(8,128)}, u32[]{:S(2)}) copy-start(f32[8,128]{1,0:T(8,128)} %copy.63) | copy-start | bytes 12292
  87.3 6.4 %collective-permute-start.9 = (f32[6,64,128]{2,1,0:T(8,128)S(1)}, f32[6,64,128]{2,1,0:T(8,128)S(1)}, u32[]{:S(2)}, u32[]{:S(2)}) collective-permute-start(f32[6,64,128]{2,1,0:T(8,128)S(1)} %multiply_add_fusion.3), channel_id=1, source_target_pairs={{0,2},{1,3},{2,4},{3,5},{4,6},{5,7},{6,8},{7,9},{8,10},{9,11},{10,... | collective-permute-start | bytes 589832 | tf_op jit(solution)/shard_map/ppermute | solution.py:45
  94.7 11.3 %copy-start.18 = (f32[8,128]{1,0:T(8,128)S(1)}, f32[8,128]{1,0:T(8,128)}, u32[]{:S(2)}) copy-start(f32[8,128]{1,0:T(8,128)} %copy.68) | copy-start | bytes 12292
  94.8 11.3 %copy-start.21 = (f32[8,128]{1,0:T(8,128)S(1)}, f32[8,128]{1,0:T(8,128)}, u32[]{:S(2)}) copy-start(f32[8,128]{1,0:T(8,128)} %copy.66) | copy-start | bytes 12292
  94.8 6.4 %collective-permute-start.10 = (f32[6,64,128]{2,1,0:T(8,128)S(1)}, f32[6,64,128]{2,1,0:T(8,128)S(1)}, u32[]{:S(2)}, u32[]{:S(2)}) collective-permute-start(f32[6,64,128]{2,1,0:T(8,128)S(1)} %get-tuple-element.18), channel_id=1, source_target_pairs={{0,2},{1,3},{2,4},{3,5},{4,6},{5,7},{6,8},{7,9},{8,10},{9,11},{10,... | collective-permute-start | bytes 589832 | tf_op jit(solution)/shard_map/ppermute | solution.py:45
  101.3 12.5 %copy-start.17 = (f32[8,128]{1,0:T(8,128)S(1)}, f32[8,128]{1,0:T(8,128)}, u32[]{:S(2)}) copy-start(f32[8,128]{1,0:T(8,128)} %copy.71) | copy-start | bytes 12292
  101.3 12.5 %copy-start.19 = (f32[8,128]{1,0:T(8,128)S(1)}, f32[8,128]{1,0:T(8,128)}, u32[]{:S(2)}) copy-start(f32[8,128]{1,0:T(8,128)} %copy.69) | copy-start | bytes 12292
  101.3 8.2 %collective-permute-start.11 = (f32[6,64,128]{2,1,0:T(8,128)S(1)}, f32[6,64,128]{2,1,0:T(8,128)S(1)}, u32[]{:S(2)}, u32[]{:S(2)}) collective-permute-start(f32[6,64,128]{2,1,0:T(8,128)S(1)} %get-tuple-element.21), channel_id=1, source_target_pairs={{0,2},{1,3},{2,4},{3,5},{4,6},{5,7},{6,8},{7,9},{8,10},{9,11},{10,... | collective-permute-start | bytes 589832 | tf_op jit(solution)/shard_map/ppermute | solution.py:45
  109.6 8.0 %collective-permute-start.12 = (f32[6,64,128]{2,1,0:T(8,128)S(1)}, f32[6,64,128]{2,1,0:T(8,128)S(1)}, u32[]{:S(2)}, u32[]{:S(2)}) collective-permute-start(f32[6,64,128]{2,1,0:T(8,128)S(1)} %get-tuple-element.19), channel_id=1, source_target_pairs={{0,2},{1,3},{2,4},{3,5},{4,6},{5,7},{6,8},{7,9},{8,10},{9,11},{10,... | collective-permute-start | bytes 589832 | tf_op jit(solution)/shard_map/ppermute | solution.py:45
  114.1 4.9 %copy-start.1 = (f32[24,64,128]{2,1,0:T(8,128)S(1)}, f32[24,64,128]{2,1,0:T(8,128)}, u32[]{:S(2)}) copy-start(f32[24,64,128]{2,1,0:T(8,128)} %copy-done) | copy-start | bytes 2359300
  119.0 11.1 %copy-start.14 = (f32[8,128]{1,0:T(8,128)S(1)}, f32[8,128]{1,0:T(8,128)}, u32[]{:S(2)}) copy-start(f32[8,128]{1,0:T(8,128)} %copy.74) | copy-start | bytes 12292
  119.0 11.1 %copy-start.16 = (f32[8,128]{1,0:T(8,128)S(1)}, f32[8,128]{1,0:T(8,128)}, u32[]{:S(2)}) copy-start(f32[8,128]{1,0:T(8,128)} %copy.72) | copy-start | bytes 12292
  119.1 11.4 %copy-start.13 = (f32[8,128]{1,0:T(8,128)S(1)}, f32[8,128]{1,0:T(8,128)}, u32[]{:S(2)}) copy-start(f32[8,128]{1,0:T(8,128)} %copy.77) | copy-start | bytes 12292
  119.1 11.4 %copy-start.15 = (f32[8,128]{1,0:T(8,128)S(1)}, f32[8,128]{1,0:T(8,128)}, u32[]{:S(2)}) copy-start(f32[8,128]{1,0:T(8,128)} %copy.75) | copy-start | bytes 12292
  119.3 12.1 %collective-permute-start.13 = (bf16[24,64,128]{2,1,0:T(8,128)(2,1)S(1)}, bf16[24,64,128]{2,1,0:T(8,128)(2,1)S(1)}, u32[]{:S(2)}, u32[]{:S(2)}) collective-permute-start(bf16[24,64,128]{2,1,0:T(8,128)(2,1)S(1)} %bitcast_select_fusion.1), channel_id=1, source_target_pairs={{0,1},{1,0},{2,3},{3,2},{4,5},{5,4},{6,7},{7,6},{8,9},{9,8},{10,11... | collective-permute-start | bytes 1179656 | tf_op jit(solution)/shard_map/ppermute | solution.py:50
  (7 other events, 13.2 us)

commit v3 on v2

--- a/solution.py
+++ b/solution.py
@@ -10,7 +10,7 @@
     return lax.ppermute(block, axis, route)
 
 
-def chain_carry(decay, local, chunks):
+def chain_carry(decay, local):
     size, position = (lax.axis_size("ctx"), lax.axis_index("ctx"))
     chips = size // 2
     chip = position // 2
@@ -18,10 +18,8 @@
     low = core == 0
     heads = decay.shape[0]
     half = heads // 2
-    width = half // chunks
     rest = local.shape[1:]
     swap = [(2 * i + j, 2 * i + 1 - j) for i in range(chips) for j in range(2)]
-    ahead = [(i, i + 2) for i in range(size - 2)]
     mine = lax.dynamic_slice_in_dim(local, core * half, half, 0)
     theirs = lax.dynamic_slice_in_dim(local, (1 - core) * half, half, 0)
     got_local = lax.ppermute(theirs, "ctx", swap)
@@ -30,22 +28,16 @@
     decay_lo = lax.dynamic_slice_in_dim(jnp.where(low, decay, got_decay), core * half, half, 0)
     local_lo = jnp.where(low, mine, got_local)
     local_hi = jnp.where(low, got_local, mine)
-    chip_decay = jnp.roll((decay_hi * decay_lo).reshape(chunks, width), chip, axis=0)
-    chip_local = jnp.roll(
-        (decay_hi[:, None, None] * local_lo + local_hi).reshape((chunks, width) + rest), chip, axis=0
-    )
-    received = jnp.zeros((width,) + rest, local.dtype)
-    slots = [received] * chunks
-    for step in range(chunks + chips - 1):
-        k = step - chip
-        valid = (k >= 0) & (k < chunks)
-        j = step % chunks
-        slots[j] = jnp.where(valid, received, slots[j])
-        if step < chunks + chips - 2:
-            received = lax.ppermute(
-                chip_decay[j][:, None, None] * received + chip_local[j], "ctx", ahead
-            )
-    carry_half = jnp.roll(jnp.stack(slots), -chip, axis=0).reshape((half,) + rest)
+    chip_decay = decay_hi * decay_lo
+    chip_local = decay_hi[:, None, None] * local_lo + local_hi
+    one = [(i, i + 2) for i in range(size - 2)]
+    two = [(i, i + 4) for i in range(size - 4)]
+    decay_a, local_a = lax.ppermute((chip_decay, chip_local), "ctx", one)
+    decay_b, local_b = lax.ppermute((decay_a, local_a), "ctx", one)
+    decay_ab = decay_a * decay_b
+    local_ab = decay_a[:, None, None] * local_b + local_a
+    local_c = lax.ppermute(local_ab, "ctx", two)
+    carry_half = decay_ab[:, None, None] * local_c + local_ab
     onward = decay_lo[:, None, None] * carry_half + local_lo
     got_end = lax.ppermute(jnp.where(low, onward, carry_half), "ctx", swap)
     first = jnp.where(low, carry_half, got_end)
@@ -108,7 +100,7 @@
             )
         )
     inner = jnp.concatenate(pieces, axis=1)
-    carry = chain_carry(block_decay, local, 4)
+    carry = chain_carry(block_decay, local)
     carried = carry.astype(jnp.bfloat16)
     outer = (
         jnp.exp(cum)[:, :, None]

time: 136 us -> 126 us (0.926)
  the two profiles are of different devices: /device:TPU:1 before, /device:TPU:183 now
where the time goes in v3:
time: 126 us; the launch traced here: 125 us
  starting transfers between devices  57.6 us (46%)
  waiting for transfers between devices  31.1 us (25%)
  local copies, waits for them, and re-layouts  18.1 us (14%)
  other arithmetic  11.7 us (9%)
  matrix products  6.21 us (5%)
    ppermute x1, starting transfers between devices, chain_carry(): got_end = lax.ppermute(jnp.where(low, onward, carry_half), 'ctx', swap)  22.7 us
    ppermute x2, waiting for transfers between devices, chain_carry(): decay_a, local_a = lax.ppermute((chip_decay, chip_local), 'ctx', one)  17.5 us
    ppermute x1, waiting for transfers between devices, chain_carry(): local_c = lax.ppermute(local_ab, 'ctx', two)  11.5 us
    ppermute x2, starting transfers between devices, chain_carry(): decay_a, local_a = lax.ppermute((chip_decay, chip_local), 'ctx', one)  9.52 us
    ppermute x2, starting transfers between devices, chain_carry(): decay_b, local_b = lax.ppermute((decay_a, local_a), 'ctx', one)  8.5 us
    ppermute x1, starting transfers between devices, chain_carry(): local_c = lax.ppermute(local_ab, 'ctx', two)  7.92 us
    transpose x7, local copies, waits for them, and re-layouts, body(): step_size[:, part_start:part_start + group].T[:, None, :]  4.63 us
    ppermute x1, starting transfers between devices, shifted(): return lax.ppermute(block, axis, route)  4.56 us
  transfers between devices with their start and end apart: 9, of which 6 were waited for; matrix products, arithmetic and copies ran while one was open for 19% of the time, Pallas kernels for 0%

profile of v3, /device:TPU:183, one launch (start us, length us, event | category | flops | bytes accessed | tf_op | source)
XLA Modules:
  0.0 125.0 jit_solution(4538331205995248036)
XLA Ops:
  0.0 0.9 slice.116
  0.9 4.6 %collective-permute-start = (bf16[3,3328]{1,0:T(4,128)(2,1)S(1)}, bf16[3,3328]{1,0:T(4,128)(2,1)S(1)}, u32[]{:S(2)}, u32[]{:S(2)}) collective-permute-start(bf16[3,3328]{1,0:T(4,128)(2,1)S(1)} %slice.116), channel_id=1, source_target_pairs={{0,1},{1,2},{2,3},{3,4},{4,5},{5,6},{6,7},{7,8},{8,9},{9,10},{10,1... | collective-permute-start | bytes 59912 | tf_op jit(solution)/shard_map/ppermute | solution.py:10
  5.5 0.8 reduce-window.15
  8.1 0.8 copy.59
  10.6 1.1 slice_reduce_fusion.3
  11.8 2.6 %multiply_convert_fusion = bf16[128,3328]{1,0:T(8,128)(2,1)S(1)} fusion(bf16[128,3328]{1,0:T(8,128)(2,1)S(1)} %copy-done.1, bf16[3,3328]{1,0:T(4,128)(2,1)S(1)} %collective-permute-done, f32[3328]{0:T(1024)S(1)} %get-tuple-element.7, f32[3328]{0:T(1024)S(1)} %get-tuple-element.8, f32[3328]{0:T(1024)S(1)} %get-tuple-element.6, f32[3328]{0:T(1024)S(1)} %get-tuple-element.5, ...), kind=kLoop, calls=%fused_computation.2 | loop fusion | flops 12353536 | bytes 1790848 | tf_op jit(solution)/shard_map/convert_element_type | solution.py:70
  14.4 0.9 copy-done
  15.8 1.1 fusion.10
  16.9 0.9 constant_dynamic-slice_fusion
  17.8 1.9 %collective-permute-start.4 = (f32[24,64,128]{2,1,0:T(8,128)}, f32[24,64,128]{2,1,0:T(8,128)S(1)}, u32[]{:S(2)}, u32[]{:S(2)}) collective-permute-start(f32[24,64,128]{2,1,0:T(8,128)} %constant_dynamic-slice_fusion), channel_id=1, source_target_pairs={{0,1},{1,0},{2,3},{3,2},{4,5},{5,4},{6,7},{7,6},{8,9},{9,8},{10,11... | collective-permute-start | bytes 2359304 | tf_op jit(solution)/shard_map/ppermute | solution.py:25
  21.0 2.4 %collective-permute-start.1 = (f32[48]{0:T(128)S(1)}, f32[48]{0:T(128)S(1)}, u32[]{:S(2)}, u32[]{:S(2)}) collective-permute-start(f32[48]{0:T(128)S(1)} %exponential_multiply_fusion.1), channel_id=1, source_target_pairs={{0,1},{1,0},{2,3},{3,2},{4,5},{5,4},{6,7},{7,6},{8,9},{9,8},{10,11... | collective-permute-start | bytes 584 | tf_op jit(solution)/shard_map/ppermute | solution.py:26
  23.4 0.8 collective-permute-done.1
  25.7 5.2 %collective-permute-start.5 = (f32[24,64,128]{2,1,0:T(8,128)S(1)}, f32[24,64,128]{2,1,0:T(8,128)}, u32[]{:S(2)}, u32[]{:S(2)}) collective-permute-start(f32[24,64,128]{2,1,0:T(8,128)S(1)} %select_add_fusion), channel_id=1, source_target_pairs={{0,2},{1,3},{2,4},{3,5},{4,6},{5,7},{6,8},{7,9},{8,10},{9,11},{10,... | collective-permute-start | bytes 2359304 | tf_op jit(solution)/shard_map/ppermute | solution.py:35
  30.9 16.6 %collective-permute-done.5 = f32[24,64,128]{2,1,0:T(8,128)} collective-permute-done((f32[24,64,128]{2,1,0:T(8,128)S(1)}, f32[24,64,128]{2,1,0:T(8,128)}, u32[]{:S(2)}, u32[]{:S(2)}) %collective-permute-start.5) | collective-permute-done | bytes 786464 | tf_op jit(solution)/shard_map/ppermute | solution.py:35
  47.5 4.2 %collective-permute-start.6 = (f32[24,64,128]{2,1,0:T(8,128)}, f32[24,64,128]{2,1,0:T(8,128)}, u32[]{:S(2)}, u32[]{:S(2)}) collective-permute-start(f32[24,64,128]{2,1,0:T(8,128)} %collective-permute-done.5), channel_id=1, source_target_pairs={{0,2},{1,3},{2,4},{3,5},{4,6},{5,7},{6,8},{7,9},{8,10},{9,11},{10,... | collective-permute-start | bytes 2359304 | tf_op jit(solution)/shard_map/ppermute | solution.py:36
  51.7 0.8 slice_bitcast_fusion
  53.8 1.5 %copy.79 = f32[128,48]{0,1:T(8,128)} copy(f32[128,48]{1,0:T(8,128)} %get-tuple-element.18) | data formatting | bytes 49152 | tf_op jit(solution)/shard_map/mul | solution.py:106
  55.3 0.9 copy.77
  56.2 0.9 copy.74
  59.9 0.9 copy.75
  61.6 0.8 fusion.52
  62.5 4.3 %collective-permute-start.2 = (f32[24]{0:T(128)}, f32[24]{0:T(128)S(1)}, u32[]{:S(2)}, u32[]{:S(2)}) collective-permute-start(f32[24]{0:T(128)} %get-tuple-element.11), channel_id=1, source_target_pairs={{0,2},{1,3},{2,4},{3,5},{4,6},{5,7},{6,8},{7,9},{8,10},{9,11},{10,... | collective-permute-start | bytes 296 | tf_op jit(solution)/shard_map/ppermute | solution.py:35
  66.8 0.9 collective-permute-done.2
  67.7 4.3 %collective-permute-start.3 = (f32[24]{0:T(128)S(1)}, f32[24]{0:T(128)S(1)}, u32[]{:S(2)}, u32[]{:S(2)}) collective-permute-start(f32[24]{0:T(128)S(1)} %collective-permute-done.2), channel_id=1, source_target_pairs={{0,2},{1,3},{2,4},{3,5},{4,6},{5,7},{6,8},{7,9},{8,10},{9,11},{10,... | collective-permute-start | bytes 296 | tf_op jit(solution)/shard_map/ppermute | solution.py:36
  72.7 0.9 fusion.56
  73.7 1.5 %multiply_add_fusion.2 = f32[24,64,128]{2,1,0:T(8,128)S(1)} fusion(f32[24,64,128]{2,1,0:T(8,128)} %collective-permute-done.5, f32[24,64,128]{2,1,0:T(8,128)} %collective-permute-done.6, f32[24]{0:T(128)S(1)} %collective-permute-done.2), kind=kLoop, calls=%fused_computation.32 | loop fusion | flops 393216 | bytes 2359392 | tf_op jit(solution)/shard_map/add | solution.py:38
  75.2 7.9 %collective-permute-start.7 = (f32[24,64,128]{2,1,0:T(8,128)S(1)}, f32[24,64,128]{2,1,0:T(8,128)S(1)}, u32[]{:S(2)}, u32[]{:S(2)}) collective-permute-start(f32[24,64,128]{2,1,0:T(8,128)S(1)} %multiply_add_fusion.2), channel_id=1, source_target_pairs={{0,4},{1,5},{2,6},{3,7},{4,8},{5,9},{6,10},{7,11},{8,12},{9,13},{1... | collective-permute-start | bytes 2359304 | tf_op jit(solution)/shard_map/ppermute | solution.py:39
  83.1 1.0 fusion.7
  85.3 11.5 %collective-permute-done.7 = f32[24,64,128]{2,1,0:T(8,128)S(1)} collective-permute-done((f32[24,64,128]{2,1,0:T(8,128)S(1)}, f32[24,64,128]{2,1,0:T(8,128)S(1)}, u32[]{:S(2)}, u32[]{:S(2)}) %collective-permute-start.7) | collective-permute-done | bytes 786464 | tf_op jit(solution)/shard_map/ppermute | solution.py:39
  97.1 22.7 %collective-permute-start.8 = (bf16[24,64,128]{2,1,0:T(8,128)(2,1)S(1)}, bf16[24,64,128]{2,1,0:T(8,128)(2,1)S(1)}, u32[]{:S(2)}, u32[]{:S(2)}) collective-permute-start(bf16[24,64,128]{2,1,0:T(8,128)(2,1)S(1)} %get-tuple-element.9), channel_id=1, source_target_pairs={{0,1},{1,0},{2,3},{3,2},{4,5},{5,4},{6,7},{7,6},{8,9},{9,8},{10,11... | collective-permute-start | bytes 1179656 | tf_op jit(solution)/shard_map/ppermute | solution.py:42
  121.9 1.4 %multiply_reduce_fusion = (f32[128,48]{0,1:T(8,128)S(1)}, f32[128,48,64]{0,2,1:T(8,128)S(1)}) fusion(bf16[128,48,64]{0,2,1:T(8,128)(2,1)S(1)} %bitcast.83, f32[48]{0:T(128)S(1)} %copy-done.9, f32[128,48,64]{0,2,1:T(8,128)S(1)} %fusion.2, bf16[24,64,128]{2,1,0:T(8,128)(2,1)S(1)} %get-tuple-element.17, bf16[24,64,128]{2,1,0:T(8,128)(2,1)S(1)} %get-tuple-element.16, ...), kind=kOutput, calls=%fused_computation.6 | convolution fusion | flops 104982528 | bytes 4800704 | tf_op jit(solution)/shard_map/hpn,tn->thp/dot_general | solution.py:108
  123.8 1.2 copy.81
  (67 shorter events, 16.2 us)
Async XLA Ops:
  0.0 11.8 %copy-start.1 = (bf16[128,3328]{1,0:T(8,128)(2,1)S(1)}, bf16[128,3328]{1,0:T(8,128)(2,1)}, u32[]{:S(2)}) copy-start(bf16[128,3328]{1,0:T(8,128)(2,1)} %param.9) | copy-start | bytes 2555908
  0.9 10.9 %collective-permute-start = (bf16[3,3328]{1,0:T(4,128)(2,1)S(1)}, bf16[3,3328]{1,0:T(4,128)(2,1)S(1)}, u32[]{:S(2)}, u32[]{:S(2)}) collective-permute-start(bf16[3,3328]{1,0:T(4,128)(2,1)S(1)} %slice.116), channel_id=1, source_target_pairs={{0,1},{1,2},{2,3},{3,4},{4,5},{5,6},{6,7},{7,8},{8,9},{9,10},{10,1... | collective-permute-start | bytes 59912 | tf_op jit(solution)/shard_map/ppermute | solution.py:10
  14.4 0.9 copy-start
  17.8 7.6 %collective-permute-start.4 = (f32[24,64,128]{2,1,0:T(8,128)}, f32[24,64,128]{2,1,0:T(8,128)S(1)}, u32[]{:S(2)}, u32[]{:S(2)}) collective-permute-start(f32[24,64,128]{2,1,0:T(8,128)} %constant_dynamic-slice_fusion), channel_id=1, source_target_pairs={{0,1},{1,0},{2,3},{3,2},{4,5},{5,4},{6,7},{7,6},{8,9},{9,8},{10,11... | collective-permute-start | bytes 2359304 | tf_op jit(solution)/shard_map/ppermute | solution.py:25
  21.0 3.2 %collective-permute-start.1 = (f32[48]{0:T(128)S(1)}, f32[48]{0:T(128)S(1)}, u32[]{:S(2)}, u32[]{:S(2)}) collective-permute-start(f32[48]{0:T(128)S(1)} %exponential_multiply_fusion.1), channel_id=1, source_target_pairs={{0,1},{1,0},{2,3},{3,2},{4,5},{5,4},{6,7},{7,6},{8,9},{9,8},{10,11... | collective-permute-start | bytes 584 | tf_op jit(solution)/shard_map/ppermute | solution.py:26
  25.5 27.6 %copy-start.4 = (f32[3072]{0:T(1024)S(1)}, f32[3072]{0:T(1024)}, u32[]{:S(2)}) copy-start(f32[3072]{0:T(1024)} %param.17) | copy-start | bytes 36868
  25.7 21.8 %collective-permute-start.5 = (f32[24,64,128]{2,1,0:T(8,128)S(1)}, f32[24,64,128]{2,1,0:T(8,128)}, u32[]{:S(2)}, u32[]{:S(2)}) collective-permute-start(f32[24,64,128]{2,1,0:T(8,128)S(1)} %select_add_fusion), channel_id=1, source_target_pairs={{0,2},{1,3},{2,4},{3,5},{4,6},{5,7},{6,8},{7,9},{8,10},{9,11},{10,... | collective-permute-start | bytes 2359304 | tf_op jit(solution)/shard_map/ppermute | solution.py:35
  47.5 26.1 %collective-permute-start.6 = (f32[24,64,128]{2,1,0:T(8,128)}, f32[24,64,128]{2,1,0:T(8,128)}, u32[]{:S(2)}, u32[]{:S(2)}) collective-permute-start(f32[24,64,128]{2,1,0:T(8,128)} %collective-permute-done.5), channel_id=1, source_target_pairs={{0,2},{1,3},{2,4},{3,5},{4,6},{5,7},{6,8},{7,9},{8,10},{9,11},{10,... | collective-permute-start | bytes 2359304 | tf_op jit(solution)/shard_map/ppermute | solution.py:36
  62.5 5.2 %collective-permute-start.2 = (f32[24]{0:T(128)}, f32[24]{0:T(128)S(1)}, u32[]{:S(2)}, u32[]{:S(2)}) collective-permute-start(f32[24]{0:T(128)} %get-tuple-element.11), channel_id=1, source_target_pairs={{0,2},{1,3},{2,4},{3,5},{4,6},{5,7},{6,8},{7,9},{8,10},{9,11},{10,... | collective-permute-start | bytes 296 | tf_op jit(solution)/shard_map/ppermute | solution.py:35
  67.7 5.0 %collective-permute-start.3 = (f32[24]{0:T(128)S(1)}, f32[24]{0:T(128)S(1)}, u32[]{:S(2)}, u32[]{:S(2)}) collective-permute-start(f32[24]{0:T(128)S(1)} %collective-permute-done.2), channel_id=1, source_target_pairs={{0,2},{1,3},{2,4},{3,5},{4,6},{5,7},{6,8},{7,9},{8,10},{9,11},{10,... | collective-permute-start | bytes 296 | tf_op jit(solution)/shard_map/ppermute | solution.py:36
  73.6 10.5 %copy-start.8 = (f32[8,128]{1,0:T(8,128)S(1)}, f32[8,128]{1,0:T(8,128)}, u32[]{:S(2)}) copy-start(f32[8,128]{1,0:T(8,128)} %copy.65) | copy-start | bytes 12292
  75.2 9.3 %copy-start.7 = (f32[8,128]{1,0:T(8,128)S(1)}, f32[8,128]{1,0:T(8,128)}, u32[]{:S(2)}) copy-start(f32[8,128]{1,0:T(8,128)} %copy.68) | copy-start | bytes 12292
  75.2 21.6 %collective-permute-start.7 = (f32[24,64,128]{2,1,0:T(8,128)S(1)}, f32[24,64,128]{2,1,0:T(8,128)S(1)}, u32[]{:S(2)}, u32[]{:S(2)}) collective-permute-start(f32[24,64,128]{2,1,0:T(8,128)S(1)} %multiply_add_fusion.2), channel_id=1, source_target_pairs={{0,4},{1,5},{2,6},{3,7},{4,8},{5,9},{6,10},{7,11},{8,12},{9,13},{1... | collective-permute-start | bytes 2359304 | tf_op jit(solution)/shard_map/ppermute | solution.py:39
  84.5 12.3 %copy-start.5 = (f32[24]{0:T(128)S(1)}, f32[24]{0:T(128)}, u32[]{:S(2)}) copy-start(f32[24]{0:T(128)} %get-tuple-element.12) | copy-start | bytes 292
  96.8 23.1 %copy-start.6 = (f32[8,128]{1,0:T(8,128)S(1)}, f32[8,128]{1,0:T(8,128)}, u32[]{:S(2)}) copy-start(f32[8,128]{1,0:T(8,128)} %copy.72) | copy-start | bytes 12292
  97.1 24.1 %collective-permute-start.8 = (bf16[24,64,128]{2,1,0:T(8,128)(2,1)S(1)}, bf16[24,64,128]{2,1,0:T(8,128)(2,1)S(1)}, u32[]{:S(2)}, u32[]{:S(2)}) collective-permute-start(bf16[24,64,128]{2,1,0:T(8,128)(2,1)S(1)} %get-tuple-element.9), channel_id=1, source_target_pairs={{0,1},{1,0},{2,3},{3,2},{4,5},{5,4},{6,7},{7,6},{8,9},{9,8},{10,11... | collective-permute-start | bytes 1179656 | tf_op jit(solution)/shard_map/ppermute | solution.py:42
  121.2 0.7 copy-start.3
  121.2 0.7 copy-start.9
  121.9 1.4 %copy-start.2 = (f32[48,64]{1,0:T(8,128)S(1)}, f32[48,64]{1,0:T(8,128)}, u32[]{:S(2)}) copy-start(f32[48,64]{1,0:T(8,128)} %mul.325) | copy-start | bytes 36868

commit v4 on v3

--- a/solution.py
+++ b/solution.py
@@ -10,10 +10,21 @@
     return lax.ppermute(block, axis, route)
 
 
+def packed(decay, local):
+    lanes = local.shape[-1]
+    flat = local.reshape(-1, lanes)
+    spare = jnp.pad(decay, (0, 8 * lanes - decay.shape[0])).reshape(8, lanes)
+    return jnp.concatenate([flat, spare], axis=0)
+
+
+def unpacked(block, heads, rest):
+    rows = block.shape[0] - 8
+    return (block[rows, :heads], block[:rows].reshape((heads,) + rest))
+
+
 def chain_carry(decay, local):
     size, position = (lax.axis_size("ctx"), lax.axis_index("ctx"))
     chips = size // 2
-    chip = position // 2
     core = position % 2
     low = core == 0
     heads = decay.shape[0]
@@ -22,8 +33,10 @@
     swap = [(2 * i + j, 2 * i + 1 - j) for i in range(chips) for j in range(2)]
     mine = lax.dynamic_slice_in_dim(local, core * half, half, 0)
     theirs = lax.dynamic_slice_in_dim(local, (1 - core) * half, half, 0)
-    got_local = lax.ppermute(theirs, "ctx", swap)
-    got_decay = lax.ppermute(decay, "ctx", swap)
+    got = lax.ppermute(packed(decay, theirs), "ctx", swap)
+    rows = half * rest[0]
+    got_local = got[:rows].reshape((half,) + rest)
+    got_decay = got[rows:].reshape(-1)[:heads]
     decay_hi = lax.dynamic_slice_in_dim(jnp.where(low, got_decay, decay), core * half, half, 0)
     decay_lo = lax.dynamic_slice_in_dim(jnp.where(low, decay, got_decay), core * half, half, 0)
     local_lo = jnp.where(low, mine, got_local)
@@ -32,8 +45,10 @@
     chip_local = decay_hi[:, None, None] * local_lo + local_hi
     one = [(i, i + 2) for i in range(size - 2)]
     two = [(i, i + 4) for i in range(size - 4)]
-    decay_a, local_a = lax.ppermute((chip_decay, chip_local), "ctx", one)
-    decay_b, local_b = lax.ppermute((decay_a, local_a), "ctx", one)
+    first_hop = lax.ppermute(packed(chip_decay, chip_local), "ctx", one)
+    second_hop = lax.ppermute(first_hop, "ctx", one)
+    decay_a, local_a = unpacked(first_hop, half, rest)
+    decay_b, local_b = unpacked(second_hop, half, rest)
     decay_ab = decay_a * decay_b
     local_ab = decay_a[:, None, None] * local_b + local_a
     local_c = lax.ppermute(local_ab, "ctx", two)

time: 126 us -> 119 us (0.944)
  the two profiles are of different devices: /device:TPU:183 before, /device:TPU:173 now
where the time goes in v4:
time: 119 us; the launch traced here: 118 us
  waiting for transfers between devices  50.1 us (42%)
  starting transfers between devices  28 us (24%)
  local copies, waits for them, and re-layouts  23.4 us (20%)
  other arithmetic  10.7 us (9%)
  matrix products  5.5 us (5%)
    ppermute x1, waiting for transfers between devices, chain_carry(): local_c = lax.ppermute(local_ab, 'ctx', two)  30 us
    ppermute x1, waiting for transfers between devices, chain_carry(): first_hop = lax.ppermute(packed(chip_decay, chip_local), 'ctx', one)  15.2 us
    transpose x7, local copies, waits for them, and re-layouts, body(): step_size[:, part_start:part_start + group].T[:, None, :]  8.67 us
    ppermute x1, starting transfers between devices, chain_carry(): local_c = lax.ppermute(local_ab, 'ctx', two)  7.44 us
    ppermute x1, starting transfers between devices, chain_carry(): first_hop = lax.ppermute(packed(chip_decay, chip_local), 'ctx', one)  5.21 us
    ppermute x1, starting transfers between devices, chain_carry(): got_end = lax.ppermute(jnp.where(low, onward, carry_half), 'ctx', swap)  4.65 us
    ppermute x1, starting transfers between devices, shifted(): return lax.ppermute(block, axis, route)  4.56 us
    ppermute x1, starting transfers between devices, chain_carry(): second_hop = lax.ppermute(first_hop, 'ctx', one)  4.2 us
  transfers between devices with their start and end apart: 6, of which 5 were waited for; matrix products, arithmetic and copies ran while one was open for 22% of the time, Pallas kernels for 0%

profile of v4, /device:TPU:173, one launch (start us, length us, event | category | flops | bytes accessed | tf_op | source)
XLA Modules:
  0.0 118.0 jit_solution(13715797281702117484)
XLA Ops:
  0.0 0.9 slice.137
  0.9 4.6 %collective-permute-start = (bf16[3,3328]{1,0:T(4,128)(2,1)S(1)}, bf16[3,3328]{1,0:T(4,128)(2,1)S(1)}, u32[]{:S(2)}, u32[]{:S(2)}) collective-permute-start(bf16[3,3328]{1,0:T(4,128)(2,1)S(1)} %slice.137), channel_id=1, source_target_pairs={{0,1},{1,2},{2,3},{3,4},{4,5},{5,6},{6,7},{7,8},{8,9},{9,10},{10,1... | collective-permute-start | bytes 59912 | tf_op jit(solution)/shard_map/ppermute | solution.py:10
  5.5 0.8 reduce-window.15
  8.7 0.8 copy.59
  9.5 1.1 slice_reduce_fusion.3
  13.0 2.6 %multiply_convert_fusion = bf16[128,3328]{1,0:T(8,128)(2,1)S(1)} fusion(bf16[128,3328]{1,0:T(8,128)(2,1)S(1)} %copy-done.1, bf16[3,3328]{1,0:T(4,128)(2,1)S(1)} %collective-permute-done, f32[3328]{0:T(1024)S(1)} %get-tuple-element.7, f32[3328]{0:T(1024)S(1)} %get-tuple-element.8, f32[3328]{0:T(1024)S(1)} %get-tuple-element.6, f32[3328]{0:T(1024)S(1)} %get-tuple-element.5, ...), kind=kLoop, calls=%fused_computation.2 | loop fusion | flops 12353536 | bytes 1790848 | tf_op jit(solution)/shard_map/convert_element_type | solution.py:85
  16.5 0.9 pad_maximum_fusion.1
  17.4 1.9 %collective-permute-start.1 = (f32[1544,128]{1,0:T(8,128)}, f32[1544,128]{1,0:T(8,128)}, u32[]{:S(2)}, u32[]{:S(2)}) collective-permute-start(f32[1544,128]{1,0:T(8,128)} %pad_maximum_fusion.1), channel_id=1, source_target_pairs={{0,1},{1,0},{2,3},{3,2},{4,5},{5,4},{6,7},{7,6},{8,9},{9,8},{10,11... | collective-permute-start | bytes 2371592 | tf_op jit(solution)/shard_map/ppermute | solution.py:36
  19.4 2.6 %collective-permute-done.1 = f32[1544,128]{1,0:T(8,128)} collective-permute-done((f32[1544,128]{1,0:T(8,128)}, f32[1544,128]{1,0:T(8,128)}, u32[]{:S(2)}, u32[]{:S(2)}) %collective-permute-start.1) | collective-permute-done | bytes 790560 | tf_op jit(solution)/shard_map/ppermute | solution.py:36
  23.4 1.2 %slice.198 = f32[1536,128]{1,0:T(8,128)S(1)} slice(f32[1544,128]{1,0:T(8,128)} %collective-permute-done.1), slice={[0:1536], [0:128]} | slice | bytes 1572864 | tf_op jit(solution)/shard_map/slice | solution.py:38
  24.8 5.2 %collective-permute-start.2 = (f32[1544,128]{1,0:T(8,128)S(1)}, f32[1544,128]{1,0:T(8,128)}, u32[]{:S(2)}, u32[]{:S(2)}) collective-permute-start(f32[1544,128]{1,0:T(8,128)S(1)} %pad_maximum_fusion.2), channel_id=1, source_target_pairs={{0,2},{1,3},{2,4},{3,5},{4,6},{5,7},{6,8},{7,9},{8,10},{9,11},{10,... | collective-permute-start | bytes 2371592 | tf_op jit(solution)/shard_map/ppermute | solution.py:48
  30.1 0.8 slice_bitcast_fusion
  31.7 15.2 %collective-permute-done.2 = f32[1544,128]{1,0:T(8,128)} collective-permute-done((f32[1544,128]{1,0:T(8,128)S(1)}, f32[1544,128]{1,0:T(8,128)}, u32[]{:S(2)}, u32[]{:S(2)}) %collective-permute-start.2) | collective-permute-done | bytes 790560 | tf_op jit(solution)/shard_map/ppermute | solution.py:48
  46.9 4.2 %collective-permute-start.3 = (f32[1544,128]{1,0:T(8,128)}, f32[1544,128]{1,0:T(8,128)}, u32[]{:S(2)}, u32[]{:S(2)}) collective-permute-start(f32[1544,128]{1,0:T(8,128)} %collective-permute-done.2), channel_id=1, source_target_pairs={{0,2},{1,3},{2,4},{3,5},{4,6},{5,7},{6,8},{7,9},{8,10},{9,11},{10,... | collective-permute-start | bytes 2371592 | tf_op jit(solution)/shard_map/ppermute | solution.py:49
  51.3 0.9 copy.79
  52.2 0.9 copy.77
  53.1 0.9 copy.74
  54.0 1.5 %copy.71 = f32[8,128]{1,0:T(8,128)} copy(f32[8,128]{0,1:T(8,128)} %get-tuple-element.28) | data formatting | bytes 8192 | tf_op jit(solution)/shard_map/transpose | solution.py:107
  55.5 1.5 %copy.68 = f32[8,128]{1,0:T(8,128)} copy(f32[8,128]{0,1:T(8,128)} %get-tuple-element.29) | data formatting | bytes 8192 | tf_op jit(solution)/shard_map/transpose | solution.py:107
  57.0 1.5 %copy.65 = f32[8,128]{1,0:T(8,128)} copy(f32[8,128]{0,1:T(8,128)} %get-tuple-element.30) | data formatting | bytes 8192 | tf_op jit(solution)/shard_map/transpose | solution.py:107
  58.5 1.5 %copy.62 = f32[8,128]{1,0:T(8,128)} copy(f32[8,128]{0,1:T(8,128)} %get-tuple-element.31) | data formatting | bytes 8192 | tf_op jit(solution)/shard_map/transpose | solution.py:107
  60.0 0.9 copy.75
  61.9 0.9 fusion.56
  62.8 1.1 fusion.7
  63.9 1.2 %slice.202 = f32[1536,128]{1,0:T(8,128)S(1)} slice(f32[1544,128]{1,0:T(8,128)} %collective-permute-done.2), slice={[0:1536], [0:128]} | slice | bytes 1572864 | tf_op jit(solution)/shard_map/slice | solution.py:22
  65.7 1.7 %collective-permute-done.3 = f32[1544,128]{1,0:T(8,128)} collective-permute-done((f32[1544,128]{1,0:T(8,128)}, f32[1544,128]{1,0:T(8,128)}, u32[]{:S(2)}, u32[]{:S(2)}) %collective-permute-start.3) | collective-permute-done | bytes 790560 | tf_op jit(solution)/shard_map/ppermute | solution.py:49
  67.4 1.2 %slice.201 = f32[1536,128]{1,0:T(8,128)S(1)} slice(f32[1544,128]{1,0:T(8,128)} %collective-permute-done.3), slice={[0:1536], [0:128]} | slice | bytes 1572864 | tf_op jit(solution)/shard_map/slice | solution.py:22
  68.8 7.4 %collective-permute-start.4 = (f32[24,64,128]{2,1,0:T(8,128)S(1)}, f32[24,64,128]{2,1,0:T(8,128)S(1)}, u32[]{:S(2)}, u32[]{:S(2)}) collective-permute-start(f32[24,64,128]{2,1,0:T(8,128)S(1)} %multiply_add_fusion.2), channel_id=1, source_target_pairs={{0,4},{1,5},{2,6},{3,7},{4,8},{5,9},{6,10},{7,11},{8,12},{9,13},{1... | collective-permute-start | bytes 2359304 | tf_op jit(solution)/shard_map/ppermute | solution.py:54
  78.0 30.0 %collective-permute-done.4 = f32[24,64,128]{2,1,0:T(8,128)S(1)} collective-permute-done((f32[24,64,128]{2,1,0:T(8,128)S(1)}, f32[24,64,128]{2,1,0:T(8,128)S(1)}, u32[]{:S(2)}, u32[]{:S(2)}) %collective-permute-start.4) | collective-permute-done | bytes 786464 | tf_op jit(solution)/shard_map/ppermute | solution.py:54
  108.3 4.7 %collective-permute-start.5 = (bf16[24,64,128]{2,1,0:T(8,128)(2,1)S(1)}, bf16[24,64,128]{2,1,0:T(8,128)(2,1)S(1)}, u32[]{:S(2)}, u32[]{:S(2)}) collective-permute-start(bf16[24,64,128]{2,1,0:T(8,128)(2,1)S(1)} %get-tuple-element.9), channel_id=1, source_target_pairs={{0,1},{1,0},{2,3},{3,2},{4,5},{5,4},{6,7},{7,6},{8,9},{9,8},{10,11... | collective-permute-start | bytes 1179656 | tf_op jit(solution)/shard_map/ppermute | solution.py:57
  115.0 1.3 %multiply_reduce_fusion = (f32[128,48]{0,1:T(8,128)S(1)}, f32[128,48,64]{0,2,1:T(8,128)S(1)}) fusion(bf16[128,48,64]{0,2,1:T(8,128)(2,1)S(1)} %bitcast.105, f32[48]{0:T(128)S(1)} %copy-done.7, f32[128,48,64]{0,2,1:T(8,128)S(1)} %fusion.2, bf16[24,64,128]{2,1,0:T(8,128)(2,1)S(1)} %get-tuple-element.17, bf16[24,64,128]{2,1,0:T(8,128)(2,1)S(1)} %get-tuple-element.16, ...), kind=kOutput, calls=%fused_computation.6 | convolution fusion | flops 104982528 | bytes 4800704 | tf_op jit(solution)/shard_map/hpn,tn->thp/dot_general | solution.py:123
  116.8 1.2 copy.81
  (66 shorter events, 14.5 us)
Async XLA Ops:
  0.0 13.0 %copy-start.1 = (bf16[128,3328]{1,0:T(8,128)(2,1)S(1)}, bf16[128,3328]{1,0:T(8,128)(2,1)}, u32[]{:S(2)}) copy-start(bf16[128,3328]{1,0:T(8,128)(2,1)} %param.9) | copy-start | bytes 2555908
  0.9 12.0 %collective-permute-start = (bf16[3,3328]{1,0:T(4,128)(2,1)S(1)}, bf16[3,3328]{1,0:T(4,128)(2,1)S(1)}, u32[]{:S(2)}, u32[]{:S(2)}) collective-permute-start(bf16[3,3328]{1,0:T(4,128)(2,1)S(1)} %slice.137), channel_id=1, source_target_pairs={{0,1},{1,2},{2,3},{3,4},{4,5},{5,6},{6,7},{7,8},{8,9},{9,10},{10,1... | collective-permute-start | bytes 59912 | tf_op jit(solution)/shard_map/ppermute | solution.py:10
  15.6 7.8 %copy-start = (bf16[128,3328]{1,0:T(8,128)(2,1)}, bf16[128,3328]{1,0:T(8,128)(2,1)S(1)}, u32[]{:S(2)}) copy-start(bf16[128,3328]{1,0:T(8,128)(2,1)S(1)} %multiply_convert_fusion) | copy-start | bytes 2555908
  17.4 4.5 %collective-permute-start.1 = (f32[1544,128]{1,0:T(8,128)}, f32[1544,128]{1,0:T(8,128)}, u32[]{:S(2)}, u32[]{:S(2)}) collective-permute-start(f32[1544,128]{1,0:T(8,128)} %pad_maximum_fusion.1), channel_id=1, source_target_pairs={{0,1},{1,0},{2,3},{3,2},{4,5},{5,4},{6,7},{7,6},{8,9},{9,8},{10,11... | collective-permute-start | bytes 2371592 | tf_op jit(solution)/shard_map/ppermute | solution.py:36
  24.8 26.5 %copy-start.2 = (f32[3072]{0:T(1024)S(1)}, f32[3072]{0:T(1024)}, u32[]{:S(2)}) copy-start(f32[3072]{0:T(1024)} %param.17) | copy-start | bytes 36868
  24.8 22.1 %collective-permute-start.2 = (f32[1544,128]{1,0:T(8,128)S(1)}, f32[1544,128]{1,0:T(8,128)}, u32[]{:S(2)}, u32[]{:S(2)}) collective-permute-start(f32[1544,128]{1,0:T(8,128)S(1)} %pad_maximum_fusion.2), channel_id=1, source_target_pairs={{0,2},{1,3},{2,4},{3,5},{4,6},{5,7},{6,8},{7,9},{8,10},{9,11},{10,... | collective-permute-start | bytes 2371592 | tf_op jit(solution)/shard_map/ppermute | solution.py:48
  46.9 20.5 %collective-permute-start.3 = (f32[1544,128]{1,0:T(8,128)}, f32[1544,128]{1,0:T(8,128)}, u32[]{:S(2)}, u32[]{:S(2)}) collective-permute-start(f32[1544,128]{1,0:T(8,128)} %collective-permute-done.2), channel_id=1, source_target_pairs={{0,2},{1,3},{2,4},{3,5},{4,6},{5,7},{6,8},{7,9},{8,10},{9,11},{10,... | collective-permute-start | bytes 2371592 | tf_op jit(solution)/shard_map/ppermute | solution.py:49
  68.6 7.6 %copy-start.6 = (f32[8,128]{1,0:T(8,128)S(1)}, f32[8,128]{1,0:T(8,128)}, u32[]{:S(2)}) copy-start(f32[8,128]{1,0:T(8,128)} %copy.65) | copy-start | bytes 12292
  68.6 8.0 %copy-start.5 = (f32[8,128]{1,0:T(8,128)S(1)}, f32[8,128]{1,0:T(8,128)}, u32[]{:S(2)}) copy-start(f32[8,128]{1,0:T(8,128)} %copy.68) | copy-start | bytes 12292
  68.8 8.2 %copy-start.4 = (f32[8,128]{1,0:T(8,128)S(1)}, f32[8,128]{1,0:T(8,128)}, u32[]{:S(2)}) copy-start(f32[8,128]{1,0:T(8,128)} %copy.71) | copy-start | bytes 12292
  68.8 39.2 %collective-permute-start.4 = (f32[24,64,128]{2,1,0:T(8,128)S(1)}, f32[24,64,128]{2,1,0:T(8,128)S(1)}, u32[]{:S(2)}, u32[]{:S(2)}) collective-permute-start(f32[24,64,128]{2,1,0:T(8,128)S(1)} %multiply_add_fusion.2), channel_id=1, source_target_pairs={{0,4},{1,5},{2,6},{3,7},{4,8},{5,9},{6,10},{7,11},{8,12},{9,13},{1... | collective-permute-start | bytes 2359304 | tf_op jit(solution)/shard_map/ppermute | solution.py:54
  108.0 5.0 %copy-start.3 = (f32[8,128]{1,0:T(8,128)S(1)}, f32[8,128]{1,0:T(8,128)}, u32[]{:S(2)}) copy-start(f32[8,128]{1,0:T(8,128)} %copy.72) | copy-start | bytes 12292
  108.3 6.0 %collective-permute-start.5 = (bf16[24,64,128]{2,1,0:T(8,128)(2,1)S(1)}, bf16[24,64,128]{2,1,0:T(8,128)(2,1)S(1)}, u32[]{:S(2)}, u32[]{:S(2)}) collective-permute-start(bf16[24,64,128]{2,1,0:T(8,128)(2,1)S(1)} %get-tuple-element.9), channel_id=1, source_target_pairs={{0,1},{1,0},{2,3},{3,2},{4,5},{5,4},{6,7},{7,6},{8,9},{9,8},{10,11... | collective-permute-start | bytes 1179656 | tf_op jit(solution)/shard_map/ppermute | solution.py:57
  114.3 0.7 copy-start.7

commit v5 on v4

--- a/solution.py
+++ b/solution.py
@@ -51,7 +51,7 @@
     decay_b, local_b = unpacked(second_hop, half, rest)
     decay_ab = decay_a * decay_b
     local_ab = decay_a[:, None, None] * local_b + local_a
-    local_c = lax.ppermute(local_ab, "ctx", two)
+    local_c = lax.ppermute(local_ab.astype(jnp.bfloat16), "ctx", two).astype(jnp.float32)
     carry_half = decay_ab[:, None, None] * local_c + local_ab
     onward = decay_lo[:, None, None] * carry_half + local_lo
     got_end = lax.ppermute(jnp.where(low, onward, carry_half), "ctx", swap)

time: 119 us -> 103 us (0.87)
  waiting for transfers between devices: 50.1 us -> 34.4 us
  local copies, waits for them, and re-layouts: 23.4 us -> 20.1 us
  other arithmetic: 10.7 us -> 13 us
    ppermute x1, waiting for transfers between devices: 30 us -> 13.9 us  [chain_carry(): lax.ppermute(local_ab.astype(jnp.bfloat16), 'ctx', two).astype(jnp.float32)]
    ppermute x1, waiting for transfers between devices: 1.69 us -> 11.9 us  [chain_carry(): second_hop = lax.ppermute(first_hop, 'ctx', one)]
    ppermute x1, waiting for transfers between devices: 15.2 us -> 5.38 us  [chain_carry(): first_hop = lax.ppermute(packed(chip_decay, chip_local), 'ctx', one)]
    transpose x7, local copies, waits for them, and re-layouts: 8.67 us -> 5.22 us  [body(): step_size[:, part_start:part_start + group].T[:, None, :]]
  transfers between devices with their start and end apart: 6 -> 6, of which waited for: 5 -> 5; matrix products, arithmetic and copies ran while one was open for 22% -> 25% of each run, Pallas kernels for 0% -> 0%
where the time goes in v5:
time: 103 us; the launch traced here: 102 us
  waiting for transfers between devices  34.4 us (33%)
  starting transfers between devices  27.8 us (27%)
  local copies, waits for them, and re-layouts  20.1 us (20%)
  other arithmetic  13 us (13%)
  matrix products  6.14 us (6%)
    ppermute x1, waiting for transfers between devices, chain_carry(): lax.ppermute(local_ab.astype(jnp.bfloat16), 'ctx', two).astype(jnp.float32)  13.9 us
    ppermute x1, waiting for transfers between devices, chain_carry(): second_hop = lax.ppermute(first_hop, 'ctx', one)  11.9 us
    ppermute x1, starting transfers between devices, chain_carry(): lax.ppermute(local_ab.astype(jnp.bfloat16), 'ctx', two).astype(jnp.float32)  7.34 us
    ppermute x1, waiting for transfers between devices, chain_carry(): first_hop = lax.ppermute(packed(chip_decay, chip_local), 'ctx', one)  5.38 us
    transpose x7, local copies, waits for them, and re-layouts, body(): step_size[:, part_start:part_start + group].T[:, None, :]  5.22 us
    ppermute x1, starting transfers between devices, chain_carry(): first_hop = lax.ppermute(packed(chip_decay, chip_local), 'ctx', one)  5.2 us
    ppermute x1, starting transfers between devices, chain_carry(): got_end = lax.ppermute(jnp.where(low, onward, carry_half), 'ctx', swap)  4.65 us
    ppermute x1, starting transfers between devices, shifted(): return lax.ppermute(block, axis, route)  4.56 us
  transfers between devices with their start and end apart: 6, of which 5 were waited for; matrix products, arithmetic and copies ran while one was open for 25% of the time, Pallas kernels for 0%

profile of v5, /device:TPU:173, one launch (start us, length us, event | category | flops | bytes accessed | tf_op | source)
XLA Modules:
  0.0 101.7 jit_solution(1492448168057092697)
XLA Ops:
  0.0 0.9 slice.137
  0.9 4.6 %collective-permute-start = (bf16[3,3328]{1,0:T(4,128)(2,1)S(1)}, bf16[3,3328]{1,0:T(4,128)(2,1)S(1)}, u32[]{:S(2)}, u32[]{:S(2)}) collective-permute-start(bf16[3,3328]{1,0:T(4,128)(2,1)S(1)} %slice.137), channel_id=1, source_target_pairs={{0,1},{1,2},{2,3},{3,4},{4,5},{5,6},{6,7},{7,8},{8,9},{9,10},{10,1... | collective-permute-start | bytes 59912 | tf_op jit(solution)/shard_map/ppermute | solution.py:10
  5.5 0.8 reduce-window.15
  8.7 0.8 copy.59
  9.5 1.1 %slice_reduce_fusion.3 = (f32[3328]{0:T(1024)S(1)}, f32[3328]{0:T(1024)S(1)}, f32[3328]{0:T(1024)S(1)}, f32[3328]{0:T(1024)S(1)}) fusion(f32[4,3328]{1,0:T(4,128)} %param.12), kind=kLoop, calls=%fused_computation.112 | loop fusion | bytes 106496 | tf_op jit(solution)/shard_map/slice | solution.py:80
  10.6 0.7 negate_multiply_fusion
  13.0 2.6 %multiply_convert_fusion = bf16[128,3328]{1,0:T(8,128)(2,1)S(1)} fusion(bf16[128,3328]{1,0:T(8,128)(2,1)S(1)} %copy-done.1, bf16[3,3328]{1,0:T(4,128)(2,1)S(1)} %collective-permute-done, f32[3328]{0:T(1024)S(1)} %get-tuple-element.7, f32[3328]{0:T(1024)S(1)} %get-tuple-element.8, f32[3328]{0:T(1024)S(1)} %get-tuple-element.6, f32[3328]{0:T(1024)S(1)} %get-tuple-element.5, ...), kind=kLoop, calls=%fused_computation.2 | loop fusion | flops 12353536 | bytes 1790848 | tf_op jit(solution)/shard_map/convert_element_type | solution.py:85
  16.5 1.0 pad_maximum_fusion.1
  17.5 1.9 %collective-permute-start.1 = (f32[1544,128]{1,0:T(8,128)}, f32[1544,128]{1,0:T(8,128)}, u32[]{:S(2)}, u32[]{:S(2)}) collective-permute-start(f32[1544,128]{1,0:T(8,128)} %pad_maximum_fusion.1), channel_id=1, source_target_pairs={{0,1},{1,0},{2,3},{3,2},{4,5},{5,4},{6,7},{7,6},{8,9},{9,8},{10,11... | collective-permute-start | bytes 2371592 | tf_op jit(solution)/shard_map/ppermute | solution.py:36
  19.4 2.6 %collective-permute-done.1 = f32[1544,128]{1,0:T(8,128)} collective-permute-done((f32[1544,128]{1,0:T(8,128)}, f32[1544,128]{1,0:T(8,128)}, u32[]{:S(2)}, u32[]{:S(2)}) %collective-permute-start.1) | collective-permute-done | bytes 790560 | tf_op jit(solution)/shard_map/ppermute | solution.py:36
  23.9 1.2 %slice.198 = f32[1536,128]{1,0:T(8,128)S(1)} slice(f32[1544,128]{1,0:T(8,128)} %collective-permute-done.1), slice={[0:1536], [0:128]} | slice | bytes 1572864 | tf_op jit(solution)/shard_map/slice | solution.py:38
  25.3 1.0 pad_maximum_fusion.2
  26.2 5.2 %collective-permute-start.2 = (f32[1544,128]{1,0:T(8,128)}, f32[1544,128]{1,0:T(8,128)}, u32[]{:S(2)}, u32[]{:S(2)}) collective-permute-start(f32[1544,128]{1,0:T(8,128)} %pad_maximum_fusion.2), channel_id=1, source_target_pairs={{0,2},{1,3},{2,4},{3,5},{4,6},{5,7},{6,8},{7,9},{8,10},{9,11},{10,... | collective-permute-start | bytes 2371592 | tf_op jit(solution)/shard_map/ppermute | solution.py:48
  31.4 0.8 slice_bitcast_fusion
  33.5 1.5 %copy.79 = f32[128,48]{0,1:T(8,128)} copy(f32[128,48]{1,0:T(8,128)} %get-tuple-element.18) | data formatting | bytes 49152 | tf_op jit(solution)/shard_map/mul | solution.py:121
  35.1 0.9 copy.77
  35.9 0.9 copy.74
  39.5 0.8 slice_bitcast_fusion.1
  40.3 0.9 copy.75
  41.5 0.8 fusion.53
  42.3 0.9 fusion.57
  43.3 5.4 %collective-permute-done.2 = f32[1544,128]{1,0:T(8,128)} collective-permute-done((f32[1544,128]{1,0:T(8,128)}, f32[1544,128]{1,0:T(8,128)}, u32[]{:S(2)}, u32[]{:S(2)}) %collective-permute-start.2) | collective-permute-done | bytes 790560 | tf_op jit(solution)/shard_map/ppermute | solution.py:48
  48.6 4.1 %collective-permute-start.3 = (f32[1544,128]{1,0:T(8,128)}, f32[1544,128]{1,0:T(8,128)S(1)}, u32[]{:S(2)}, u32[]{:S(2)}) collective-permute-start(f32[1544,128]{1,0:T(8,128)} %collective-permute-done.2), channel_id=1, source_target_pairs={{0,2},{1,3},{2,4},{3,5},{4,6},{5,7},{6,8},{7,9},{8,10},{9,11},{10,... | collective-permute-start | bytes 2371592 | tf_op jit(solution)/shard_map/ppermute | solution.py:49
  52.7 1.0 %fusion.7 = f32[128,48,64]{0,2,1:T(8,128)S(1)} fusion(bf16[128,48,64]{0,2,1:T(8,128)(2,1)S(1)} %bitcast.99, f32[8,128]{1,0:T(8,128)} %copy.62, f32[8,128]{1,0:T(8,128)S(1)} %copy.60, f32[128,128]{1,0:T(8,128)S(1)} %fusion.57, pred[128,128]{1,0:T(8,128)(4,1)S(1)} %fusion.53), kind=kOutput, calls=%fused_computation.20 | convolution fusion | flops 17563648 | bytes 1142784 | tf_op jit(solution)/shard_map/hts,shp->thp/dot_general | solution.py:110
  53.8 1.0 %fusion.6 = f32[128,48,64]{0,2,1:T(8,128)S(1)} fusion(f32[128,48,64]{0,2,1:T(8,128)S(1)} %fusion.7, bf16[128,48,64]{0,2,1:T(8,128)(2,1)S(1)} %bitcast.100, f32[8,128]{1,0:T(8,128)} %copy.65, f32[8,128]{1,0:T(8,128)S(1)} %copy.63, f32[128,128]{1,0:T(8,128)S(1)} %fusion.57, pred[128,128]{1,0:T(8,128)(4,1)S(1)} %fusion.53), kind=kOutput, calls=%fused_computation.18 | convolution fusion | flops 17563648 | bytes 1142784 | tf_op jit(solution)/shard_map/hts,shp->thp/dot_general | solution.py:110
  55.2 1.2 %slice.202 = f32[1536,128]{1,0:T(8,128)S(1)} slice(f32[1544,128]{1,0:T(8,128)} %collective-permute-done.2), slice={[0:1536], [0:128]} | slice | bytes 1572864 | tf_op jit(solution)/shard_map/slice | solution.py:22
  57.1 11.9 %collective-permute-done.3 = f32[1544,128]{1,0:T(8,128)S(1)} collective-permute-done((f32[1544,128]{1,0:T(8,128)}, f32[1544,128]{1,0:T(8,128)S(1)}, u32[]{:S(2)}, u32[]{:S(2)}) %collective-permute-start.3) | collective-permute-done | bytes 790560 | tf_op jit(solution)/shard_map/ppermute | solution.py:49
  69.2 7.3 %collective-permute-start.4 = (bf16[24,64,128]{2,1,0:T(8,128)(2,1)S(1)}, bf16[24,64,128]{2,1,0:T(8,128)(2,1)S(1)}, u32[]{:S(2)}, u32[]{:S(2)}) collective-permute-start(bf16[24,64,128]{2,1,0:T(8,128)(2,1)S(1)} %fusion.52), channel_id=1, source_target_pairs={{0,4},{1,5},{2,6},{3,7},{4,8},{5,9},{6,10},{7,11},{8,12},{9,13},{1... | collective-permute-start | bytes 1179656 | tf_op jit(solution)/shard_map/ppermute | solution.py:54
  77.6 13.9 %collective-permute-done.4 = bf16[24,64,128]{2,1,0:T(8,128)(2,1)S(1)} collective-permute-done((bf16[24,64,128]{2,1,0:T(8,128)(2,1)S(1)}, bf16[24,64,128]{2,1,0:T(8,128)(2,1)S(1)}, u32[]{:S(2)}, u32[]{:S(2)}) %collective-permute-start.4) | collective-permute-done | bytes 393248 | tf_op jit(solution)/shard_map/ppermute | solution.py:54
  91.9 4.7 %collective-permute-start.5 = (bf16[24,64,128]{2,1,0:T(8,128)(2,1)S(1)}, bf16[24,64,128]{2,1,0:T(8,128)(2,1)S(1)}, u32[]{:S(2)}, u32[]{:S(2)}) collective-permute-start(bf16[24,64,128]{2,1,0:T(8,128)(2,1)S(1)} %get-tuple-element.9), channel_id=1, source_target_pairs={{0,1},{1,0},{2,3},{3,2},{4,5},{5,4},{6,7},{7,6},{8,9},{9,8},{10,11... | collective-permute-start | bytes 1179656 | tf_op jit(solution)/shard_map/ppermute | solution.py:57
  98.6 1.4 %multiply_reduce_fusion = (f32[128,48]{0,1:T(8,128)S(1)}, f32[128,48,64]{0,2,1:T(8,128)S(1)}) fusion(bf16[128,48,64]{0,2,1:T(8,128)(2,1)S(1)} %bitcast.105, f32[48]{0:T(128)S(1)} %copy-done.8, f32[128,48,64]{0,2,1:T(8,128)S(1)} %fusion.2, bf16[24,64,128]{2,1,0:T(8,128)(2,1)S(1)} %get-tuple-element.17, bf16[24,64,128]{2,1,0:T(8,128)(2,1)S(1)} %get-tuple-element.16, ...), kind=kOutput, calls=%fused_computation.6 | convolution fusion | flops 104982528 | bytes 4800704 | tf_op jit(solution)/shard_map/hpn,tn->thp/dot_general | solution.py:123
  100.5 1.2 %copy.81 = bf16[128,3072]{1,0:T(8,128)(2,1)} copy(bf16[128,3072]{0,1:T(8,128)(2,1)S(1)} %bitcast.111) | data formatting | bytes 1572864 | tf_op jit(solution)/shard_map/reshape | solution.py:131
  (68 shorter events, 16.4 us)
Async XLA Ops:
  0.0 13.0 %copy-start.1 = (bf16[128,3328]{1,0:T(8,128)(2,1)S(1)}, bf16[128,3328]{1,0:T(8,128)(2,1)}, u32[]{:S(2)}) copy-start(bf16[128,3328]{1,0:T(8,128)(2,1)} %param.9) | copy-start | bytes 2555908
  0.9 12.0 %collective-permute-start = (bf16[3,3328]{1,0:T(4,128)(2,1)S(1)}, bf16[3,3328]{1,0:T(4,128)(2,1)S(1)}, u32[]{:S(2)}, u32[]{:S(2)}) collective-permute-start(bf16[3,3328]{1,0:T(4,128)(2,1)S(1)} %slice.137), channel_id=1, source_target_pairs={{0,1},{1,2},{2,3},{3,4},{4,5},{5,6},{6,7},{7,8},{8,9},{9,10},{10,1... | collective-permute-start | bytes 59912 | tf_op jit(solution)/shard_map/ppermute | solution.py:10
  15.6 8.3 %copy-start = (bf16[128,3328]{1,0:T(8,128)(2,1)}, bf16[128,3328]{1,0:T(8,128)(2,1)S(1)}, u32[]{:S(2)}) copy-start(bf16[128,3328]{1,0:T(8,128)(2,1)S(1)} %multiply_convert_fusion) | copy-start | bytes 2555908
  17.5 4.5 %collective-permute-start.1 = (f32[1544,128]{1,0:T(8,128)}, f32[1544,128]{1,0:T(8,128)}, u32[]{:S(2)}, u32[]{:S(2)}) collective-permute-start(f32[1544,128]{1,0:T(8,128)} %pad_maximum_fusion.1), channel_id=1, source_target_pairs={{0,1},{1,0},{2,3},{3,2},{4,5},{5,4},{6,7},{7,6},{8,9},{9,8},{10,11... | collective-permute-start | bytes 2371592 | tf_op jit(solution)/shard_map/ppermute | solution.py:36
  25.3 7.6 %copy-start.4 = (f32[3072]{0:T(1024)S(1)}, f32[3072]{0:T(1024)}, u32[]{:S(2)}) copy-start(f32[3072]{0:T(1024)} %param.17) | copy-start | bytes 36868
  26.2 22.4 %collective-permute-start.2 = (f32[1544,128]{1,0:T(8,128)}, f32[1544,128]{1,0:T(8,128)}, u32[]{:S(2)}, u32[]{:S(2)}) collective-permute-start(f32[1544,128]{1,0:T(8,128)} %pad_maximum_fusion.2), channel_id=1, source_target_pairs={{0,2},{1,3},{2,4},{3,5},{4,6},{5,7},{6,8},{7,9},{8,10},{9,11},{10,... | collective-permute-start | bytes 2371592 | tf_op jit(solution)/shard_map/ppermute | solution.py:48
  43.2 11.6 %copy-start.7 = (f32[8,128]{1,0:T(8,128)S(1)}, f32[8,128]{1,0:T(8,128)}, u32[]{:S(2)}) copy-start(f32[8,128]{1,0:T(8,128)} %copy.68) | copy-start | bytes 12292
  48.6 20.4 %collective-permute-start.3 = (f32[1544,128]{1,0:T(8,128)}, f32[1544,128]{1,0:T(8,128)S(1)}, u32[]{:S(2)}, u32[]{:S(2)}) collective-permute-start(f32[1544,128]{1,0:T(8,128)} %collective-permute-done.2), channel_id=1, source_target_pairs={{0,2},{1,3},{2,4},{3,5},{4,6},{5,7},{6,8},{7,9},{8,10},{9,11},{10,... | collective-permute-start | bytes 2371592 | tf_op jit(solution)/shard_map/ppermute | solution.py:49
  57.1 19.5 %copy-start.6 = (f32[8,128]{1,0:T(8,128)S(1)}, f32[8,128]{1,0:T(8,128)}, u32[]{:S(2)}) copy-start(f32[8,128]{1,0:T(8,128)} %copy.71) | copy-start | bytes 12292
  69.1 22.5 %copy-start.5 = (f32[24]{0:T(128)S(1)}, f32[24]{0:T(128)}, u32[]{:S(2)}) copy-start(f32[24]{0:T(128)} %get-tuple-element.12) | copy-start | bytes 292
  69.2 22.3 %collective-permute-start.4 = (bf16[24,64,128]{2,1,0:T(8,128)(2,1)S(1)}, bf16[24,64,128]{2,1,0:T(8,128)(2,1)S(1)}, u32[]{:S(2)}, u32[]{:S(2)}) collective-permute-start(bf16[24,64,128]{2,1,0:T(8,128)(2,1)S(1)} %fusion.52), channel_id=1, source_target_pairs={{0,4},{1,5},{2,6},{3,7},{4,8},{5,9},{6,10},{7,11},{8,12},{9,13},{1... | collective-permute-start | bytes 1179656 | tf_op jit(solution)/shard_map/ppermute | solution.py:54
  91.9 6.0 %collective-permute-start.5 = (bf16[24,64,128]{2,1,0:T(8,128)(2,1)S(1)}, bf16[24,64,128]{2,1,0:T(8,128)(2,1)S(1)}, u32[]{:S(2)}, u32[]{:S(2)}) collective-permute-start(bf16[24,64,128]{2,1,0:T(8,128)(2,1)S(1)} %get-tuple-element.9), channel_id=1, source_target_pairs={{0,1},{1,0},{2,3},{3,2},{4,5},{5,4},{6,7},{7,6},{8,9},{9,8},{10,11... | collective-permute-start | bytes 1179656 | tf_op jit(solution)/shard_map/ppermute | solution.py:57
  97.9 0.7 copy-start.3
  97.9 0.7 copy-start.8
  98.6 1.4 %copy-start.2 = (f32[48,64]{1,0:T(8,128)S(1)}, f32[48,64]{1,0:T(8,128)}, u32[]{:S(2)}) copy-start(f32[48,64]{1,0:T(8,128)} %mul.329) | copy-start | bytes 36868

commit v6 on v5

--- a/solution.py
+++ b/solution.py
@@ -46,9 +46,8 @@
     one = [(i, i + 2) for i in range(size - 2)]
     two = [(i, i + 4) for i in range(size - 4)]
     first_hop = lax.ppermute(packed(chip_decay, chip_local), "ctx", one)
-    second_hop = lax.ppermute(first_hop, "ctx", one)
     decay_a, local_a = unpacked(first_hop, half, rest)
-    decay_b, local_b = unpacked(second_hop, half, rest)
+    decay_b, local_b = unpacked(lax.ppermute(first_hop.astype(jnp.bfloat16), "ctx", one).astype(jnp.float32), half, rest)
     decay_ab = decay_a * decay_b
     local_ab = decay_a[:, None, None] * local_b + local_a
     local_c = lax.ppermute(local_ab.astype(jnp.bfloat16), "ctx", two).astype(jnp.float32)

time: 103 us -> 95.5 us (0.927)
  the two profiles are of different devices: /device:TPU:173 before, /device:TPU:183 now
where the time goes in v6:
time: 95.5 us; the launch traced here: 94.2 us
  starting transfers between devices  28 us (29%)
  local copies, waits for them, and re-layouts  24.7 us (26%)
  waiting for transfers between devices  22.1 us (23%)
  other arithmetic  13.5 us (14%)
  matrix products  5.53 us (6%)
    ppermute x1, waiting for transfers between devices, chain_carry(): lax.ppermute(local_ab.astype(jnp.bfloat16), 'ctx', two).astype(jnp.float32)  13.7 us
    transpose x7, local copies, waits for them, and re-layouts, body(): step_size[:, part_start:part_start + group].T[:, None, :]  8.98 us
    ppermute x1, starting transfers between devices, chain_carry(): lax.ppermute(local_ab.astype(jnp.bfloat16), 'ctx', two).astype(jnp.float32)  7.44 us
    ppermute x1, starting transfers between devices, chain_carry(): first_hop = lax.ppermute(packed(chip_decay, chip_local), 'ctx', one)  5.2 us
    ppermute x1, waiting for transfers between devices, chain_carry(): lax.ppermute(first_hop.astype(jnp.bfloat16), 'ctx', one).astype(jnp.float32)  5.15 us
    ppermute x1, starting transfers between devices, chain_carry(): got_end = lax.ppermute(jnp.where(low, onward, carry_half), 'ctx', swap)  4.74 us
    ppermute x1, starting transfers between devices, shifted(): return lax.ppermute(block, axis, route)  4.56 us
    ppermute x1, starting transfers between devices, chain_carry(): lax.ppermute(first_hop.astype(jnp.bfloat16), 'ctx', one).astype(jnp.float32)  4.11 us
  transfers between devices with their start and end apart: 6, of which 5 were waited for; matrix products, arithmetic and copies ran while one was open for 30% of the time, Pallas kernels for 0%

profile of v6, /device:TPU:183, one launch (start us, length us, event | category | flops | bytes accessed | tf_op | source)
XLA Modules:
  0.0 94.2 jit_solution(18033203890125356507)
XLA Ops:
  0.0 0.9 slice.137
  0.9 4.6 %collective-permute-start = (bf16[3,3328]{1,0:T(4,128)(2,1)S(1)}, bf16[3,3328]{1,0:T(4,128)(2,1)S(1)}, u32[]{:S(2)}, u32[]{:S(2)}) collective-permute-start(bf16[3,3328]{1,0:T(4,128)(2,1)S(1)} %slice.137), channel_id=1, source_target_pairs={{0,1},{1,2},{2,3},{3,4},{4,5},{5,6},{6,7},{7,8},{8,9},{9,10},{10,1... | collective-permute-start | bytes 59912 | tf_op jit(solution)/shard_map/ppermute | solution.py:10
  5.5 0.8 reduce-window.15
  8.7 0.8 copy.59
  9.6 1.1 %slice_reduce_fusion.3 = (f32[3328]{0:T(1024)S(1)}, f32[3328]{0:T(1024)S(1)}, f32[3328]{0:T(1024)S(1)}, f32[3328]{0:T(1024)S(1)}) fusion(f32[4,3328]{1,0:T(4,128)} %param.12), kind=kLoop, calls=%fused_computation.112 | loop fusion | bytes 106496 | tf_op jit(solution)/shard_map/slice | solution.py:79
  13.1 2.6 %multiply_convert_fusion = bf16[128,3328]{1,0:T(8,128)(2,1)S(1)} fusion(bf16[128,3328]{1,0:T(8,128)(2,1)S(1)} %copy-done.1, bf16[3,3328]{1,0:T(4,128)(2,1)S(1)} %collective-permute-done, f32[3328]{0:T(1024)S(1)} %get-tuple-element.7, f32[3328]{0:T(1024)S(1)} %get-tuple-element.8, f32[3328]{0:T(1024)S(1)} %get-tuple-element.6, f32[3328]{0:T(1024)S(1)} %get-tuple-element.5, ...), kind=kLoop, calls=%fused_computation.2 | loop fusion | flops 12353536 | bytes 1790848 | tf_op jit(solution)/shard_map/convert_element_type | solution.py:84
  16.6 0.9 pad_maximum_fusion.1
  17.6 1.9 %collective-permute-start.1 = (f32[1544,128]{1,0:T(8,128)}, f32[1544,128]{1,0:T(8,128)}, u32[]{:S(2)}, u32[]{:S(2)}) collective-permute-start(f32[1544,128]{1,0:T(8,128)} %pad_maximum_fusion.1), channel_id=1, source_target_pairs={{0,1},{1,0},{2,3},{3,2},{4,5},{5,4},{6,7},{7,6},{8,9},{9,8},{10,11... | collective-permute-start | bytes 2371592 | tf_op jit(solution)/shard_map/ppermute | solution.py:36
  20.1 0.8 slice_bitcast_fusion
  24.1 1.2 %slice.198 = f32[1536,128]{1,0:T(8,128)S(1)} slice(f32[1544,128]{1,0:T(8,128)} %collective-permute-done.1), slice={[0:1536], [0:128]} | slice | bytes 1572864 | tf_op jit(solution)/shard_map/slice | solution.py:38
  25.5 0.9 pad_maximum_fusion.2
  26.4 5.2 %collective-permute-start.2 = (f32[1544,128]{1,0:T(8,128)}, f32[1544,128]{1,0:T(8,128)}, u32[]{:S(2)}, u32[]{:S(2)}) collective-permute-start(f32[1544,128]{1,0:T(8,128)} %pad_maximum_fusion.2), channel_id=1, source_target_pairs={{0,2},{1,3},{2,4},{3,5},{4,6},{5,7},{6,8},{7,9},{8,10},{9,11},{10,... | collective-permute-start | bytes 2371592 | tf_op jit(solution)/shard_map/ppermute | solution.py:48
  31.7 1.4 %mul.329 = f32[48,64]{1,0:T(8,128)} reshape(f32[3072]{0:T(1024)} %param.17) | data formatting | bytes 24576 | tf_op jit(solution)/shard_map/mul | solution.py:126
  33.1 1.5 %copy.79 = f32[128,48]{0,1:T(8,128)} copy(f32[128,48]{1,0:T(8,128)} %get-tuple-element.18) | data formatting | bytes 49152 | tf_op jit(solution)/shard_map/mul | solution.py:120
  34.6 1.5 %copy.77 = f32[8,128]{1,0:T(8,128)} copy(f32[8,128]{0,1:T(8,128)} %get-tuple-element.26) | data formatting | bytes 8192 | tf_op jit(solution)/shard_map/transpose | solution.py:106
  36.1 1.5 %copy.74 = f32[8,128]{1,0:T(8,128)} copy(f32[8,128]{0,1:T(8,128)} %get-tuple-element.27) | data formatting | bytes 8192 | tf_op jit(solution)/shard_map/transpose | solution.py:106
  37.6 1.5 %copy.71 = f32[8,128]{1,0:T(8,128)} copy(f32[8,128]{0,1:T(8,128)} %get-tuple-element.28) | data formatting | bytes 8192 | tf_op jit(solution)/shard_map/transpose | solution.py:106
  39.1 1.5 %copy.68 = f32[8,128]{1,0:T(8,128)} copy(f32[8,128]{0,1:T(8,128)} %get-tuple-element.29) | data formatting | bytes 8192 | tf_op jit(solution)/shard_map/transpose | solution.py:106
  40.6 1.5 %copy.65 = f32[8,128]{1,0:T(8,128)} copy(f32[8,128]{0,1:T(8,128)} %get-tuple-element.30) | data formatting | bytes 8192 | tf_op jit(solution)/shard_map/transpose | solution.py:106
  42.8 0.9 copy.75
  44.0 0.9 fusion.57
  44.9 1.1 %fusion.7 = f32[128,48,64]{0,2,1:T(8,128)S(1)} fusion(bf16[128,48,64]{0,2,1:T(8,128)(2,1)S(1)} %bitcast.99, f32[8,128]{1,0:T(8,128)} %copy.62, f32[8,128]{1,0:T(8,128)S(1)} %copy.60, f32[128,128]{1,0:T(8,128)S(1)} %fusion.57, pred[128,128]{1,0:T(8,128)(4,1)S(1)} %fusion.53), kind=kOutput, calls=%fused_computation.20 | convolution fusion | flops 17563648 | bytes 1142784 | tf_op jit(solution)/shard_map/hts,shp->thp/dot_general | solution.py:109
  46.4 2.3 %collective-permute-done.2 = f32[1544,128]{1,0:T(8,128)} collective-permute-done((f32[1544,128]{1,0:T(8,128)}, f32[1544,128]{1,0:T(8,128)}, u32[]{:S(2)}, u32[]{:S(2)}) %collective-permute-start.2) | collective-permute-done | bytes 790560 | tf_op jit(solution)/shard_map/ppermute | solution.py:48
  48.7 1.2 %convert_element_type.94 = bf16[1544,128]{1,0:T(8,128)(2,1)S(1)} convert(f32[1544,128]{1,0:T(8,128)} %collective-permute-done.2) | non-fusion elementwise | flops 197632 | bytes 1185792 | tf_op jit(solution)/shard_map/convert_element_type | solution.py:50
  49.9 4.1 %collective-permute-start.3 = (bf16[1544,128]{1,0:T(8,128)(2,1)S(1)}, bf16[1544,128]{1,0:T(8,128)(2,1)S(1)}, u32[]{:S(2)}, u32[]{:S(2)}) collective-permute-start(bf16[1544,128]{1,0:T(8,128)(2,1)S(1)} %convert_element_type.94), channel_id=1, source_target_pairs={{0,2},{1,3},{2,4},{3,5},{4,6},{5,7},{6,8},{7,9},{8,10},{9,11},{10,... | collective-permute-start | bytes 1185800 | tf_op jit(solution)/shard_map/ppermute | solution.py:50
  54.4 1.2 %slice.202 = f32[1536,128]{1,0:T(8,128)S(1)} slice(f32[1544,128]{1,0:T(8,128)} %collective-permute-done.2), slice={[0:1536], [0:128]} | slice | bytes 1572864 | tf_op jit(solution)/shard_map/slice | solution.py:22
  56.3 5.2 %collective-permute-done.3 = bf16[1544,128]{1,0:T(8,128)(2,1)S(1)} collective-permute-done((bf16[1544,128]{1,0:T(8,128)(2,1)S(1)}, bf16[1544,128]{1,0:T(8,128)(2,1)S(1)}, u32[]{:S(2)}, u32[]{:S(2)}) %collective-permute-start.3) | collective-permute-done | bytes 395296 | tf_op jit(solution)/shard_map/ppermute | solution.py:50
  61.7 7.4 %collective-permute-start.4 = (bf16[24,64,128]{2,1,0:T(8,128)(2,1)S(1)}, bf16[24,64,128]{2,1,0:T(8,128)(2,1)S(1)}, u32[]{:S(2)}, u32[]{:S(2)}) collective-permute-start(bf16[24,64,128]{2,1,0:T(8,128)(2,1)S(1)} %fusion.52), channel_id=1, source_target_pairs={{0,4},{1,5},{2,6},{3,7},{4,8},{5,9},{6,10},{7,11},{8,12},{9,13},{1... | collective-permute-start | bytes 1179656 | tf_op jit(solution)/shard_map/ppermute | solution.py:53
  70.2 13.7 %collective-permute-done.4 = bf16[24,64,128]{2,1,0:T(8,128)(2,1)S(1)} collective-permute-done((bf16[24,64,128]{2,1,0:T(8,128)(2,1)S(1)}, bf16[24,64,128]{2,1,0:T(8,128)(2,1)S(1)}, u32[]{:S(2)}, u32[]{:S(2)}) %collective-permute-start.4) | collective-permute-done | bytes 393248 | tf_op jit(solution)/shard_map/ppermute | solution.py:53
  84.3 4.7 %collective-permute-start.5 = (bf16[24,64,128]{2,1,0:T(8,128)(2,1)S(1)}, bf16[24,64,128]{2,1,0:T(8,128)(2,1)S(1)}, u32[]{:S(2)}, u32[]{:S(2)}) collective-permute-start(bf16[24,64,128]{2,1,0:T(8,128)(2,1)S(1)} %get-tuple-element.9), channel_id=1, source_target_pairs={{0,1},{1,0},{2,3},{3,2},{4,5},{5,4},{6,7},{7,6},{8,9},{9,8},{10,11... | collective-permute-start | bytes 1179656 | tf_op jit(solution)/shard_map/ppermute | solution.py:56
  91.2 1.4 %multiply_reduce_fusion = (f32[128,48]{0,1:T(8,128)S(1)}, f32[128,48,64]{0,2,1:T(8,128)S(1)}) fusion(bf16[128,48,64]{0,2,1:T(8,128)(2,1)S(1)} %bitcast.105, f32[48]{0:T(128)S(1)} %copy-done.14, f32[128,48,64]{0,2,1:T(8,128)S(1)} %fusion.2, bf16[24,64,128]{2,1,0:T(8,128)(2,1)S(1)} %get-tuple-element.17, bf16[24,64,128]{2,1,0:T(8,128)(2,1)S(1)} %get-tuple-element.16, ...), kind=kOutput, calls=%fused_computation.6 | convolution fusion | flops 104982528 | bytes 4800704 | tf_op jit(solution)/shard_map/hpn,tn->thp/dot_general | solution.py:122
  93.0 1.2 %copy.81 = bf16[128,3072]{1,0:T(8,128)(2,1)} copy(bf16[128,3072]{0,1:T(8,128)(2,1)S(1)} %bitcast.111) | data formatting | bytes 1572864 | tf_op jit(solution)/shard_map/reshape | solution.py:130
  (82 shorter events, 16.3 us)
Async XLA Ops:
  0.0 13.1 %copy-start.1 = (bf16[128,3328]{1,0:T(8,128)(2,1)S(1)}, bf16[128,3328]{1,0:T(8,128)(2,1)}, u32[]{:S(2)}) copy-start(bf16[128,3328]{1,0:T(8,128)(2,1)} %param.9) | copy-start | bytes 2555908
  0.9 12.2 %collective-permute-start = (bf16[3,3328]{1,0:T(4,128)(2,1)S(1)}, bf16[3,3328]{1,0:T(4,128)(2,1)S(1)}, u32[]{:S(2)}, u32[]{:S(2)}) collective-permute-start(bf16[3,3328]{1,0:T(4,128)(2,1)S(1)} %slice.137), channel_id=1, source_target_pairs={{0,1},{1,2},{2,3},{3,4},{4,5},{5,6},{6,7},{7,8},{8,9},{9,10},{10,1... | collective-permute-start | bytes 59912 | tf_op jit(solution)/shard_map/ppermute | solution.py:10
  15.7 5.3 %copy-start = (bf16[128,3328]{1,0:T(8,128)(2,1)}, bf16[128,3328]{1,0:T(8,128)(2,1)S(1)}, u32[]{:S(2)}) copy-start(bf16[128,3328]{1,0:T(8,128)(2,1)S(1)} %multiply_convert_fusion) | copy-start | bytes 2555908
  17.6 4.5 %collective-permute-start.1 = (f32[1544,128]{1,0:T(8,128)}, f32[1544,128]{1,0:T(8,128)}, u32[]{:S(2)}, u32[]{:S(2)}) collective-permute-start(f32[1544,128]{1,0:T(8,128)} %pad_maximum_fusion.1), channel_id=1, source_target_pairs={{0,1},{1,0},{2,3},{3,2},{4,5},{5,4},{6,7},{7,6},{8,9},{9,8},{10,11... | collective-permute-start | bytes 2371592 | tf_op jit(solution)/shard_map/ppermute | solution.py:36
  25.2 6.4 %copy-start.13 = (s32[128]{0:T(128)S(1)}, s32[128]{0:T(128)}, u32[]{:S(2)}) copy-start(s32[128]{0:T(128)} %slice.136) | copy-start | bytes 1540
  25.4 16.7 %copy-start.4 = (f32[8,128]{0,1:T(8,128)S(1)}, f32[8,128]{0,1:T(8,128)}, u32[]{:S(2)}) copy-start(f32[8,128]{0,1:T(8,128)} %get-tuple-element.31) | copy-start | bytes 12292
  25.5 18.2 %copy-start.3 = (f32[8,128]{0,1:T(8,128)S(1)}, f32[8,128]{0,1:T(8,128)}, u32[]{:S(2)}) copy-start(f32[8,128]{0,1:T(8,128)} %get-tuple-element.21) | copy-start | bytes 12292
  25.5 18.3 %copy-start.2 = (f32[8,128]{0,1:T(8,128)S(1)}, f32[8,128]{0,1:T(8,128)}, u32[]{:S(2)}) copy-start(f32[8,128]{0,1:T(8,128)} %get-tuple-element.22) | copy-start | bytes 12292
  26.4 22.3 %collective-permute-start.2 = (f32[1544,128]{1,0:T(8,128)}, f32[1544,128]{1,0:T(8,128)}, u32[]{:S(2)}, u32[]{:S(2)}) collective-permute-start(f32[1544,128]{1,0:T(8,128)} %pad_maximum_fusion.2), channel_id=1, source_target_pairs={{0,2},{1,3},{2,4},{3,5},{4,6},{5,7},{6,8},{7,9},{8,10},{9,11},{10,... | collective-permute-start | bytes 2371592 | tf_op jit(solution)/shard_map/ppermute | solution.py:48
  42.8 3.2 %copy-start.12 = (f32[8,128]{1,0:T(8,128)S(1)}, f32[8,128]{1,0:T(8,128)}, u32[]{:S(2)}) copy-start(f32[8,128]{1,0:T(8,128)} %copy.65) | copy-start | bytes 12292
  46.0 8.0 %copy-start.11 = (f32[8,128]{1,0:T(8,128)S(1)}, f32[8,128]{1,0:T(8,128)}, u32[]{:S(2)}) copy-start(f32[8,128]{1,0:T(8,128)} %copy.68) | copy-start | bytes 12292
  49.9 11.5 %collective-permute-start.3 = (bf16[1544,128]{1,0:T(8,128)(2,1)S(1)}, bf16[1544,128]{1,0:T(8,128)(2,1)S(1)}, u32[]{:S(2)}, u32[]{:S(2)}) collective-permute-start(bf16[1544,128]{1,0:T(8,128)(2,1)S(1)} %convert_element_type.94), channel_id=1, source_target_pairs={{0,2},{1,3},{2,4},{3,5},{4,6},{5,7},{6,8},{7,9},{8,10},{9,11},{10,... | collective-permute-start | bytes 1185800 | tf_op jit(solution)/shard_map/ppermute | solution.py:50
  56.3 12.8 %copy-start.10 = (f32[8,128]{1,0:T(8,128)S(1)}, f32[8,128]{1,0:T(8,128)}, u32[]{:S(2)}) copy-start(f32[8,128]{1,0:T(8,128)} %copy.71) | copy-start | bytes 12292
  61.6 22.3 %copy-start.7 = (f32[24]{0:T(128)S(1)}, f32[24]{0:T(128)}, u32[]{:S(2)}) copy-start(f32[24]{0:T(128)} %get-tuple-element.12) | copy-start | bytes 292
  61.7 22.3 %collective-permute-start.4 = (bf16[24,64,128]{2,1,0:T(8,128)(2,1)S(1)}, bf16[24,64,128]{2,1,0:T(8,128)(2,1)S(1)}, u32[]{:S(2)}, u32[]{:S(2)}) collective-permute-start(bf16[24,64,128]{2,1,0:T(8,128)(2,1)S(1)} %fusion.52), channel_id=1, source_target_pairs={{0,4},{1,5},{2,6},{3,7},{4,8},{5,9},{6,10},{7,11},{8,12},{9,13},{1... | collective-permute-start | bytes 1179656 | tf_op jit(solution)/shard_map/ppermute | solution.py:53
  84.0 5.1 %copy-start.9 = (f32[8,128]{1,0:T(8,128)S(1)}, f32[8,128]{1,0:T(8,128)}, u32[]{:S(2)}) copy-start(f32[8,128]{1,0:T(8,128)} %copy.74) | copy-start | bytes 12292
  84.3 5.1 %copy-start.8 = (f32[8,128]{1,0:T(8,128)S(1)}, f32[8,128]{1,0:T(8,128)}, u32[]{:S(2)}) copy-start(f32[8,128]{1,0:T(8,128)} %copy.77) | copy-start | bytes 12292
  84.3 6.1 %collective-permute-start.5 = (bf16[24,64,128]{2,1,0:T(8,128)(2,1)S(1)}, bf16[24,64,128]{2,1,0:T(8,128)(2,1)S(1)}, u32[]{:S(2)}, u32[]{:S(2)}) collective-permute-start(bf16[24,64,128]{2,1,0:T(8,128)(2,1)S(1)} %get-tuple-element.9), channel_id=1, source_target_pairs={{0,1},{1,0},{2,3},{3,2},{4,5},{5,4},{6,7},{7,6},{8,9},{9,8},{10,11... | collective-permute-start | bytes 1179656 | tf_op jit(solution)/shard_map/ppermute | solution.py:56
  90.4 0.7 copy-start.6
  90.4 0.7 copy-start.14
  91.2 1.4 %copy-start.5 = (f32[48,64]{1,0:T(8,128)S(1)}, f32[48,64]{1,0:T(8,128)}, u32[]{:S(2)}) copy-start(f32[48,64]{1,0:T(8,128)} %mul.329) | copy-start | bytes 36868

commit v7 on v6

--- a/solution.py
+++ b/solution.py
@@ -68,18 +68,20 @@
     taps = conv_weight.shape[0]
     device = lax.axis_index("ctx")
     first = device * rows
-    ends = jnp.cumsum(lengths)
-    places = first - (taps - 1) + jnp.arange(rows + taps - 1, dtype=jnp.int32)
+    docs = lengths.shape[0]
+    order = jnp.arange(docs, dtype=jnp.int32)
+    ends = jnp.sum(jnp.where(order[None, :] <= order[:, None], lengths[None, :], 0), axis=1)
+    halo = 16
+    places = first - halo + jnp.arange(rows + halo, dtype=jnp.int32)
     counted = jnp.sum((places[:, None] >= ends[None, :]).astype(jnp.int32), axis=1)
     seg_wide = jnp.where(places < 0, -1, counted)
-    seg = seg_wide[taps - 1 :]
-    start = seg != seg_wide[taps - 2 : -1]
-    rim = shifted(xbc[rows - (taps - 1) :], "ctx", 1)
+    seg = seg_wide[halo:]
+    rim = shifted(xbc[rows - halo :], "ctx", 1)
     widened = jnp.concatenate([rim, xbc], axis=0)
     total = conv_bias[None, :] + conv_weight[taps - 1][None, :] * xbc.astype(jnp.float32)
     for lag in range(1, taps):
-        moved = widened[taps - 1 - lag : taps - 1 - lag + rows].astype(jnp.float32)
-        same = seg_wide[taps - 1 - lag : taps - 1 - lag + rows] == seg
+        moved = widened[halo - lag : halo - lag + rows].astype(jnp.float32)
+        same = seg_wide[halo - lag : halo - lag + rows] == seg
         total = total + conv_weight[taps - 1 - lag][None, :] * jnp.where(same[:, None], moved, 0.0)
     act = jax.nn.silu(total).astype(jnp.bfloat16)
     xs = act[:, :inner_width].reshape(rows, heads, head_dim)
@@ -87,7 +89,7 @@
     cs = act[:, inner_width + state_dim :]
     step_size = jax.nn.softplus(dt_raw + dt_bias[None, :])
     cum = jnp.cumsum(-step_size * decay_rate[None, :], axis=0)
-    alive = (jnp.cumsum(start.astype(jnp.int32)) == 0).astype(jnp.float32)
+    alive = (seg == seg_wide[halo - 1]).astype(jnp.float32)
     same_end = (seg == seg[-1]).astype(jnp.float32)
     factor = jnp.exp(cum[-1][None, :] - cum) * same_end[:, None] * step_size
     scaled = (factor[:, :, None] * xs.astype(jnp.float32)).astype(jnp.bfloat16)

time: 95.5 us -> 94.9 us (level)
    another operation x3 -> x1, other arithmetic: 1.3 us -> 0.29 us
    convert_element_type x1, other arithmetic: 2.6 us -> 1.61 us  [body(): act = jax.nn.silu(total).astype(jnp.bfloat16)]
  transfers between devices with their start and end apart: 6 -> 6, of which waited for: 5 -> 5; matrix products, arithmetic and copies ran while one was open for 30% -> 31% of each run, Pallas kernels for 0% -> 0%
where the time goes in v7:
time: 94.9 us; the launch traced here: 93.7 us
  starting transfers between devices  27.9 us (29%)
  local copies, waits for them, and re-layouts  24.9 us (26%)
  waiting for transfers between devices  22.1 us (23%)
  other arithmetic  12.8 us (13%)
  matrix products  5.53 us (6%)
    ppermute x1, waiting for transfers between devices, chain_carry(): lax.ppermute(local_ab.astype(jnp.bfloat16), 'ctx', two).astype(jnp.float32)  13.7 us
    transpose x7, local copies, waits for them, and re-layouts, body(): step_size[:, part_start:part_start + group].T[:, None, :]  8.99 us
    ppermute x1, starting transfers between devices, chain_carry(): lax.ppermute(local_ab.astype(jnp.bfloat16), 'ctx', two).astype(jnp.float32)  7.44 us
    ppermute x1, starting transfers between devices, chain_carry(): first_hop = lax.ppermute(packed(chip_decay, chip_local), 'ctx', one)  5.2 us
    ppermute x1, waiting for transfers between devices, chain_carry(): lax.ppermute(first_hop.astype(jnp.bfloat16), 'ctx', one).astype(jnp.float32)  5.15 us
    ppermute x1, starting transfers between devices, chain_carry(): got_end = lax.ppermute(jnp.where(low, onward, carry_half), 'ctx', swap)  4.73 us
    ppermute x1, starting transfers between devices, shifted(): return lax.ppermute(block, axis, route)  4.55 us
    ppermute x1, starting transfers between devices, chain_carry(): lax.ppermute(first_hop.astype(jnp.bfloat16), 'ctx', one).astype(jnp.float32)  4.11 us
  transfers between devices with their start and end apart: 6, of which 5 were waited for; matrix products, arithmetic and copies ran while one was open for 31% of the time, Pallas kernels for 0%

profile of v7, /device:TPU:183, one launch (start us, length us, event | category | flops | bytes accessed | tf_op | source)
XLA Modules:
  0.0 93.7 jit_solution(6983764470399022365)
XLA Ops:
  0.0 1.0 %slice.138 = bf16[16,3328]{1,0:T(8,128)(2,1)S(1)} slice(bf16[128,3328]{1,0:T(8,128)(2,1)} %param.9), slice={[112:128], [0:3328]} | slice | bytes 212992 | tf_op jit(solution)/shard_map/slice | solution.py:79
  1.0 4.5 %collective-permute-start = (bf16[16,3328]{1,0:T(8,128)(2,1)S(1)}, bf16[16,3328]{1,0:T(8,128)(2,1)S(1)}, u32[]{:S(2)}, u32[]{:S(2)}) collective-permute-start(bf16[16,3328]{1,0:T(8,128)(2,1)S(1)} %slice.138), channel_id=1, source_target_pairs={{0,1},{1,2},{2,3},{3,4},{4,5},{5,6},{6,7},{7,8},{8,9},{9,10},{10,1... | collective-permute-start | bytes 319496 | tf_op jit(solution)/shard_map/ppermute | solution.py:10
  7.0 1.4 %compare_convert_fusion = (f32[128]{0:T(128)S(1)}, f32[128]{0:T(128)S(1)}, pred[128]{0:T(512)(128)(4,1)S(1)}, pred[128]{0:T(512)(128)(4,1)S(1)}, pred[128]{0:T(512)(128)(4,1)S(1)}) fusion(s32[]{:T(128)} %bitcast.22, s32[144]{0:T(256)S(1)} %compare_select_fusion.1, s32[]{:T(128)} %bitcast.19), kind=kLoop, calls=%fused_computation.115 | loop fusion | flops 896 | bytes 3464 | tf_op jit(solution)/shard_map/convert_element_type | solution.py:93
  9.1 0.8 copy.34
  9.9 1.1 %slice_reduce_fusion.3 = (f32[3328]{0:T(1024)S(1)}, f32[3328]{0:T(1024)S(1)}, f32[3328]{0:T(1024)S(1)}, f32[3328]{0:T(1024)S(1)}) fusion(f32[4,3328]{1,0:T(4,128)} %param.12), kind=kLoop, calls=%fused_computation.108 | loop fusion | bytes 106496 | tf_op jit(solution)/shard_map/slice | solution.py:81
  13.5 1.6 %multiply_convert_fusion = bf16[128,3328]{1,0:T(8,128)(2,1)S(1)} fusion(bf16[128,3328]{1,0:T(8,128)(2,1)S(1)} %copy-done, bf16[144,3328]{1,0:T(8,128)(2,1)S(1)} %constant_dynamic-update-slice_fusion, f32[3328]{0:T(1024)S(1)} %get-tuple-element.7, f32[3328]{0:T(1024)S(1)} %get-tuple-element.8, f32[3328]{0:T(1024)S(1)} %get-tuple-element.6, ...), kind=kLoop, calls=%fused_computation.2 | loop fusion | flops 8519680 | bytes 4326784 | tf_op jit(solution)/shard_map/convert_element_type | solution.py:86
  16.0 1.0 %pad_maximum_fusion = f32[1544,128]{1,0:T(8,128)} fusion(f32[8,128]{1,0:T(8,128)S(1)} %pad_bitcast_fusion.1, f32[1536,128]{1,0:T(8,128)S(1)} %bitcast.107), kind=kLoop, calls=%fused_computation.19 | loop fusion | flops 197632 | bytes 1581056 | tf_op jit(solution)/shard_map/concatenate | solution.py:17
  17.0 1.9 %collective-permute-start.1 = (f32[1544,128]{1,0:T(8,128)}, f32[1544,128]{1,0:T(8,128)}, u32[]{:S(2)}, u32[]{:S(2)}) collective-permute-start(f32[1544,128]{1,0:T(8,128)} %pad_maximum_fusion), channel_id=1, source_target_pairs={{0,1},{1,0},{2,3},{3,2},{4,5},{5,4},{6,7},{7,6},{8,9},{9,8},{10,11... | collective-permute-start | bytes 2371592 | tf_op jit(solution)/shard_map/ppermute | solution.py:36
  19.6 0.8 slice_bitcast_fusion
  23.5 1.2 %slice.198 = f32[1536,128]{1,0:T(8,128)S(1)} slice(f32[1544,128]{1,0:T(8,128)} %collective-permute-done.1), slice={[0:1536], [0:128]} | slice | bytes 1572864 | tf_op jit(solution)/shard_map/slice | solution.py:38
  24.9 1.0 %pad_maximum_fusion.1 = f32[1544,128]{1,0:T(8,128)} fusion(f32[8,128]{1,0:T(8,128)S(1)} %pad_bitcast_fusion, f32[1536,128]{1,0:T(8,128)S(1)} %bitcast.109), kind=kLoop, calls=%fused_computation.20 | loop fusion | flops 197632 | bytes 1581056 | tf_op jit(solution)/shard_map/concatenate | solution.py:17
  25.9 5.2 %collective-permute-start.2 = (f32[1544,128]{1,0:T(8,128)}, f32[1544,128]{1,0:T(8,128)}, u32[]{:S(2)}, u32[]{:S(2)}) collective-permute-start(f32[1544,128]{1,0:T(8,128)} %pad_maximum_fusion.1), channel_id=1, source_target_pairs={{0,2},{1,3},{2,4},{3,5},{4,6},{5,7},{6,8},{7,9},{8,10},{9,11},{10,... | collective-permute-start | bytes 2371592 | tf_op jit(solution)/shard_map/ppermute | solution.py:48
  31.2 1.4 %mul.329 = f32[48,64]{1,0:T(8,128)} reshape(f32[3072]{0:T(1024)} %param.17) | data formatting | bytes 24576 | tf_op jit(solution)/shard_map/mul | solution.py:128
  32.6 1.5 %copy.53 = f32[128,48]{0,1:T(8,128)} copy(f32[128,48]{1,0:T(8,128)} %get-tuple-element.18) | data formatting | bytes 49152 | tf_op jit(solution)/shard_map/mul | solution.py:122
  34.1 1.5 %copy.52 = f32[8,128]{1,0:T(8,128)} copy(f32[8,128]{0,1:T(8,128)} %get-tuple-element.26) | data formatting | bytes 8192 | tf_op jit(solution)/shard_map/transpose | solution.py:108
  35.6 1.5 %copy.49 = f32[8,128]{1,0:T(8,128)} copy(f32[8,128]{0,1:T(8,128)} %get-tuple-element.27) | data formatting | bytes 8192 | tf_op jit(solution)/shard_map/transpose | solution.py:108
  37.1 1.5 %copy.46 = f32[8,128]{1,0:T(8,128)} copy(f32[8,128]{0,1:T(8,128)} %get-tuple-element.28) | data formatting | bytes 8192 | tf_op jit(solution)/shard_map/transpose | solution.py:108
  38.6 1.5 %copy.43 = f32[8,128]{1,0:T(8,128)} copy(f32[8,128]{0,1:T(8,128)} %get-tuple-element.29) | data formatting | bytes 8192 | tf_op jit(solution)/shard_map/transpose | solution.py:108
  40.1 1.5 %copy.40 = f32[8,128]{1,0:T(8,128)} copy(f32[8,128]{0,1:T(8,128)} %get-tuple-element.30) | data formatting | bytes 8192 | tf_op jit(solution)/shard_map/transpose | solution.py:108
  42.2 0.9 copy.50
  43.5 0.9 fusion.55
  44.4 1.1 %fusion.7 = f32[128,48,64]{0,2,1:T(8,128)S(1)} fusion(bf16[128,48,64]{0,2,1:T(8,128)(2,1)S(1)} %bitcast.96, f32[8,128]{1,0:T(8,128)} %copy.37, f32[8,128]{1,0:T(8,128)S(1)} %copy.35, f32[128,128]{1,0:T(8,128)S(1)} %fusion.55, pred[128,128]{1,0:T(8,128)(4,1)S(1)} %fusion.51), kind=kOutput, calls=%fused_computation.18 | convolution fusion | flops 17563648 | bytes 1142784 | tf_op jit(solution)/shard_map/hts,shp->thp/dot_general | solution.py:111
  45.9 2.3 %collective-permute-done.2 = f32[1544,128]{1,0:T(8,128)} collective-permute-done((f32[1544,128]{1,0:T(8,128)}, f32[1544,128]{1,0:T(8,128)}, u32[]{:S(2)}, u32[]{:S(2)}) %collective-permute-start.2) | collective-permute-done | bytes 790560 | tf_op jit(solution)/shard_map/ppermute | solution.py:48
  48.2 1.2 %convert_element_type.85 = bf16[1544,128]{1,0:T(8,128)(2,1)S(1)} convert(f32[1544,128]{1,0:T(8,128)} %collective-permute-done.2) | non-fusion elementwise | flops 197632 | bytes 1185792 | tf_op jit(solution)/shard_map/convert_element_type | solution.py:50
  49.4 4.1 %collective-permute-start.3 = (bf16[1544,128]{1,0:T(8,128)(2,1)S(1)}, bf16[1544,128]{1,0:T(8,128)(2,1)S(1)}, u32[]{:S(2)}, u32[]{:S(2)}) collective-permute-start(bf16[1544,128]{1,0:T(8,128)(2,1)S(1)} %convert_element_type.85), channel_id=1, source_target_pairs={{0,2},{1,3},{2,4},{3,5},{4,6},{5,7},{6,8},{7,9},{8,10},{9,11},{10,... | collective-permute-start | bytes 1185800 | tf_op jit(solution)/shard_map/ppermute | solution.py:50
  53.9 1.2 %slice.202 = f32[1536,128]{1,0:T(8,128)S(1)} slice(f32[1544,128]{1,0:T(8,128)} %collective-permute-done.2), slice={[0:1536], [0:128]} | slice | bytes 1572864 | tf_op jit(solution)/shard_map/slice | solution.py:22
  55.7 5.2 %collective-permute-done.3 = bf16[1544,128]{1,0:T(8,128)(2,1)S(1)} collective-permute-done((bf16[1544,128]{1,0:T(8,128)(2,1)S(1)}, bf16[1544,128]{1,0:T(8,128)(2,1)S(1)}, u32[]{:S(2)}, u32[]{:S(2)}) %collective-permute-start.3) | collective-permute-done | bytes 395296 | tf_op jit(solution)/shard_map/ppermute | solution.py:50
  61.1 7.4 %collective-permute-start.4 = (bf16[24,64,128]{2,1,0:T(8,128)(2,1)S(1)}, bf16[24,64,128]{2,1,0:T(8,128)(2,1)S(1)}, u32[]{:S(2)}, u32[]{:S(2)}) collective-permute-start(bf16[24,64,128]{2,1,0:T(8,128)(2,1)S(1)} %fusion.50), channel_id=1, source_target_pairs={{0,4},{1,5},{2,6},{3,7},{4,8},{5,9},{6,10},{7,11},{8,12},{9,13},{1... | collective-permute-start | bytes 1179656 | tf_op jit(solution)/shard_map/ppermute | solution.py:53
  69.7 13.7 %collective-permute-done.4 = bf16[24,64,128]{2,1,0:T(8,128)(2,1)S(1)} collective-permute-done((bf16[24,64,128]{2,1,0:T(8,128)(2,1)S(1)}, bf16[24,64,128]{2,1,0:T(8,128)(2,1)S(1)}, u32[]{:S(2)}, u32[]{:S(2)}) %collective-permute-start.4) | collective-permute-done | bytes 393248 | tf_op jit(solution)/shard_map/ppermute | solution.py:53
  83.8 4.7 %collective-permute-start.5 = (bf16[24,64,128]{2,1,0:T(8,128)(2,1)S(1)}, bf16[24,64,128]{2,1,0:T(8,128)(2,1)S(1)}, u32[]{:S(2)}, u32[]{:S(2)}) collective-permute-start(bf16[24,64,128]{2,1,0:T(8,128)(2,1)S(1)} %get-tuple-element.9), channel_id=1, source_target_pairs={{0,1},{1,0},{2,3},{3,2},{4,5},{5,4},{6,7},{7,6},{8,9},{9,8},{10,11... | collective-permute-start | bytes 1179656 | tf_op jit(solution)/shard_map/ppermute | solution.py:56
  90.6 1.4 %multiply_reduce_fusion = (f32[128,48]{0,1:T(8,128)S(1)}, f32[128,48,64]{0,2,1:T(8,128)S(1)}) fusion(bf16[128,48,64]{0,2,1:T(8,128)(2,1)S(1)} %bitcast.102, f32[48]{0:T(128)S(1)} %copy-done.15, f32[128,48,64]{0,2,1:T(8,128)S(1)} %fusion.2, bf16[24,64,128]{2,1,0:T(8,128)(2,1)S(1)} %get-tuple-element.17, bf16[24,64,128]{2,1,0:T(8,128)(2,1)S(1)} %get-tuple-element.16, ...), kind=kOutput, calls=%fused_computation.6 | convolution fusion | flops 104982528 | bytes 4800704 | tf_op jit(solution)/shard_map/hpn,tn->thp/dot_general | solution.py:124
  92.5 1.2 %copy.55 = bf16[128,3072]{1,0:T(8,128)(2,1)} copy(bf16[128,3072]{0,1:T(8,128)(2,1)S(1)} %bitcast.108) | data formatting | bytes 1572864 | tf_op jit(solution)/shard_map/reshape | solution.py:132
  (82 shorter events, 16.1 us)
Async XLA Ops:
  0.0 13.4 %copy-start = (bf16[128,3328]{1,0:T(8,128)(2,1)S(1)}, bf16[128,3328]{1,0:T(8,128)(2,1)}, u32[]{:S(2)}) copy-start(bf16[128,3328]{1,0:T(8,128)(2,1)} %param.9) | copy-start | bytes 2555908
  0.0 13.5 %copy-start.7 = (f32[3328]{0:T(1024)S(1)}, f32[3328]{0:T(1024)}, u32[]{:S(2)}) copy-start(f32[3328]{0:T(1024)} %param.13) | copy-start | bytes 39940
  1.0 12.4 %collective-permute-start = (bf16[16,3328]{1,0:T(8,128)(2,1)S(1)}, bf16[16,3328]{1,0:T(8,128)(2,1)S(1)}, u32[]{:S(2)}, u32[]{:S(2)}) collective-permute-start(bf16[16,3328]{1,0:T(8,128)(2,1)S(1)} %slice.138), channel_id=1, source_target_pairs={{0,1},{1,2},{2,3},{3,4},{4,5},{5,6},{6,7},{7,8},{8,9},{9,10},{10,1... | collective-permute-start | bytes 319496 | tf_op jit(solution)/shard_map/ppermute | solution.py:10
  15.1 5.3 %copy-start.1 = (bf16[128,3328]{1,0:T(8,128)(2,1)}, bf16[128,3328]{1,0:T(8,128)(2,1)S(1)}, u32[]{:S(2)}) copy-start(bf16[128,3328]{1,0:T(8,128)(2,1)S(1)} %multiply_convert_fusion) | copy-start | bytes 2555908
  17.0 4.5 %collective-permute-start.1 = (f32[1544,128]{1,0:T(8,128)}, f32[1544,128]{1,0:T(8,128)}, u32[]{:S(2)}, u32[]{:S(2)}) collective-permute-start(f32[1544,128]{1,0:T(8,128)} %pad_maximum_fusion), channel_id=1, source_target_pairs={{0,1},{1,0},{2,3},{3,2},{4,5},{5,4},{6,7},{7,6},{8,9},{9,8},{10,11... | collective-permute-start | bytes 2371592 | tf_op jit(solution)/shard_map/ppermute | solution.py:36
  24.7 6.4 %copy-start.14 = (s32[128]{0:T(128)S(1)}, s32[128]{0:T(128)}, u32[]{:S(2)}) copy-start(s32[128]{0:T(128)} %slice.137) | copy-start | bytes 1540
  24.9 16.7 %copy-start.4 = (f32[8,128]{0,1:T(8,128)S(1)}, f32[8,128]{0,1:T(8,128)}, u32[]{:S(2)}) copy-start(f32[8,128]{0,1:T(8,128)} %get-tuple-element.31) | copy-start | bytes 12292
  24.9 18.2 %copy-start.3 = (f32[8,128]{0,1:T(8,128)S(1)}, f32[8,128]{0,1:T(8,128)}, u32[]{:S(2)}) copy-start(f32[8,128]{0,1:T(8,128)} %get-tuple-element.21) | copy-start | bytes 12292
  24.9 18.3 %copy-start.2 = (f32[8,128]{0,1:T(8,128)S(1)}, f32[8,128]{0,1:T(8,128)}, u32[]{:S(2)}) copy-start(f32[8,128]{0,1:T(8,128)} %get-tuple-element.22) | copy-start | bytes 12292
  25.9 22.3 %collective-permute-start.2 = (f32[1544,128]{1,0:T(8,128)}, f32[1544,128]{1,0:T(8,128)}, u32[]{:S(2)}, u32[]{:S(2)}) collective-permute-start(f32[1544,128]{1,0:T(8,128)} %pad_maximum_fusion.1), channel_id=1, source_target_pairs={{0,2},{1,3},{2,4},{3,5},{4,6},{5,7},{6,8},{7,9},{8,10},{9,11},{10,... | collective-permute-start | bytes 2371592 | tf_op jit(solution)/shard_map/ppermute | solution.py:48
  42.2 3.2 %copy-start.13 = (f32[8,128]{1,0:T(8,128)S(1)}, f32[8,128]{1,0:T(8,128)}, u32[]{:S(2)}) copy-start(f32[8,128]{1,0:T(8,128)} %copy.40) | copy-start | bytes 12292
  45.5 8.0 %copy-start.12 = (f32[8,128]{1,0:T(8,128)S(1)}, f32[8,128]{1,0:T(8,128)}, u32[]{:S(2)}) copy-start(f32[8,128]{1,0:T(8,128)} %copy.43) | copy-start | bytes 12292
  49.4 11.5 %collective-permute-start.3 = (bf16[1544,128]{1,0:T(8,128)(2,1)S(1)}, bf16[1544,128]{1,0:T(8,128)(2,1)S(1)}, u32[]{:S(2)}, u32[]{:S(2)}) collective-permute-start(bf16[1544,128]{1,0:T(8,128)(2,1)S(1)} %convert_element_type.85), channel_id=1, source_target_pairs={{0,2},{1,3},{2,4},{3,5},{4,6},{5,7},{6,8},{7,9},{8,10},{9,11},{10,... | collective-permute-start | bytes 1185800 | tf_op jit(solution)/shard_map/ppermute | solution.py:50
  55.7 12.8 %copy-start.11 = (f32[8,128]{1,0:T(8,128)S(1)}, f32[8,128]{1,0:T(8,128)}, u32[]{:S(2)}) copy-start(f32[8,128]{1,0:T(8,128)} %copy.46) | copy-start | bytes 12292
  61.1 22.3 %copy-start.8 = (f32[24]{0:T(128)S(1)}, f32[24]{0:T(128)}, u32[]{:S(2)}) copy-start(f32[24]{0:T(128)} %get-tuple-element.12) | copy-start | bytes 292
  61.1 22.3 %collective-permute-start.4 = (bf16[24,64,128]{2,1,0:T(8,128)(2,1)S(1)}, bf16[24,64,128]{2,1,0:T(8,128)(2,1)S(1)}, u32[]{:S(2)}, u32[]{:S(2)}) collective-permute-start(bf16[24,64,128]{2,1,0:T(8,128)(2,1)S(1)} %fusion.50), channel_id=1, source_target_pairs={{0,4},{1,5},{2,6},{3,7},{4,8},{5,9},{6,10},{7,11},{8,12},{9,13},{1... | collective-permute-start | bytes 1179656 | tf_op jit(solution)/shard_map/ppermute | solution.py:53
  83.4 5.1 %copy-start.10 = (f32[8,128]{1,0:T(8,128)S(1)}, f32[8,128]{1,0:T(8,128)}, u32[]{:S(2)}) copy-start(f32[8,128]{1,0:T(8,128)} %copy.49) | copy-start | bytes 12292
  83.8 5.1 %copy-start.9 = (f32[8,128]{1,0:T(8,128)S(1)}, f32[8,128]{1,0:T(8,128)}, u32[]{:S(2)}) copy-start(f32[8,128]{1,0:T(8,128)} %copy.52) | copy-start | bytes 12292
  83.8 6.1 %collective-permute-start.5 = (bf16[24,64,128]{2,1,0:T(8,128)(2,1)S(1)}, bf16[24,64,128]{2,1,0:T(8,128)(2,1)S(1)}, u32[]{:S(2)}, u32[]{:S(2)}) collective-permute-start(bf16[24,64,128]{2,1,0:T(8,128)(2,1)S(1)} %get-tuple-element.9), channel_id=1, source_target_pairs={{0,1},{1,0},{2,3},{3,2},{4,5},{5,4},{6,7},{7,6},{8,9},{9,8},{10,11... | collective-permute-start | bytes 1179656 | tf_op jit(solution)/shard_map/ppermute | solution.py:56
  89.9 0.7 copy-start.6
  89.9 0.7 copy-start.15
  90.6 1.4 %copy-start.5 = (f32[48,64]{1,0:T(8,128)S(1)}, f32[48,64]{1,0:T(8,128)}, u32[]{:S(2)}) copy-start(f32[48,64]{1,0:T(8,128)} %mul.329) | copy-start | bytes 36868

commit v8 on v7

--- a/solution.py
+++ b/solution.py
@@ -22,7 +22,7 @@
     return (block[rows, :heads], block[:rows].reshape((heads,) + rest))
 
 
-def chain_carry(decay, local):
+def chain_carry(decay, local, held):
     size, position = (lax.axis_size("ctx"), lax.axis_index("ctx"))
     chips = size // 2
     core = position % 2
@@ -45,7 +45,8 @@
     chip_local = decay_hi[:, None, None] * local_lo + local_hi
     one = [(i, i + 2) for i in range(size - 2)]
     two = [(i, i + 4) for i in range(size - 4)]
-    first_hop = lax.ppermute(packed(chip_decay, chip_local), "ctx", one)
+    sent, held = lax.optimization_barrier((packed(chip_decay, chip_local), held))
+    first_hop = lax.ppermute(sent, "ctx", one)
     decay_a, local_a = unpacked(first_hop, half, rest)
     decay_b, local_b = unpacked(lax.ppermute(first_hop.astype(jnp.bfloat16), "ctx", one).astype(jnp.float32), half, rest)
     decay_ab = decay_a * decay_b
@@ -56,7 +57,7 @@
     got_end = lax.ppermute(jnp.where(low, onward, carry_half), "ctx", swap)
     first = jnp.where(low, carry_half, got_end)
     second = jnp.where(low, got_end, onward)
-    return jnp.concatenate([first, second], axis=0)
+    return (jnp.concatenate([first, second], axis=0), held)
 
 
 def body(xbc, dt_raw, lengths, conv_weight, conv_bias, dt_bias, decay_rate, skip, norm_gain):
@@ -95,17 +96,18 @@
     scaled = (factor[:, :, None] * xs.astype(jnp.float32)).astype(jnp.bfloat16)
     local = jnp.einsum("shp,sn->hpn", scaled, bs, preferred_element_type=jnp.float32)
     block_decay = jnp.exp(cum[-1]) * alive[-1]
+    carry, (cum_late, step_late, seg_late) = chain_carry(block_decay, local, (cum, step_size, seg))
     scores = jnp.dot(cs, bs.T, preferred_element_type=jnp.float32)
     index = jnp.arange(rows, dtype=jnp.int32)
-    mask = (index[:, None] >= index[None, :]) & (seg[:, None] == seg[None, :])
+    mask = (index[:, None] >= index[None, :]) & (seg_late[:, None] == seg_late[None, :])
     group = 8
     pieces = []
     for part_start in range(0, heads, group):
-        cum_part = cum[:, part_start : part_start + group].T
+        cum_part = cum_late[:, part_start : part_start + group].T
         diff = cum_part[:, :, None] - cum_part[:, None, :]
         decay = jnp.where(mask[None], jnp.exp(jnp.where(mask[None], diff, 0.0)), 0.0)
         weights = (
-            scores[None] * decay * step_size[:, part_start : part_start + group].T[:, None, :]
+            scores[None] * decay * step_late[:, part_start : part_start + group].T[:, None, :]
         ).astype(jnp.bfloat16)
         pieces.append(
             jnp.einsum(
@@ -116,7 +118,6 @@
             )
         )
     inner = jnp.concatenate(pieces, axis=1)
-    carry = chain_carry(block_decay, local)
     carried = carry.astype(jnp.bfloat16)
     outer = (
         jnp.exp(cum)[:, :, None]

time: 94.9 us -> 95 us (level)
  the two profiles are of different devices: /device:TPU:183 before, /device:TPU:189 now
where the time goes in v8:
time: 95 us; the launch traced here: 93.7 us
  starting transfers between devices  28.4 us (30%)
  waiting for transfers between devices  25.4 us (27%)
  local copies, waits for them, and re-layouts  21 us (22%)
  other arithmetic  11.6 us (12%)
  matrix products  7.02 us (7%)
    ppermute x1, waiting for transfers between devices, chain_carry(): lax.ppermute(local_ab.astype(jnp.bfloat16), 'ctx', two).astype(jnp.float32)  13.3 us
    ppermute x1, starting transfers between devices, chain_carry(): lax.ppermute(local_ab.astype(jnp.bfloat16), 'ctx', two).astype(jnp.float32)  7.44 us
    ppermute x1, waiting for transfers between devices, chain_carry(): first_hop = lax.ppermute(sent, 'ctx', one)  6.61 us
    transpose x7, local copies, waits for them, and re-layouts, body(): step_late[:, part_start:part_start + group].T[:, None, :]  6.39 us
    ppermute x1, starting transfers between devices, chain_carry(): first_hop = lax.ppermute(sent, 'ctx', one)  5.2 us
    ppermute x1, starting transfers between devices, chain_carry(): got_end = lax.ppermute(jnp.where(low, onward, carry_half), 'ctx', swap)  5.2 us
    ppermute x1, waiting for transfers between devices, chain_carry(): lax.ppermute(first_hop.astype(jnp.bfloat16), 'ctx', one).astype(jnp.float32)  4.85 us
    ppermute x1, starting transfers between devices, shifted(): return lax.ppermute(block, axis, route)  4.55 us
  transfers between devices with their start and end apart: 6, of which 4 were waited for; matrix products, arithmetic and copies ran while one was open for 26% of the time, Pallas kernels for 0%

profile of v8, /device:TPU:189, one launch (start us, length us, event | category | flops | bytes accessed | tf_op | source)
XLA Modules:
  0.0 93.7 jit_solution(5813241422914294968)
XLA Ops:
  0.0 1.0 %slice.138 = bf16[16,3328]{1,0:T(8,128)(2,1)S(1)} slice(bf16[128,3328]{1,0:T(8,128)(2,1)} %param.9), slice={[112:128], [0:3328]} | slice | bytes 212992 | tf_op jit(solution)/shard_map/slice | solution.py:80
  1.0 4.5 %collective-permute-start = (bf16[16,3328]{1,0:T(8,128)(2,1)S(1)}, bf16[16,3328]{1,0:T(8,128)(2,1)S(1)}, u32[]{:S(2)}, u32[]{:S(2)}) collective-permute-start(bf16[16,3328]{1,0:T(8,128)(2,1)S(1)} %slice.138), channel_id=1, source_target_pairs={{0,1},{1,2},{2,3},{3,4},{4,5},{5,6},{6,7},{7,8},{8,9},{9,10},{10,1... | collective-permute-start | bytes 319496 | tf_op jit(solution)/shard_map/ppermute | solution.py:10
  7.0 1.4 %compare_convert_fusion.1 = (f32[128]{0:T(128)S(1)}, f32[128]{0:T(128)S(1)}, pred[128]{0:T(512)(128)(4,1)S(1)}, pred[128]{0:T(512)(128)(4,1)S(1)}, pred[128]{0:T(512)(128)(4,1)S(1)}) fusion(s32[]{:T(128)} %bitcast.2, s32[144]{0:T(256)S(1)} %compare_select_fusion.1, s32[]{:T(128)} %bitcast.5), kind=kLoop, calls=%fused_computation.116 | loop fusion | flops 896 | bytes 3464 | tf_op jit(solution)/shard_map/convert_element_type | solution.py:94
  9.8 1.1 %slice_reduce_fusion.3 = (f32[3328]{0:T(1024)S(1)}, f32[3328]{0:T(1024)S(1)}, f32[3328]{0:T(1024)S(1)}, f32[3328]{0:T(1024)S(1)}) fusion(f32[4,3328]{1,0:T(4,128)} %param.12), kind=kLoop, calls=%fused_computation.108 | loop fusion | bytes 106496 | tf_op jit(solution)/shard_map/slice | solution.py:82
  12.8 1.6 %multiply_convert_fusion = bf16[128,3328]{1,0:T(8,128)(2,1)S(1)} fusion(bf16[128,3328]{1,0:T(8,128)(2,1)S(1)} %copy-done, bf16[144,3328]{1,0:T(8,128)(2,1)S(1)} %constant_dynamic-update-slice_fusion, f32[3328]{0:T(1024)S(1)} %get-tuple-element.15, f32[3328]{0:T(1024)S(1)} %get-tuple-element.16, f32[3328]{0:T(1024)S(1)} %get-tuple-element.14, ...), kind=kLoop, calls=%fused_computation.2 | loop fusion | flops 8519680 | bytes 4326784 | tf_op jit(solution)/shard_map/convert_element_type | solution.py:87
  15.8 1.1 %fusion.8 = f32[48,64,128]{2,1,0:T(8,128)S(1)} fusion(bf16[128,48,64]{0,2,1:T(8,128)(2,1)S(1)} %bitcast.95, f32[128,48]{0,1:T(8,128)S(1)} %copy.64, bf16[128,3328]{1,0:T(8,128)(2,1)} %copy-done.1), kind=kOutput, calls=%fused_computation.21 | convolution fusion | flops 101842944 | bytes 2416640 | tf_op jit(solution)/shard_map/shp,sn->hpn/dot_general | solution.py:97
  17.0 0.9 %pad_maximum_fusion = f32[1544,128]{1,0:T(8,128)} fusion(f32[8,128]{1,0:T(8,128)S(1)} %pad_bitcast_fusion.1, f32[1536,128]{1,0:T(8,128)S(1)} %bitcast.107), kind=kLoop, calls=%fused_computation.19 | loop fusion | flops 197632 | bytes 1581056 | tf_op jit(solution)/shard_map/concatenate | solution.py:17
  17.9 1.9 %collective-permute-start.1 = (f32[1544,128]{1,0:T(8,128)}, f32[1544,128]{1,0:T(8,128)}, u32[]{:S(2)}, u32[]{:S(2)}) collective-permute-start(f32[1544,128]{1,0:T(8,128)} %pad_maximum_fusion), channel_id=1, source_target_pairs={{0,1},{1,0},{2,3},{3,2},{4,5},{5,4},{6,7},{7,6},{8,9},{9,8},{10,11... | collective-permute-start | bytes 2371592 | tf_op jit(solution)/shard_map/ppermute | solution.py:36
  21.3 1.5 %fusion.55 = f32[128,128]{1,0:T(8,128)} fusion(bf16[128,3328]{1,0:T(8,128)(2,1)} %copy-done.1), kind=kOutput, calls=%fused_computation.98 | convolution fusion | flops 4194304 | bytes 131072 | tf_op jit(solution)/shard_map/dot_general | solution.py:100
  24.3 1.2 %slice.186 = f32[1536,128]{1,0:T(8,128)S(1)} slice(f32[1544,128]{1,0:T(8,128)} %collective-permute-done.1), slice={[0:1536], [0:128]} | slice | bytes 1572864 | tf_op jit(solution)/shard_map/slice | solution.py:38
  25.6 0.9 %pad_maximum_fusion.1 = f32[1544,128]{1,0:T(8,128)} fusion(f32[8,128]{1,0:T(8,128)S(1)} %pad_bitcast_fusion, f32[1536,128]{1,0:T(8,128)S(1)} %bitcast.109), kind=kLoop, calls=%fused_computation.20 | loop fusion | flops 197632 | bytes 1581056 | tf_op jit(solution)/shard_map/concatenate | solution.py:17
  26.6 5.2 %collective-permute-start.2 = (f32[1544,128]{1,0:T(8,128)}, f32[1544,128]{1,0:T(8,128)}, u32[]{:S(2)}, u32[]{:S(2)}) collective-permute-start(f32[1544,128]{1,0:T(8,128)} %pad_maximum_fusion.1), channel_id=1, source_target_pairs={{0,2},{1,3},{2,4},{3,5},{4,6},{5,7},{6,8},{7,9},{8,10},{9,11},{10,... | collective-permute-start | bytes 2371592 | tf_op jit(solution)/shard_map/ppermute | solution.py:49
  31.8 0.9 %slice_bitcast_fusion = (f32[8,128]{0,1:T(8,128)}, f32[8,128]{0,1:T(8,128)}, f32[8,128]{0,1:T(8,128)}, f32[8,128]{0,1:T(8,128)}, f32[8,128]{0,1:T(8,128)}, /*ind...) fusion(f32[128,48]{1,0:T(8,128)S(1)} %get-tuple-element.11, ...), kind=kLoop, calls=%fused_computation.79 | loop fusion | bytes 98304 | tf_op jit(solution)/shard_map/transpose | solution.py:110
  32.7 0.9 copy.82
  33.6 0.9 copy.79
  34.6 0.9 copy.76
  35.5 0.9 copy.73
  36.4 0.9 copy.70
  37.3 0.9 copy.67
  38.2 0.9 copy.65
  39.1 0.9 copy.68
  40.4 1.2 %fusion.7 = f32[128,48,64]{0,2,1:T(8,128)S(1)} fusion(bf16[128,48,64]{0,2,1:T(8,128)(2,1)S(1)} %bitcast.96, f32[8,128]{1,0:T(8,128)S(1)} %copy.67, f32[8,128]{1,0:T(8,128)S(1)} %copy.65, f32[128,128]{1,0:T(8,128)} %fusion.55, pred[128,128]{1,0:T(8,128)(4,1)S(1)} %fusion.51), kind=kOutput, calls=%fused_computation.18 | convolution fusion | flops 17563648 | bytes 1142784 | tf_op jit(solution)/shard_map/hts,shp->thp/dot_general | solution.py:113
  42.0 6.6 %collective-permute-done.2 = f32[1544,128]{1,0:T(8,128)} collective-permute-done((f32[1544,128]{1,0:T(8,128)}, f32[1544,128]{1,0:T(8,128)}, u32[]{:S(2)}, u32[]{:S(2)}) %collective-permute-start.2) | collective-permute-done | bytes 790560 | tf_op jit(solution)/shard_map/ppermute | solution.py:49
  48.6 1.2 %convert_element_type.85 = bf16[1544,128]{1,0:T(8,128)(2,1)S(1)} convert(f32[1544,128]{1,0:T(8,128)} %collective-permute-done.2) | non-fusion elementwise | flops 197632 | bytes 1185792 | tf_op jit(solution)/shard_map/convert_element_type | solution.py:51
  49.8 4.1 %collective-permute-start.3 = (bf16[1544,128]{1,0:T(8,128)(2,1)S(1)}, bf16[1544,128]{1,0:T(8,128)(2,1)S(1)}, u32[]{:S(2)}, u32[]{:S(2)}) collective-permute-start(bf16[1544,128]{1,0:T(8,128)(2,1)S(1)} %convert_element_type.85), channel_id=1, source_target_pairs={{0,2},{1,3},{2,4},{3,5},{4,6},{5,7},{6,8},{7,9},{8,10},{9,11},{10,... | collective-permute-start | bytes 1185800 | tf_op jit(solution)/shard_map/ppermute | solution.py:51
  54.2 1.2 %slice.190 = f32[1536,128]{1,0:T(8,128)S(1)} slice(f32[1544,128]{1,0:T(8,128)} %collective-permute-done.2), slice={[0:1536], [0:128]} | slice | bytes 1572864 | tf_op jit(solution)/shard_map/slice | solution.py:22
  56.1 4.8 %collective-permute-done.3 = bf16[1544,128]{1,0:T(8,128)(2,1)S(1)} collective-permute-done((bf16[1544,128]{1,0:T(8,128)(2,1)S(1)}, bf16[1544,128]{1,0:T(8,128)(2,1)S(1)}, u32[]{:S(2)}, u32[]{:S(2)}) %collective-permute-start.3) | collective-permute-done | bytes 395296 | tf_op jit(solution)/shard_map/ppermute | solution.py:51
  61.2 7.4 %collective-permute-start.4 = (bf16[24,64,128]{2,1,0:T(8,128)(2,1)S(1)}, bf16[24,64,128]{2,1,0:T(8,128)(2,1)S(1)}, u32[]{:S(2)}, u32[]{:S(2)}) collective-permute-start(bf16[24,64,128]{2,1,0:T(8,128)(2,1)S(1)} %fusion.50), channel_id=1, source_target_pairs={{0,4},{1,5},{2,6},{3,7},{4,8},{5,9},{6,10},{7,11},{8,12},{9,13},{1... | collective-permute-start | bytes 1179656 | tf_op jit(solution)/shard_map/ppermute | solution.py:54
  69.7 13.3 %collective-permute-done.4 = bf16[24,64,128]{2,1,0:T(8,128)(2,1)S(1)} collective-permute-done((bf16[24,64,128]{2,1,0:T(8,128)(2,1)S(1)}, bf16[24,64,128]{2,1,0:T(8,128)(2,1)S(1)}, u32[]{:S(2)}, u32[]{:S(2)}) %collective-permute-start.4) | collective-permute-done | bytes 393248 | tf_op jit(solution)/shard_map/ppermute | solution.py:54
  83.4 5.2 %collective-permute-start.5 = (bf16[24,64,128]{2,1,0:T(8,128)(2,1)S(1)}, bf16[24,64,128]{2,1,0:T(8,128)(2,1)S(1)}, u32[]{:S(2)}, u32[]{:S(2)}) collective-permute-start(bf16[24,64,128]{2,1,0:T(8,128)(2,1)S(1)} %get-tuple-element.17), channel_id=1, source_target_pairs={{0,1},{1,0},{2,3},{3,2},{4,5},{5,4},{6,7},{7,6},{8,9},{9,8},{10,11... | collective-permute-start | bytes 1179656 | tf_op jit(solution)/shard_map/ppermute | solution.py:57
  90.7 1.4 %multiply_reduce_fusion = (f32[128,48]{0,1:T(8,128)S(1)}, f32[128,48,64]{0,2,1:T(8,128)S(1)}) fusion(bf16[128,48,64]{0,2,1:T(8,128)(2,1)S(1)} %bitcast.102, f32[48]{0:T(128)S(1)} %copy-done.7, f32[128,48,64]{0,2,1:T(8,128)S(1)} %fusion.2, bf16[24,64,128]{2,1,0:T(8,128)(2,1)S(1)} %get-tuple-element.25, bf16[24,64,128]{2,1,0:T(8,128)(2,1)S(1)} %get-tuple-element.24, ...), kind=kOutput, calls=%fused_computation.6 | convolution fusion | flops 104982528 | bytes 4800704 | tf_op jit(solution)/shard_map/hpn,tn->thp/dot_general | solution.py:125
  92.5 1.2 %copy.84 = bf16[128,3072]{1,0:T(8,128)(2,1)} copy(bf16[128,3072]{0,1:T(8,128)(2,1)S(1)} %bitcast.108) | data formatting | bytes 1572864 | tf_op jit(solution)/shard_map/reshape | solution.py:133
  (65 shorter events, 15.2 us)
Async XLA Ops:
  0.0 12.7 %copy-start = (bf16[128,3328]{1,0:T(8,128)(2,1)S(1)}, bf16[128,3328]{1,0:T(8,128)(2,1)}, u32[]{:S(2)}) copy-start(bf16[128,3328]{1,0:T(8,128)(2,1)} %param.9) | copy-start | bytes 2555908
  0.0 12.8 %copy-start.5 = (f32[3328]{0:T(1024)S(1)}, f32[3328]{0:T(1024)}, u32[]{:S(2)}) copy-start(f32[3328]{0:T(1024)} %param.13) | copy-start | bytes 39940
  1.0 11.7 %collective-permute-start = (bf16[16,3328]{1,0:T(8,128)(2,1)S(1)}, bf16[16,3328]{1,0:T(8,128)(2,1)S(1)}, u32[]{:S(2)}, u32[]{:S(2)}) collective-permute-start(bf16[16,3328]{1,0:T(8,128)(2,1)S(1)} %slice.138), channel_id=1, source_target_pairs={{0,1},{1,2},{2,3},{3,4},{4,5},{5,6},{6,7},{7,8},{8,9},{9,10},{10,1... | collective-permute-start | bytes 319496 | tf_op jit(solution)/shard_map/ppermute | solution.py:10
  14.4 0.9 copy-start.1
  16.9 3.0 %copy-start.6 = (f32[3072]{0:T(1024)S(1)}, f32[3072]{0:T(1024)}, u32[]{:S(2)}) copy-start(f32[3072]{0:T(1024)} %param.17) | copy-start | bytes 36868
  17.9 4.9 %collective-permute-start.1 = (f32[1544,128]{1,0:T(8,128)}, f32[1544,128]{1,0:T(8,128)}, u32[]{:S(2)}, u32[]{:S(2)}) collective-permute-start(f32[1544,128]{1,0:T(8,128)} %pad_maximum_fusion), channel_id=1, source_target_pairs={{0,1},{1,0},{2,3},{3,2},{4,5},{5,4},{6,7},{7,6},{8,9},{9,8},{10,11... | collective-permute-start | bytes 2371592 | tf_op jit(solution)/shard_map/ppermute | solution.py:36
  26.6 22.0 %collective-permute-start.2 = (f32[1544,128]{1,0:T(8,128)}, f32[1544,128]{1,0:T(8,128)}, u32[]{:S(2)}, u32[]{:S(2)}) collective-permute-start(f32[1544,128]{1,0:T(8,128)} %pad_maximum_fusion.1), channel_id=1, source_target_pairs={{0,2},{1,3},{2,4},{3,5},{4,6},{5,7},{6,8},{7,9},{8,10},{9,11},{10,... | collective-permute-start | bytes 2371592 | tf_op jit(solution)/shard_map/ppermute | solution.py:49
  32.7 8.9 %copy-start.4 = (f32[128,128]{1,0:T(8,128)S(1)}, f32[128,128]{1,0:T(8,128)}, u32[]{:S(2)}) copy-start(f32[128,128]{1,0:T(8,128)} %fusion.55) | copy-start | bytes 196612
  49.8 11.2 %collective-permute-start.3 = (bf16[1544,128]{1,0:T(8,128)(2,1)S(1)}, bf16[1544,128]{1,0:T(8,128)(2,1)S(1)}, u32[]{:S(2)}, u32[]{:S(2)}) collective-permute-start(bf16[1544,128]{1,0:T(8,128)(2,1)S(1)} %convert_element_type.85), channel_id=1, source_target_pairs={{0,2},{1,3},{2,4},{3,5},{4,6},{5,7},{6,8},{7,9},{8,10},{9,11},{10,... | collective-permute-start | bytes 1185800 | tf_op jit(solution)/shard_map/ppermute | solution.py:51
  61.2 21.8 %collective-permute-start.4 = (bf16[24,64,128]{2,1,0:T(8,128)(2,1)S(1)}, bf16[24,64,128]{2,1,0:T(8,128)(2,1)S(1)}, u32[]{:S(2)}, u32[]{:S(2)}) collective-permute-start(bf16[24,64,128]{2,1,0:T(8,128)(2,1)S(1)} %fusion.50), channel_id=1, source_target_pairs={{0,4},{1,5},{2,6},{3,7},{4,8},{5,9},{6,10},{7,11},{8,12},{9,13},{1... | collective-permute-start | bytes 1179656 | tf_op jit(solution)/shard_map/ppermute | solution.py:54
  83.4 6.5 %collective-permute-start.5 = (bf16[24,64,128]{2,1,0:T(8,128)(2,1)S(1)}, bf16[24,64,128]{2,1,0:T(8,128)(2,1)S(1)}, u32[]{:S(2)}, u32[]{:S(2)}) collective-permute-start(bf16[24,64,128]{2,1,0:T(8,128)(2,1)S(1)} %get-tuple-element.17), channel_id=1, source_target_pairs={{0,1},{1,0},{2,3},{3,2},{4,5},{5,4},{6,7},{7,6},{8,9},{9,8},{10,11... | collective-permute-start | bytes 1179656 | tf_op jit(solution)/shard_map/ppermute | solution.py:57
  89.9 0.7 copy-start.3
  89.9 0.7 copy-start.7
  90.7 1.4 %copy-start.2 = (f32[48,64]{1,0:T(8,128)S(1)}, f32[48,64]{1,0:T(8,128)}, u32[]{:S(2)}) copy-start(f32[48,64]{1,0:T(8,128)} %mul.329) | copy-start | bytes 36868

commit v9 on v8

--- a/solution.py
+++ b/solution.py
@@ -13,12 +13,12 @@
 def packed(decay, local):
     lanes = local.shape[-1]
     flat = local.reshape(-1, lanes)
-    spare = jnp.pad(decay, (0, 8 * lanes - decay.shape[0])).reshape(8, lanes)
+    spare = jnp.pad(decay, (0, 16 * lanes - decay.shape[0])).reshape(16, lanes)
     return jnp.concatenate([flat, spare], axis=0)
 
 
 def unpacked(block, heads, rest):
-    rows = block.shape[0] - 8
+    rows = block.shape[0] - 16
     return (block[rows, :heads], block[:rows].reshape((heads,) + rest))
 
 
@@ -96,8 +96,10 @@
     scaled = (factor[:, :, None] * xs.astype(jnp.float32)).astype(jnp.bfloat16)
     local = jnp.einsum("shp,sn->hpn", scaled, bs, preferred_element_type=jnp.float32)
     block_decay = jnp.exp(cum[-1]) * alive[-1]
-    carry, (cum_late, step_late, seg_late) = chain_carry(block_decay, local, (cum, step_size, seg))
-    scores = jnp.dot(cs, bs.T, preferred_element_type=jnp.float32)
+    carry, (cum_late, step_late, seg_late, cs_late, bs_late, xs_late) = chain_carry(
+        block_decay, local, (cum, step_size, seg, cs, bs, xs)
+    )
+    scores = jnp.dot(cs_late, bs_late.T, preferred_element_type=jnp.float32)
     index = jnp.arange(rows, dtype=jnp.int32)
     mask = (index[:, None] >= index[None, :]) & (seg_late[:, None] == seg_late[None, :])
     group = 8
@@ -113,7 +115,7 @@
             jnp.einsum(
                 "hts,shp->thp",
                 weights,
-                xs[:, part_start : part_start + group, :],
+                xs_late[:, part_start : part_start + group, :],
                 preferred_element_type=jnp.float32,
             )
         )

time: 95 us -> 95.1 us (level)
  the two profiles are of different devices: /device:TPU:189 before, /device:TPU:185 now
where the time goes in v9:
time: 95.1 us; the launch traced here: 93.7 us
  starting transfers between devices  28.4 us (30%)
  waiting for transfers between devices  25.4 us (27%)
  local copies, waits for them, and re-layouts  22.4 us (24%)
  other arithmetic  11.6 us (12%)
  matrix products  5.59 us (6%)
    ppermute x1, waiting for transfers between devices, chain_carry(): lax.ppermute(local_ab.astype(jnp.bfloat16), 'ctx', two).astype(jnp.float32)  13.3 us
    ppermute x1, starting transfers between devices, chain_carry(): lax.ppermute(local_ab.astype(jnp.bfloat16), 'ctx', two).astype(jnp.float32)  7.44 us
    ppermute x1, waiting for transfers between devices, chain_carry(): first_hop = lax.ppermute(sent, 'ctx', one)  6.66 us
    transpose x7, local copies, waits for them, and re-layouts, body(): step_late[:, part_start:part_start + group].T[:, None, :]  6.36 us
    ppermute x1, starting transfers between devices, chain_carry(): first_hop = lax.ppermute(sent, 'ctx', one)  5.2 us
    ppermute x1, starting transfers between devices, chain_carry(): got_end = lax.ppermute(jnp.where(low, onward, carry_half), 'ctx', swap)  5.2 us
    ppermute x1, waiting for transfers between devices, chain_carry(): lax.ppermute(first_hop.astype(jnp.bfloat16), 'ctx', one).astype(jnp.float32)  4.89 us
    ppermute x1, starting transfers between devices, shifted(): return lax.ppermute(block, axis, route)  4.55 us
  transfers between devices with their start and end apart: 6, of which 4 were waited for; matrix products, arithmetic and copies ran while one was open for 26% of the time, Pallas kernels for 0%

profile of v9, /device:TPU:185, one launch (start us, length us, event | category | flops | bytes accessed | tf_op | source)
XLA Modules:
  0.0 93.7 jit_solution(12071482550650947508)
XLA Ops:
  0.0 1.0 %slice.140 = bf16[16,3328]{1,0:T(8,128)(2,1)S(1)} slice(bf16[128,3328]{1,0:T(8,128)(2,1)} %param.9), slice={[112:128], [0:3328]} | slice | bytes 212992 | tf_op jit(solution)/shard_map/slice | solution.py:80
  1.0 4.5 %collective-permute-start = (bf16[16,3328]{1,0:T(8,128)(2,1)S(1)}, bf16[16,3328]{1,0:T(8,128)(2,1)S(1)}, u32[]{:S(2)}, u32[]{:S(2)}) collective-permute-start(bf16[16,3328]{1,0:T(8,128)(2,1)S(1)} %slice.140), channel_id=1, source_target_pairs={{0,1},{1,2},{2,3},{3,4},{4,5},{5,6},{6,7},{7,8},{8,9},{9,10},{10,1... | collective-permute-start | bytes 319496 | tf_op jit(solution)/shard_map/ppermute | solution.py:10
  7.0 1.4 %compare_convert_fusion.1 = (f32[128]{0:T(128)S(1)}, f32[128]{0:T(128)S(1)}, pred[128]{0:T(512)(128)(4,1)S(1)}, pred[128]{0:T(512)(128)(4,1)S(1)}, pred[128]{0:T(512)(128)(4,1)S(1)}) fusion(s32[]{:T(128)} %bitcast.1, s32[144]{0:T(256)S(1)} %compare_select_fusion.1, s32[]{:T(128)} %bitcast.5), kind=kLoop, calls=%fused_computation.111 | loop fusion | flops 896 | bytes 3464 | tf_op jit(solution)/shard_map/convert_element_type | solution.py:94
  9.8 1.1 %slice_reduce_fusion.3 = (f32[3328]{0:T(1024)S(1)}, f32[3328]{0:T(1024)S(1)}, f32[3328]{0:T(1024)S(1)}, f32[3328]{0:T(1024)S(1)}) fusion(f32[4,3328]{1,0:T(4,128)} %param.12), kind=kLoop, calls=%fused_computation.103 | loop fusion | bytes 106496 | tf_op jit(solution)/shard_map/slice | solution.py:82
  12.8 1.6 %multiply_convert_fusion = bf16[128,3328]{1,0:T(8,128)(2,1)S(1)} fusion(bf16[128,3328]{1,0:T(8,128)(2,1)S(1)} %copy-done, bf16[144,3328]{1,0:T(8,128)(2,1)S(1)} %constant_dynamic-update-slice_fusion, f32[3328]{0:T(1024)S(1)} %get-tuple-element.21, f32[3328]{0:T(1024)S(1)} %get-tuple-element.22, f32[3328]{0:T(1024)S(1)} %get-tuple-element.20, ...), kind=kLoop, calls=%fused_computation.2 | loop fusion | flops 8519680 | bytes 4326784 | tf_op jit(solution)/shard_map/convert_element_type | solution.py:87
  14.4 0.9 copy-done.1
  15.8 1.1 %fusion.8 = f32[48,64,128]{2,1,0:T(8,128)S(1)} fusion(bf16[128,48,64]{0,2,1:T(8,128)(2,1)S(1)} %bitcast.97, f32[128,48]{0,1:T(8,128)S(1)} %copy.63, bf16[128,3328]{1,0:T(8,128)(2,1)} %copy-done.1), kind=kOutput, calls=%fused_computation.21 | convolution fusion | flops 101842944 | bytes 2416640 | tf_op jit(solution)/shard_map/shp,sn->hpn/dot_general | solution.py:97
  17.0 0.9 %pad_maximum_fusion = f32[1552,128]{1,0:T(8,128)} fusion(f32[16,128]{1,0:T(8,128)S(1)} %pad_bitcast_fusion.1, f32[1536,128]{1,0:T(8,128)S(1)} %bitcast.109), kind=kLoop, calls=%fused_computation.19 | loop fusion | flops 198656 | bytes 1589248 | tf_op jit(solution)/shard_map/concatenate | solution.py:17
  17.9 1.9 %collective-permute-start.1 = (f32[1552,128]{1,0:T(8,128)}, f32[1552,128]{1,0:T(8,128)}, u32[]{:S(2)}, u32[]{:S(2)}) collective-permute-start(f32[1552,128]{1,0:T(8,128)} %pad_maximum_fusion), channel_id=1, source_target_pairs={{0,1},{1,0},{2,3},{3,2},{4,5},{5,4},{6,7},{7,6},{8,9},{9,8},{10,11... | collective-permute-start | bytes 2383880 | tf_op jit(solution)/shard_map/ppermute | solution.py:36
  21.3 1.4 %fusion.65 = (bf16[128,128]{1,0:T(8,128)(2,1)}, bf16[128,128]{1,0:T(8,128)(2,1)}) fusion(bf16[128,3328]{1,0:T(8,128)(2,1)} %copy-done.1), kind=kLoop, calls=%fused_computation.135 | loop fusion | bytes 131072 | tf_op jit(solution)/shard_map/slice | solution.py:89
  24.1 1.2 %slice.186 = f32[1536,128]{1,0:T(8,128)S(1)} slice(f32[1552,128]{1,0:T(8,128)} %collective-permute-done.1), slice={[0:1536], [0:128]} | slice | bytes 1572864 | tf_op jit(solution)/shard_map/slice | solution.py:38
  25.5 0.9 %pad_maximum_fusion.1 = f32[1552,128]{1,0:T(8,128)} fusion(f32[16,128]{1,0:T(8,128)S(1)} %pad_bitcast_fusion, f32[1536,128]{1,0:T(8,128)S(1)} %bitcast.111), kind=kLoop, calls=%fused_computation.20 | loop fusion | flops 198656 | bytes 1589248 | tf_op jit(solution)/shard_map/concatenate | solution.py:17
  26.5 5.2 %collective-permute-start.2 = (f32[1552,128]{1,0:T(8,128)}, f32[1552,128]{1,0:T(8,128)}, u32[]{:S(2)}, u32[]{:S(2)}) collective-permute-start(f32[1552,128]{1,0:T(8,128)} %pad_maximum_fusion.1), channel_id=1, source_target_pairs={{0,2},{1,3},{2,4},{3,5},{4,6},{5,7},{6,8},{7,9},{8,10},{9,11},{10,... | collective-permute-start | bytes 2383880 | tf_op jit(solution)/shard_map/ppermute | solution.py:49
  31.7 0.9 slice_bitcast_fusion
  33.6 0.9 copy.79
  34.5 0.9 copy.76
  35.4 0.9 copy.73
  36.3 0.9 copy.70
  37.2 0.9 copy.67
  38.1 0.9 copy.65
  39.0 0.9 copy.68
  40.2 0.9 fusion.67
  41.9 6.7 %collective-permute-done.2 = f32[1552,128]{1,0:T(8,128)} collective-permute-done((f32[1552,128]{1,0:T(8,128)}, f32[1552,128]{1,0:T(8,128)}, u32[]{:S(2)}, u32[]{:S(2)}) %collective-permute-start.2) | collective-permute-done | bytes 794656 | tf_op jit(solution)/shard_map/ppermute | solution.py:49
  48.5 1.2 %convert_element_type.85 = bf16[1552,128]{1,0:T(8,128)(2,1)S(1)} convert(f32[1552,128]{1,0:T(8,128)} %collective-permute-done.2) | non-fusion elementwise | flops 198656 | bytes 1191936 | tf_op jit(solution)/shard_map/convert_element_type | solution.py:51
  49.7 4.1 %collective-permute-start.3 = (bf16[1552,128]{1,0:T(8,128)(2,1)S(1)}, bf16[1552,128]{1,0:T(8,128)(2,1)S(1)}, u32[]{:S(2)}, u32[]{:S(2)}) collective-permute-start(bf16[1552,128]{1,0:T(8,128)(2,1)S(1)} %convert_element_type.85), channel_id=1, source_target_pairs={{0,2},{1,3},{2,4},{3,5},{4,6},{5,7},{6,8},{7,9},{8,10},{9,11},{10,... | collective-permute-start | bytes 1191944 | tf_op jit(solution)/shard_map/ppermute | solution.py:51
  54.2 1.2 %slice.191 = f32[1536,128]{1,0:T(8,128)S(1)} slice(f32[1552,128]{1,0:T(8,128)} %collective-permute-done.2), slice={[0:1536], [0:128]} | slice | bytes 1572864 | tf_op jit(solution)/shard_map/slice | solution.py:22
  56.1 4.9 %collective-permute-done.3 = bf16[1552,128]{1,0:T(8,128)(2,1)S(1)} collective-permute-done((bf16[1552,128]{1,0:T(8,128)(2,1)S(1)}, bf16[1552,128]{1,0:T(8,128)(2,1)S(1)}, u32[]{:S(2)}, u32[]{:S(2)}) %collective-permute-start.3) | collective-permute-done | bytes 397344 | tf_op jit(solution)/shard_map/ppermute | solution.py:51
  61.2 7.4 %collective-permute-start.4 = (bf16[24,64,128]{2,1,0:T(8,128)(2,1)S(1)}, bf16[24,64,128]{2,1,0:T(8,128)(2,1)S(1)}, u32[]{:S(2)}, u32[]{:S(2)}) collective-permute-start(bf16[24,64,128]{2,1,0:T(8,128)(2,1)S(1)} %fusion.50), channel_id=1, source_target_pairs={{0,4},{1,5},{2,6},{3,7},{4,8},{5,9},{6,10},{7,11},{8,12},{9,13},{1... | collective-permute-start | bytes 1179656 | tf_op jit(solution)/shard_map/ppermute | solution.py:54
  69.7 13.3 %collective-permute-done.4 = bf16[24,64,128]{2,1,0:T(8,128)(2,1)S(1)} collective-permute-done((bf16[24,64,128]{2,1,0:T(8,128)(2,1)S(1)}, bf16[24,64,128]{2,1,0:T(8,128)(2,1)S(1)}, u32[]{:S(2)}, u32[]{:S(2)}) %collective-permute-start.4) | collective-permute-done | bytes 393248 | tf_op jit(solution)/shard_map/ppermute | solution.py:54
  83.4 5.2 %collective-permute-start.5 = (bf16[24,64,128]{2,1,0:T(8,128)(2,1)S(1)}, bf16[24,64,128]{2,1,0:T(8,128)(2,1)S(1)}, u32[]{:S(2)}, u32[]{:S(2)}) collective-permute-start(bf16[24,64,128]{2,1,0:T(8,128)(2,1)S(1)} %get-tuple-element.23), channel_id=1, source_target_pairs={{0,1},{1,0},{2,3},{3,2},{4,5},{5,4},{6,7},{7,6},{8,9},{9,8},{10,11... | collective-permute-start | bytes 1179656 | tf_op jit(solution)/shard_map/ppermute | solution.py:57
  90.7 1.4 %multiply_reduce_fusion = (f32[128,48]{0,1:T(8,128)S(1)}, f32[128,48,64]{0,2,1:T(8,128)S(1)}) fusion(bf16[128,48,64]{0,2,1:T(8,128)(2,1)S(1)} %bitcast.104, f32[48]{0:T(128)S(1)} %copy-done.6, f32[128,48,64]{0,2,1:T(8,128)S(1)} %fusion.2, bf16[24,64,128]{2,1,0:T(8,128)(2,1)S(1)} %get-tuple-element.31, bf16[24,64,128]{2,1,0:T(8,128)(2,1)S(1)} %get-tuple-element.30, ...), kind=kOutput, calls=%fused_computation.6 | convolution fusion | flops 104982528 | bytes 4800704 | tf_op jit(solution)/shard_map/hpn,tn->thp/dot_general | solution.py:127
  92.5 1.2 %copy.84 = bf16[128,3072]{1,0:T(8,128)(2,1)} copy(bf16[128,3072]{0,1:T(8,128)(2,1)S(1)} %bitcast.110) | data formatting | bytes 1572864 | tf_op jit(solution)/shard_map/reshape | solution.py:135
  (64 shorter events, 15.5 us)
Async XLA Ops:
  0.0 12.7 %copy-start = (bf16[128,3328]{1,0:T(8,128)(2,1)S(1)}, bf16[128,3328]{1,0:T(8,128)(2,1)}, u32[]{:S(2)}) copy-start(bf16[128,3328]{1,0:T(8,128)(2,1)} %param.9) | copy-start | bytes 2555908
  0.0 12.8 %copy-start.4 = (f32[3328]{0:T(1024)S(1)}, f32[3328]{0:T(1024)}, u32[]{:S(2)}) copy-start(f32[3328]{0:T(1024)} %param.13) | copy-start | bytes 39940
  1.0 11.7 %collective-permute-start = (bf16[16,3328]{1,0:T(8,128)(2,1)S(1)}, bf16[16,3328]{1,0:T(8,128)(2,1)S(1)}, u32[]{:S(2)}, u32[]{:S(2)}) collective-permute-start(bf16[16,3328]{1,0:T(8,128)(2,1)S(1)} %slice.140), channel_id=1, source_target_pairs={{0,1},{1,2},{2,3},{3,4},{4,5},{5,6},{6,7},{7,8},{8,9},{9,10},{10,1... | collective-permute-start | bytes 319496 | tf_op jit(solution)/shard_map/ppermute | solution.py:10
  14.4 0.9 copy-start.1
  16.9 3.0 %copy-start.5 = (f32[3072]{0:T(1024)S(1)}, f32[3072]{0:T(1024)}, u32[]{:S(2)}) copy-start(f32[3072]{0:T(1024)} %param.17) | copy-start | bytes 36868
  17.9 4.8 %collective-permute-start.1 = (f32[1552,128]{1,0:T(8,128)}, f32[1552,128]{1,0:T(8,128)}, u32[]{:S(2)}, u32[]{:S(2)}) collective-permute-start(f32[1552,128]{1,0:T(8,128)} %pad_maximum_fusion), channel_id=1, source_target_pairs={{0,1},{1,0},{2,3},{3,2},{4,5},{5,4},{6,7},{7,6},{8,9},{9,8},{10,11... | collective-permute-start | bytes 2383880 | tf_op jit(solution)/shard_map/ppermute | solution.py:36
  26.5 22.1 %collective-permute-start.2 = (f32[1552,128]{1,0:T(8,128)}, f32[1552,128]{1,0:T(8,128)}, u32[]{:S(2)}, u32[]{:S(2)}) collective-permute-start(f32[1552,128]{1,0:T(8,128)} %pad_maximum_fusion.1), channel_id=1, source_target_pairs={{0,2},{1,3},{2,4},{3,5},{4,6},{5,7},{6,8},{7,9},{8,10},{9,11},{10,... | collective-permute-start | bytes 2383880 | tf_op jit(solution)/shard_map/ppermute | solution.py:49
  49.7 11.2 %collective-permute-start.3 = (bf16[1552,128]{1,0:T(8,128)(2,1)S(1)}, bf16[1552,128]{1,0:T(8,128)(2,1)S(1)}, u32[]{:S(2)}, u32[]{:S(2)}) collective-permute-start(bf16[1552,128]{1,0:T(8,128)(2,1)S(1)} %convert_element_type.85), channel_id=1, source_target_pairs={{0,2},{1,3},{2,4},{3,5},{4,6},{5,7},{6,8},{7,9},{8,10},{9,11},{10,... | collective-permute-start | bytes 1191944 | tf_op jit(solution)/shard_map/ppermute | solution.py:51
  61.2 21.8 %collective-permute-start.4 = (bf16[24,64,128]{2,1,0:T(8,128)(2,1)S(1)}, bf16[24,64,128]{2,1,0:T(8,128)(2,1)S(1)}, u32[]{:S(2)}, u32[]{:S(2)}) collective-permute-start(bf16[24,64,128]{2,1,0:T(8,128)(2,1)S(1)} %fusion.50), channel_id=1, source_target_pairs={{0,4},{1,5},{2,6},{3,7},{4,8},{5,9},{6,10},{7,11},{8,12},{9,13},{1... | collective-permute-start | bytes 1179656 | tf_op jit(solution)/shard_map/ppermute | solution.py:54
  83.4 6.5 %collective-permute-start.5 = (bf16[24,64,128]{2,1,0:T(8,128)(2,1)S(1)}, bf16[24,64,128]{2,1,0:T(8,128)(2,1)S(1)}, u32[]{:S(2)}, u32[]{:S(2)}) collective-permute-start(bf16[24,64,128]{2,1,0:T(8,128)(2,1)S(1)} %get-tuple-element.23), channel_id=1, source_target_pairs={{0,1},{1,0},{2,3},{3,2},{4,5},{5,4},{6,7},{7,6},{8,9},{9,8},{10,11... | collective-permute-start | bytes 1179656 | tf_op jit(solution)/shard_map/ppermute | solution.py:57
  89.9 0.7 copy-start.3
  89.9 0.7 copy-start.6
  90.7 1.4 %copy-start.2 = (f32[48,64]{1,0:T(8,128)S(1)}, f32[48,64]{1,0:T(8,128)}, u32[]{:S(2)}) copy-start(f32[48,64]{1,0:T(8,128)} %mul.329) | copy-start | bytes 36868

commit v10 on v8

--- a/solution.py
+++ b/solution.py
@@ -22,21 +22,33 @@
     return (block[rows, :heads], block[:rows].reshape((heads,) + rest))
 
 
-def chain_carry(decay, local, held):
+def chain_carry(decay, scaled, bs, held):
     size, position = (lax.axis_size("ctx"), lax.axis_index("ctx"))
     chips = size // 2
     core = position % 2
     low = core == 0
     heads = decay.shape[0]
     half = heads // 2
-    rest = local.shape[1:]
+    rows = scaled.shape[0]
+    width = half * scaled.shape[2]
     swap = [(2 * i + j, 2 * i + 1 - j) for i in range(chips) for j in range(2)]
-    mine = lax.dynamic_slice_in_dim(local, core * half, half, 0)
-    theirs = lax.dynamic_slice_in_dim(local, (1 - core) * half, half, 0)
-    got = lax.ppermute(packed(decay, theirs), "ctx", swap)
-    rows = half * rest[0]
-    got_local = got[:rows].reshape((half,) + rest)
-    got_decay = got[rows:].reshape(-1)[:heads]
+    front, back = scaled[:, :half], scaled[:, half:]
+    mine_x = jnp.where(low, front, back)
+    theirs_x = jnp.where(low, back, front)
+    mine = jnp.einsum("shp,sn->hpn", mine_x, bs, preferred_element_type=jnp.float32)
+    rest = mine.shape[1:]
+    top = decay.astype(jnp.bfloat16)
+    middle = (decay - top.astype(jnp.float32)).astype(jnp.bfloat16)
+    bottom = (decay - top.astype(jnp.float32) - middle.astype(jnp.float32)).astype(jnp.bfloat16)
+    pieces = jnp.zeros((rows, bs.shape[1]), jnp.bfloat16).at[:3, :heads].set(jnp.stack([top, middle, bottom]))
+    got = lax.ppermute(
+        jnp.concatenate([theirs_x.reshape(rows, width), bs, pieces], axis=1), "ctx", swap
+    )
+    got_x = got[:, :width].reshape(scaled.shape[0], half, scaled.shape[2])
+    got_b = got[:, width : width + bs.shape[1]]
+    spare = got[:3, width + bs.shape[1] : width + bs.shape[1] + heads].astype(jnp.float32)
+    got_decay = (spare[0] + spare[1]) + spare[2]
+    got_local = jnp.einsum("shp,sn->hpn", got_x, got_b, preferred_element_type=jnp.float32)
     decay_hi = lax.dynamic_slice_in_dim(jnp.where(low, got_decay, decay), core * half, half, 0)
     decay_lo = lax.dynamic_slice_in_dim(jnp.where(low, decay, got_decay), core * half, half, 0)
     local_lo = jnp.where(low, mine, got_local)
@@ -94,9 +106,8 @@
     same_end = (seg == seg[-1]).astype(jnp.float32)
     factor = jnp.exp(cum[-1][None, :] - cum) * same_end[:, None] * step_size
     scaled = (factor[:, :, None] * xs.astype(jnp.float32)).astype(jnp.bfloat16)
-    local = jnp.einsum("shp,sn->hpn", scaled, bs, preferred_element_type=jnp.float32)
     block_decay = jnp.exp(cum[-1]) * alive[-1]
-    carry, (cum_late, step_late, seg_late) = chain_carry(block_decay, local, (cum, step_size, seg))
+    carry, (cum_late, step_late, seg_late) = chain_carry(block_decay, scaled, bs, (cum, step_size, seg))
     scores = jnp.dot(cs, bs.T, preferred_element_type=jnp.float32)
     index = jnp.arange(rows, dtype=jnp.int32)
     mask = (index[:, None] >= index[None, :]) & (seg_late[:, None] == seg_late[None, :])

time: 95 us -> 93.5 us (0.984)
  the two profiles are of different devices: /device:TPU:189 before, /device:TPU:185 now
where the time goes in v10:
time: 93.5 us; the launch traced here: 92.3 us
  starting transfers between devices  28 us (30%)
  waiting for transfers between devices  25.7 us (27%)
  local copies, waits for them, and re-layouts  21.6 us (23%)
  other arithmetic  10.7 us (11%)
  matrix products  5.86 us (6%)
    ppermute x1, waiting for transfers between devices, chain_carry(): lax.ppermute(local_ab.astype(jnp.bfloat16), 'ctx', two).astype(jnp.float32)  13.8 us
    ppermute x1, starting transfers between devices, chain_carry(): lax.ppermute(local_ab.astype(jnp.bfloat16), 'ctx', two).astype(jnp.float32)  7.46 us
    transpose x7, local copies, waits for them, and re-layouts, body(): step_late[:, part_start:part_start + group].T[:, None, :]  6.44 us
    ppermute x1, starting transfers between devices, chain_carry(): first_hop = lax.ppermute(sent, 'ctx', one)  5.33 us
    ppermute x1, waiting for transfers between devices, chain_carry(): first_hop = lax.ppermute(sent, 'ctx', one)  5.28 us
    ppermute x1, waiting for transfers between devices, chain_carry(): lax.ppermute(first_hop.astype(jnp.bfloat16), 'ctx', one).astype(jnp.float32)  5.25 us
    ppermute x1, starting transfers between devices, chain_carry(): got_end = lax.ppermute(jnp.where(low, onward, carry_half), 'ctx', swap)  4.64 us
    ppermute x1, starting transfers between devices, shifted(): return lax.ppermute(block, axis, route)  4.56 us
  transfers between devices with their start and end apart: 6, of which 5 were waited for; matrix products, arithmetic and copies ran while one was open for 27% of the time, Pallas kernels for 0%

profile of v10, /device:TPU:185, one launch (start us, length us, event | category | flops | bytes accessed | tf_op | source)
XLA Modules:
  0.0 92.3 jit_solution(14430386216620759135)
XLA Ops:
  0.0 1.0 %slice.173 = bf16[16,3328]{1,0:T(8,128)(2,1)S(1)} slice(bf16[128,3328]{1,0:T(8,128)(2,1)} %param.11), slice={[112:128], [0:3328]} | slice | bytes 212992 | tf_op jit(solution)/shard_map/slice | solution.py:92
  1.0 4.6 %collective-permute-start = (bf16[16,3328]{1,0:T(8,128)(2,1)S(1)}, bf16[16,3328]{1,0:T(8,128)(2,1)S(1)}, u32[]{:S(2)}, u32[]{:S(2)}) collective-permute-start(bf16[16,3328]{1,0:T(8,128)(2,1)S(1)} %slice.173), channel_id=1, source_target_pairs={{0,1},{1,2},{2,3},{3,4},{4,5},{5,6},{6,7},{7,8},{8,9},{9,10},{10,1... | collective-permute-start | bytes 319496 | tf_op jit(solution)/shard_map/ppermute | solution.py:10
  7.6 1.3 %compare_convert_fusion.1 = (f32[128]{0:T(128)S(1)}, f32[128]{0:T(128)S(1)}, pred[128]{0:T(512)(128)(4,1)S(1)}, pred[128]{0:T(512)(128)(4,1)S(1)}, pred[128]{0:T(512)(128)(4,1)S(1)}) fusion(s32[]{:T(128)} %bitcast.2, s32[144]{0:T(256)S(1)} %compare_select_fusion.1, s32[]{:T(128)} %bitcast.4), kind=kLoop, calls=%fused_computation.129 | loop fusion | flops 896 | bytes 3464 | tf_op jit(solution)/shard_map/convert_element_type | solution.py:106
  10.3 0.8 copy.67
  11.1 1.1 %slice_reduce_fusion.3 = (f32[3328]{0:T(1024)S(1)}, f32[3328]{0:T(1024)S(1)}, f32[3328]{0:T(1024)S(1)}, f32[3328]{0:T(1024)S(1)}) fusion(f32[4,3328]{1,0:T(4,128)} %param.14), kind=kLoop, calls=%fused_computation.123 | loop fusion | bytes 106496 | tf_op jit(solution)/shard_map/slice | solution.py:94
  14.1 1.6 %multiply_convert_fusion = bf16[128,3328]{1,0:T(8,128)(2,1)S(1)} fusion(bf16[128,3328]{1,0:T(8,128)(2,1)S(1)} %copy-done, bf16[144,3328]{1,0:T(8,128)(2,1)S(1)} %constant_dynamic-update-slice_fusion, f32[3328]{0:T(1024)S(1)} %get-tuple-element.27, f32[3328]{0:T(1024)S(1)} %get-tuple-element.28, f32[3328]{0:T(1024)S(1)} %get-tuple-element.26, ...), kind=kLoop, calls=%fused_computation.2 | loop fusion | flops 8519680 | bytes 4326784 | tf_op jit(solution)/shard_map/convert_element_type | solution.py:99
  17.5 1.9 %collective-permute-start.1 = (bf16[128,1792]{1,0:T(8,128)(2,1)S(1)}, bf16[128,1792]{1,0:T(8,128)(2,1)S(1)}, u32[]{:S(2)}, u32[]{:S(2)}) collective-permute-start(bf16[128,1792]{1,0:T(8,128)(2,1)S(1)} %pad_maximum_fusion.1), channel_id=1, source_target_pairs={{0,1},{1,0},{2,3},{3,2},{4,5},{5,4},{6,7},{7,6},{8,9},{9,8},{10,11... | collective-permute-start | bytes 1376264 | tf_op jit(solution)/shard_map/ppermute | solution.py:44
  22.0 0.9 copy.70
  22.9 1.3 %select_add_fusion = (f32[24,64,128]{2,1,0:T(8,128)S(1)}, f32[24,64,128]{2,1,0:T(8,128)S(1)}) fusion(f32[24,64,128]{2,1,0:T(8,128)S(1)} %fusion.12, f32[24]{0:T(128)S(1)} %get-tuple-element.33, pred[]{:T(512)S(6)} %eq.46, bf16[128,24,64]{0,2,1:T(8,128)(2,1)} %bitcast.111, bf16[128,1792]{1,0:T(8,128)(2,1)} %copy-done.3), kind=kOutput, calls=%fused_computation.28 | convolution fusion | flops 51118080 | bytes 2785377 | tf_op jit(solution)/shard_map/shp,sn->hpn/dot_general | solution.py:51
  24.2 0.9 %pad_maximum_fusion = f32[1544,128]{1,0:T(8,128)} fusion(f32[8,128]{1,0:T(8,128)S(1)} %pad_bitcast_fusion, f32[1536,128]{1,0:T(8,128)S(1)} %bitcast.109), kind=kLoop, calls=%fused_computation.19 | loop fusion | flops 197632 | bytes 1581056 | tf_op jit(solution)/shard_map/concatenate | solution.py:17
  25.1 5.3 %collective-permute-start.2 = (f32[1544,128]{1,0:T(8,128)}, f32[1544,128]{1,0:T(8,128)}, u32[]{:S(2)}, u32[]{:S(2)}) collective-permute-start(f32[1544,128]{1,0:T(8,128)} %pad_maximum_fusion), channel_id=1, source_target_pairs={{0,2},{1,3},{2,4},{3,5},{4,6},{5,7},{6,8},{7,9},{8,10},{9,11},{10,... | collective-permute-start | bytes 2371592 | tf_op jit(solution)/shard_map/ppermute | solution.py:61
  30.4 1.0 %slice_bitcast_fusion = (f32[8,128]{0,1:T(8,128)}, f32[8,128]{0,1:T(8,128)}, f32[8,128]{0,1:T(8,128)}, f32[8,128]{0,1:T(8,128)}, f32[8,128]{0,1:T(8,128)}, /*ind...) fusion(f32[128,48]{1,0:T(8,128)S(1)} %get-tuple-element.23, ...), kind=kLoop, calls=%fused_computation.89 | loop fusion | bytes 98304 | tf_op jit(solution)/shard_map/transpose | solution.py:121
  31.4 0.9 copy.88
  32.3 0.9 copy.85
  33.3 0.9 copy.82
  34.2 0.9 copy.79
  35.1 0.9 copy.76
  36.0 0.9 copy.73
  36.9 0.9 copy.71
  37.8 0.9 copy.74
  38.7 0.9 copy.77
  39.6 0.9 copy.80
  40.8 1.2 %fusion.7 = f32[128,48,64]{0,2,1:T(8,128)S(1)} fusion(bf16[128,48,64]{0,2,1:T(8,128)(2,1)S(1)} %bitcast.98, f32[8,128]{1,0:T(8,128)S(1)} %copy.73, f32[8,128]{1,0:T(8,128)S(1)} %copy.71, f32[128,128]{1,0:T(8,128)} %fusion.68, pred[128,128]{1,0:T(8,128)(4,1)S(1)} %fusion.58), kind=kOutput, calls=%fused_computation.18 | convolution fusion | flops 17563648 | bytes 1142784 | tf_op jit(solution)/shard_map/hts,shp->thp/dot_general | solution.py:124
  42.3 5.3 %collective-permute-done.2 = f32[1544,128]{1,0:T(8,128)} collective-permute-done((f32[1544,128]{1,0:T(8,128)}, f32[1544,128]{1,0:T(8,128)}, u32[]{:S(2)}, u32[]{:S(2)}) %collective-permute-start.2) | collective-permute-done | bytes 790560 | tf_op jit(solution)/shard_map/ppermute | solution.py:61
  47.6 1.2 %convert_element_type.117 = bf16[1544,128]{1,0:T(8,128)(2,1)S(1)} convert(f32[1544,128]{1,0:T(8,128)} %collective-permute-done.2) | non-fusion elementwise | flops 197632 | bytes 1185792 | tf_op jit(solution)/shard_map/convert_element_type | solution.py:63
  48.8 4.1 %collective-permute-start.3 = (bf16[1544,128]{1,0:T(8,128)(2,1)S(1)}, bf16[1544,128]{1,0:T(8,128)(2,1)S(1)}, u32[]{:S(2)}, u32[]{:S(2)}) collective-permute-start(bf16[1544,128]{1,0:T(8,128)(2,1)S(1)} %convert_element_type.117), channel_id=1, source_target_pairs={{0,2},{1,3},{2,4},{3,5},{4,6},{5,7},{6,8},{7,9},{8,10},{9,11},{10,... | collective-permute-start | bytes 1185800 | tf_op jit(solution)/shard_map/ppermute | solution.py:63
  53.3 1.2 %slice.233 = f32[1536,128]{1,0:T(8,128)S(1)} slice(f32[1544,128]{1,0:T(8,128)} %collective-permute-done.2), slice={[0:1536], [0:128]} | slice | bytes 1572864 | tf_op jit(solution)/shard_map/slice | solution.py:22
  55.2 5.3 %collective-permute-done.3 = bf16[1544,128]{1,0:T(8,128)(2,1)S(1)} collective-permute-done((bf16[1544,128]{1,0:T(8,128)(2,1)S(1)}, bf16[1544,128]{1,0:T(8,128)(2,1)S(1)}, u32[]{:S(2)}, u32[]{:S(2)}) %collective-permute-start.3) | collective-permute-done | bytes 395296 | tf_op jit(solution)/shard_map/ppermute | solution.py:63
  60.6 7.5 %collective-permute-start.4 = (bf16[24,64,128]{2,1,0:T(8,128)(2,1)S(1)}, bf16[24,64,128]{2,1,0:T(8,128)(2,1)S(1)}, u32[]{:S(2)}, u32[]{:S(2)}) collective-permute-start(bf16[24,64,128]{2,1,0:T(8,128)(2,1)S(1)} %fusion.53), channel_id=1, source_target_pairs={{0,4},{1,5},{2,6},{3,7},{4,8},{5,9},{6,10},{7,11},{8,12},{9,13},{1... | collective-permute-start | bytes 1179656 | tf_op jit(solution)/shard_map/ppermute | solution.py:66
  69.2 13.8 %collective-permute-done.4 = bf16[24,64,128]{2,1,0:T(8,128)(2,1)S(1)} collective-permute-done((bf16[24,64,128]{2,1,0:T(8,128)(2,1)S(1)}, bf16[24,64,128]{2,1,0:T(8,128)(2,1)S(1)}, u32[]{:S(2)}, u32[]{:S(2)}) %collective-permute-start.4) | collective-permute-done | bytes 393248 | tf_op jit(solution)/shard_map/ppermute | solution.py:66
  83.4 4.6 %collective-permute-start.5 = (bf16[24,64,128]{2,1,0:T(8,128)(2,1)S(1)}, bf16[24,64,128]{2,1,0:T(8,128)(2,1)S(1)}, u32[]{:S(2)}, u32[]{:S(2)}) collective-permute-start(bf16[24,64,128]{2,1,0:T(8,128)(2,1)S(1)} %get-tuple-element.29), channel_id=1, source_target_pairs={{0,1},{1,0},{2,3},{3,2},{4,5},{5,4},{6,7},{7,6},{8,9},{9,8},{10,11... | collective-permute-start | bytes 1179656 | tf_op jit(solution)/shard_map/ppermute | solution.py:69
  91.2 1.2 %copy.90 = bf16[128,3072]{1,0:T(8,128)(2,1)} copy(bf16[128,3072]{0,1:T(8,128)(2,1)S(1)} %bitcast.110) | data formatting | bytes 1572864 | tf_op jit(solution)/shard_map/reshape | solution.py:144
  (69 shorter events, 15.9 us)
Async XLA Ops:
  0.0 14.1 %copy-start = (bf16[128,3328]{1,0:T(8,128)(2,1)S(1)}, bf16[128,3328]{1,0:T(8,128)(2,1)}, u32[]{:S(2)}) copy-start(bf16[128,3328]{1,0:T(8,128)(2,1)} %param.11) | copy-start | bytes 2555908
  1.0 13.2 %copy-start.5 = (f32[3328]{0:T(1024)S(1)}, f32[3328]{0:T(1024)}, u32[]{:S(2)}) copy-start(f32[3328]{0:T(1024)} %param.15) | copy-start | bytes 39940
  1.0 13.1 %collective-permute-start = (bf16[16,3328]{1,0:T(8,128)(2,1)S(1)}, bf16[16,3328]{1,0:T(8,128)(2,1)S(1)}, u32[]{:S(2)}, u32[]{:S(2)}) collective-permute-start(bf16[16,3328]{1,0:T(8,128)(2,1)S(1)} %slice.173), channel_id=1, source_target_pairs={{0,1},{1,2},{2,3},{3,4},{4,5},{5,6},{6,7},{7,8},{8,9},{9,10},{10,1... | collective-permute-start | bytes 319496 | tf_op jit(solution)/shard_map/ppermute | solution.py:10
  15.8 0.9 copy-start.1
  16.7 0.8 slice-start
  16.9 2.5 %copy-start.2 = (bf16[128,3328]{1,0:T(8,128)(2,1)S(1)}, bf16[128,3328]{1,0:T(8,128)(2,1)}, u32[]{:S(2)}) copy-start(bf16[128,3328]{1,0:T(8,128)(2,1)} %copy-done.1) | copy-start | bytes 2555908
  17.5 3.7 %collective-permute-start.1 = (bf16[128,1792]{1,0:T(8,128)(2,1)S(1)}, bf16[128,1792]{1,0:T(8,128)(2,1)S(1)}, u32[]{:S(2)}, u32[]{:S(2)}) collective-permute-start(bf16[128,1792]{1,0:T(8,128)(2,1)S(1)} %pad_maximum_fusion.1), channel_id=1, source_target_pairs={{0,1},{1,0},{2,3},{3,2},{4,5},{5,4},{6,7},{7,6},{8,9},{9,8},{10,11... | collective-permute-start | bytes 1376264 | tf_op jit(solution)/shard_map/ppermute | solution.py:44
  21.2 0.8 copy-start.3
  25.1 15.5 %copy-start.6 = (s32[128]{0:T(128)S(1)}, s32[128]{0:T(128)}, u32[]{:S(2)}) copy-start(s32[128]{0:T(128)} %slice.172) | copy-start | bytes 1540
  25.1 22.5 %collective-permute-start.2 = (f32[1544,128]{1,0:T(8,128)}, f32[1544,128]{1,0:T(8,128)}, u32[]{:S(2)}, u32[]{:S(2)}) collective-permute-start(f32[1544,128]{1,0:T(8,128)} %pad_maximum_fusion), channel_id=1, source_target_pairs={{0,2},{1,3},{2,4},{3,5},{4,6},{5,7},{6,8},{7,9},{8,10},{9,11},{10,... | collective-permute-start | bytes 2371592 | tf_op jit(solution)/shard_map/ppermute | solution.py:61
  31.4 10.5 %copy-start.4 = (f32[128,128]{1,0:T(8,128)S(1)}, f32[128,128]{1,0:T(8,128)}, u32[]{:S(2)}) copy-start(f32[128,128]{1,0:T(8,128)} %fusion.68) | copy-start | bytes 196612
  48.8 11.6 %collective-permute-start.3 = (bf16[1544,128]{1,0:T(8,128)(2,1)S(1)}, bf16[1544,128]{1,0:T(8,128)(2,1)S(1)}, u32[]{:S(2)}, u32[]{:S(2)}) collective-permute-start(bf16[1544,128]{1,0:T(8,128)(2,1)S(1)} %convert_element_type.117), channel_id=1, source_target_pairs={{0,2},{1,3},{2,4},{3,5},{4,6},{5,7},{6,8},{7,9},{8,10},{9,11},{10,... | collective-permute-start | bytes 1185800 | tf_op jit(solution)/shard_map/ppermute | solution.py:63
  60.6 22.4 %collective-permute-start.4 = (bf16[24,64,128]{2,1,0:T(8,128)(2,1)S(1)}, bf16[24,64,128]{2,1,0:T(8,128)(2,1)S(1)}, u32[]{:S(2)}, u32[]{:S(2)}) collective-permute-start(bf16[24,64,128]{2,1,0:T(8,128)(2,1)S(1)} %fusion.53), channel_id=1, source_target_pairs={{0,4},{1,5},{2,6},{3,7},{4,8},{5,9},{6,10},{7,11},{8,12},{9,13},{1... | collective-permute-start | bytes 1179656 | tf_op jit(solution)/shard_map/ppermute | solution.py:66
  83.4 6.0 %collective-permute-start.5 = (bf16[24,64,128]{2,1,0:T(8,128)(2,1)S(1)}, bf16[24,64,128]{2,1,0:T(8,128)(2,1)S(1)}, u32[]{:S(2)}, u32[]{:S(2)}) collective-permute-start(bf16[24,64,128]{2,1,0:T(8,128)(2,1)S(1)} %get-tuple-element.29), channel_id=1, source_target_pairs={{0,1},{1,0},{2,3},{3,2},{4,5},{5,4},{6,7},{7,6},{8,9},{9,8},{10,11... | collective-permute-start | bytes 1179656 | tf_op jit(solution)/shard_map/ppermute | solution.py:69
  89.4 0.7 copy-start.7

commit v11 on v10

--- a/solution.py
+++ b/solution.py
@@ -37,10 +37,11 @@
     theirs_x = jnp.where(low, back, front)
     mine = jnp.einsum("shp,sn->hpn", mine_x, bs, preferred_element_type=jnp.float32)
     rest = mine.shape[1:]
-    top = decay.astype(jnp.bfloat16)
-    middle = (decay - top.astype(jnp.float32)).astype(jnp.bfloat16)
-    bottom = (decay - top.astype(jnp.float32) - middle.astype(jnp.float32)).astype(jnp.bfloat16)
-    pieces = jnp.zeros((rows, bs.shape[1]), jnp.bfloat16).at[:3, :heads].set(jnp.stack([top, middle, bottom]))
+    top = lax.reduce_precision(decay, exponent_bits=8, mantissa_bits=7)
+    middle = lax.reduce_precision(decay - top, exponent_bits=8, mantissa_bits=7)
+    bottom = lax.reduce_precision(decay - top - middle, exponent_bits=8, mantissa_bits=7)
+    split = jnp.stack([top, middle, bottom]).astype(jnp.bfloat16)
+    pieces = jnp.zeros((rows, bs.shape[1]), jnp.bfloat16).at[:3, :heads].set(split)
     got = lax.ppermute(
         jnp.concatenate([theirs_x.reshape(rows, width), bs, pieces], axis=1), "ctx", swap
     )

time: 93.5 us -> 93.8 us (level)
  the two profiles are of different devices: /device:TPU:185 before, /device:TPU:191 now
where the time goes in v11:
time: 93.8 us; the launch traced here: 92.5 us
  starting transfers between devices  28 us (30%)
  waiting for transfers between devices  25.7 us (27%)
  local copies, waits for them, and re-layouts  21.8 us (23%)
  other arithmetic  10.8 us (12%)
  matrix products  5.86 us (6%)
    ppermute x1, waiting for transfers between devices, chain_carry(): lax.ppermute(local_ab.astype(jnp.bfloat16), 'ctx', two).astype(jnp.float32)  13.8 us
    ppermute x1, starting transfers between devices, chain_carry(): lax.ppermute(local_ab.astype(jnp.bfloat16), 'ctx', two).astype(jnp.float32)  7.46 us
    transpose x7, local copies, waits for them, and re-layouts, body(): step_late[:, part_start:part_start + group].T[:, None, :]  6.44 us
    ppermute x1, starting transfers between devices, chain_carry(): first_hop = lax.ppermute(sent, 'ctx', one)  5.33 us
    ppermute x1, waiting for transfers between devices, chain_carry(): first_hop = lax.ppermute(sent, 'ctx', one)  5.27 us
    ppermute x1, waiting for transfers between devices, chain_carry(): lax.ppermute(first_hop.astype(jnp.bfloat16), 'ctx', one).astype(jnp.float32)  5.25 us
    ppermute x1, starting transfers between devices, chain_carry(): got_end = lax.ppermute(jnp.where(low, onward, carry_half), 'ctx', swap)  4.64 us
    ppermute x1, starting transfers between devices, shifted(): return lax.ppermute(block, axis, route)  4.56 us
  transfers between devices with their start and end apart: 6, of which 5 were waited for; matrix products, arithmetic and copies ran while one was open for 28% of the time, Pallas kernels for 0%

profile of v11, /device:TPU:191, one launch (start us, length us, event | category | flops | bytes accessed | tf_op | source)
XLA Modules:
  0.0 92.5 jit_solution(14420179020962484105)
XLA Ops:
  0.0 1.0 %slice.173 = bf16[16,3328]{1,0:T(8,128)(2,1)S(1)} slice(bf16[128,3328]{1,0:T(8,128)(2,1)} %param.11), slice={[112:128], [0:3328]} | slice | bytes 212992 | tf_op jit(solution)/shard_map/slice | solution.py:93
  1.0 4.6 %collective-permute-start = (bf16[16,3328]{1,0:T(8,128)(2,1)S(1)}, bf16[16,3328]{1,0:T(8,128)(2,1)S(1)}, u32[]{:S(2)}, u32[]{:S(2)}) collective-permute-start(bf16[16,3328]{1,0:T(8,128)(2,1)S(1)} %slice.173), channel_id=1, source_target_pairs={{0,1},{1,2},{2,3},{3,4},{4,5},{5,6},{6,7},{7,8},{8,9},{9,10},{10,1... | collective-permute-start | bytes 319496 | tf_op jit(solution)/shard_map/ppermute | solution.py:10
  7.7 1.4 %compare_convert_fusion.1 = (f32[128]{0:T(128)S(1)}, f32[128]{0:T(128)S(1)}, pred[128]{0:T(512)(128)(4,1)S(1)}, pred[128]{0:T(512)(128)(4,1)S(1)}, pred[128]{0:T(512)(128)(4,1)S(1)}) fusion(s32[]{:T(128)} %bitcast.2, s32[144]{0:T(256)S(1)} %compare_select_fusion.1, s32[]{:T(128)} %bitcast.4), kind=kLoop, calls=%fused_computation.129 | loop fusion | flops 896 | bytes 3464 | tf_op jit(solution)/shard_map/convert_element_type | solution.py:107
  10.5 0.8 copy.67
  11.3 1.1 %slice_reduce_fusion.3 = (f32[3328]{0:T(1024)S(1)}, f32[3328]{0:T(1024)S(1)}, f32[3328]{0:T(1024)S(1)}, f32[3328]{0:T(1024)S(1)}) fusion(f32[4,3328]{1,0:T(4,128)} %param.14), kind=kLoop, calls=%fused_computation.123 | loop fusion | bytes 106496 | tf_op jit(solution)/shard_map/slice | solution.py:95
  14.4 1.6 %multiply_convert_fusion = bf16[128,3328]{1,0:T(8,128)(2,1)S(1)} fusion(bf16[128,3328]{1,0:T(8,128)(2,1)S(1)} %copy-done, bf16[144,3328]{1,0:T(8,128)(2,1)S(1)} %constant_dynamic-update-slice_fusion, f32[3328]{0:T(1024)S(1)} %get-tuple-element.27, f32[3328]{0:T(1024)S(1)} %get-tuple-element.28, f32[3328]{0:T(1024)S(1)} %get-tuple-element.26, ...), kind=kLoop, calls=%fused_computation.2 | loop fusion | flops 8519680 | bytes 4326784 | tf_op jit(solution)/shard_map/convert_element_type | solution.py:100
  17.7 1.9 %collective-permute-start.1 = (bf16[128,1792]{1,0:T(8,128)(2,1)S(1)}, bf16[128,1792]{1,0:T(8,128)(2,1)S(1)}, u32[]{:S(2)}, u32[]{:S(2)}) collective-permute-start(bf16[128,1792]{1,0:T(8,128)(2,1)S(1)} %pad_maximum_fusion.1), channel_id=1, source_target_pairs={{0,1},{1,0},{2,3},{3,2},{4,5},{5,4},{6,7},{7,6},{8,9},{9,8},{10,11... | collective-permute-start | bytes 1376264 | tf_op jit(solution)/shard_map/ppermute | solution.py:45
  22.2 0.9 %copy.70 = bf16[128,1536]{0,1:T(8,128)(2,1)} copy(bf16[128,1536]{1,0:T(8,128)(2,1)S(1)} %slice.228) | data formatting | bytes 786432 | tf_op jit(solution)/shard_map/slice | solution.py:48
  23.1 1.3 %select_add_fusion = (f32[24,64,128]{2,1,0:T(8,128)S(1)}, f32[24,64,128]{2,1,0:T(8,128)S(1)}) fusion(f32[24,64,128]{2,1,0:T(8,128)S(1)} %fusion.12, f32[24]{0:T(128)S(1)} %get-tuple-element.33, pred[]{:T(512)S(6)} %eq.46, bf16[128,24,64]{0,2,1:T(8,128)(2,1)} %bitcast.111, bf16[128,1792]{1,0:T(8,128)(2,1)} %copy-done.3), kind=kOutput, calls=%fused_computation.28 | convolution fusion | flops 51118080 | bytes 2785377 | tf_op jit(solution)/shard_map/shp,sn->hpn/dot_general | solution.py:52
  24.4 0.9 %pad_maximum_fusion = f32[1544,128]{1,0:T(8,128)} fusion(f32[8,128]{1,0:T(8,128)S(1)} %pad_bitcast_fusion, f32[1536,128]{1,0:T(8,128)S(1)} %bitcast.109), kind=kLoop, calls=%fused_computation.19 | loop fusion | flops 197632 | bytes 1581056 | tf_op jit(solution)/shard_map/concatenate | solution.py:17
  25.3 5.3 %collective-permute-start.2 = (f32[1544,128]{1,0:T(8,128)}, f32[1544,128]{1,0:T(8,128)}, u32[]{:S(2)}, u32[]{:S(2)}) collective-permute-start(f32[1544,128]{1,0:T(8,128)} %pad_maximum_fusion), channel_id=1, source_target_pairs={{0,2},{1,3},{2,4},{3,5},{4,6},{5,7},{6,8},{7,9},{8,10},{9,11},{10,... | collective-permute-start | bytes 2371592 | tf_op jit(solution)/shard_map/ppermute | solution.py:62
  30.7 1.0 %slice_bitcast_fusion = (f32[8,128]{0,1:T(8,128)}, f32[8,128]{0,1:T(8,128)}, f32[8,128]{0,1:T(8,128)}, f32[8,128]{0,1:T(8,128)}, f32[8,128]{0,1:T(8,128)}, /*ind...) fusion(f32[128,48]{1,0:T(8,128)S(1)} %get-tuple-element.23, ...), kind=kLoop, calls=%fused_computation.89 | loop fusion | bytes 98304 | tf_op jit(solution)/shard_map/transpose | solution.py:122
  31.7 0.9 copy.88
  32.6 0.9 copy.85
  33.5 0.9 copy.82
  34.4 0.9 copy.79
  35.3 0.9 copy.76
  36.2 0.9 copy.73
  37.1 0.9 copy.71
  38.0 0.9 copy.74
  38.9 0.9 copy.77
  39.8 0.9 copy.80
  41.0 1.2 %fusion.7 = f32[128,48,64]{0,2,1:T(8,128)S(1)} fusion(bf16[128,48,64]{0,2,1:T(8,128)(2,1)S(1)} %bitcast.98, f32[8,128]{1,0:T(8,128)S(1)} %copy.73, f32[8,128]{1,0:T(8,128)S(1)} %copy.71, f32[128,128]{1,0:T(8,128)} %fusion.68, pred[128,128]{1,0:T(8,128)(4,1)S(1)} %fusion.58), kind=kOutput, calls=%fused_computation.18 | convolution fusion | flops 17563648 | bytes 1142784 | tf_op jit(solution)/shard_map/hts,shp->thp/dot_general | solution.py:125
  42.6 5.3 %collective-permute-done.2 = f32[1544,128]{1,0:T(8,128)} collective-permute-done((f32[1544,128]{1,0:T(8,128)}, f32[1544,128]{1,0:T(8,128)}, u32[]{:S(2)}, u32[]{:S(2)}) %collective-permute-start.2) | collective-permute-done | bytes 790560 | tf_op jit(solution)/shard_map/ppermute | solution.py:62
  47.9 1.2 %convert_element_type.88 = bf16[1544,128]{1,0:T(8,128)(2,1)S(1)} convert(f32[1544,128]{1,0:T(8,128)} %collective-permute-done.2) | non-fusion elementwise | flops 197632 | bytes 1185792 | tf_op jit(solution)/shard_map/convert_element_type | solution.py:64
  49.0 4.1 %collective-permute-start.3 = (bf16[1544,128]{1,0:T(8,128)(2,1)S(1)}, bf16[1544,128]{1,0:T(8,128)(2,1)S(1)}, u32[]{:S(2)}, u32[]{:S(2)}) collective-permute-start(bf16[1544,128]{1,0:T(8,128)(2,1)S(1)} %convert_element_type.88), channel_id=1, source_target_pairs={{0,2},{1,3},{2,4},{3,5},{4,6},{5,7},{6,8},{7,9},{8,10},{9,11},{10,... | collective-permute-start | bytes 1185800 | tf_op jit(solution)/shard_map/ppermute | solution.py:64
  53.5 1.2 %slice.233 = f32[1536,128]{1,0:T(8,128)S(1)} slice(f32[1544,128]{1,0:T(8,128)} %collective-permute-done.2), slice={[0:1536], [0:128]} | slice | bytes 1572864 | tf_op jit(solution)/shard_map/slice | solution.py:22
  55.4 5.3 %collective-permute-done.3 = bf16[1544,128]{1,0:T(8,128)(2,1)S(1)} collective-permute-done((bf16[1544,128]{1,0:T(8,128)(2,1)S(1)}, bf16[1544,128]{1,0:T(8,128)(2,1)S(1)}, u32[]{:S(2)}, u32[]{:S(2)}) %collective-permute-start.3) | collective-permute-done | bytes 395296 | tf_op jit(solution)/shard_map/ppermute | solution.py:64
  60.9 7.5 %collective-permute-start.4 = (bf16[24,64,128]{2,1,0:T(8,128)(2,1)S(1)}, bf16[24,64,128]{2,1,0:T(8,128)(2,1)S(1)}, u32[]{:S(2)}, u32[]{:S(2)}) collective-permute-start(bf16[24,64,128]{2,1,0:T(8,128)(2,1)S(1)} %fusion.53), channel_id=1, source_target_pairs={{0,4},{1,5},{2,6},{3,7},{4,8},{5,9},{6,10},{7,11},{8,12},{9,13},{1... | collective-permute-start | bytes 1179656 | tf_op jit(solution)/shard_map/ppermute | solution.py:67
  69.4 13.8 %collective-permute-done.4 = bf16[24,64,128]{2,1,0:T(8,128)(2,1)S(1)} collective-permute-done((bf16[24,64,128]{2,1,0:T(8,128)(2,1)S(1)}, bf16[24,64,128]{2,1,0:T(8,128)(2,1)S(1)}, u32[]{:S(2)}, u32[]{:S(2)}) %collective-permute-start.4) | collective-permute-done | bytes 393248 | tf_op jit(solution)/shard_map/ppermute | solution.py:67
  83.6 4.6 %collective-permute-start.5 = (bf16[24,64,128]{2,1,0:T(8,128)(2,1)S(1)}, bf16[24,64,128]{2,1,0:T(8,128)(2,1)S(1)}, u32[]{:S(2)}, u32[]{:S(2)}) collective-permute-start(bf16[24,64,128]{2,1,0:T(8,128)(2,1)S(1)} %get-tuple-element.29), channel_id=1, source_target_pairs={{0,1},{1,0},{2,3},{3,2},{4,5},{5,4},{6,7},{7,6},{8,9},{9,8},{10,11... | collective-permute-start | bytes 1179656 | tf_op jit(solution)/shard_map/ppermute | solution.py:70
  91.4 1.2 %copy.90 = bf16[128,3072]{1,0:T(8,128)(2,1)} copy(bf16[128,3072]{0,1:T(8,128)(2,1)S(1)} %bitcast.110) | data formatting | bytes 1572864 | tf_op jit(solution)/shard_map/reshape | solution.py:145
  (70 shorter events, 16.0 us)
Async XLA Ops:
  0.0 14.3 %copy-start = (bf16[128,3328]{1,0:T(8,128)(2,1)S(1)}, bf16[128,3328]{1,0:T(8,128)(2,1)}, u32[]{:S(2)}) copy-start(bf16[128,3328]{1,0:T(8,128)(2,1)} %param.11) | copy-start | bytes 2555908
  1.0 13.4 %copy-start.5 = (f32[3328]{0:T(1024)S(1)}, f32[3328]{0:T(1024)}, u32[]{:S(2)}) copy-start(f32[3328]{0:T(1024)} %param.15) | copy-start | bytes 39940
  1.0 13.3 %collective-permute-start = (bf16[16,3328]{1,0:T(8,128)(2,1)S(1)}, bf16[16,3328]{1,0:T(8,128)(2,1)S(1)}, u32[]{:S(2)}, u32[]{:S(2)}) collective-permute-start(bf16[16,3328]{1,0:T(8,128)(2,1)S(1)} %slice.173), channel_id=1, source_target_pairs={{0,1},{1,2},{2,3},{3,4},{4,5},{5,6},{6,7},{7,8},{8,9},{9,10},{10,1... | collective-permute-start | bytes 319496 | tf_op jit(solution)/shard_map/ppermute | solution.py:10
  16.0 0.9 copy-start.1
  16.9 0.8 slice-start
  17.1 2.5 %copy-start.2 = (bf16[128,3328]{1,0:T(8,128)(2,1)S(1)}, bf16[128,3328]{1,0:T(8,128)(2,1)}, u32[]{:S(2)}) copy-start(bf16[128,3328]{1,0:T(8,128)(2,1)} %copy-done.1) | copy-start | bytes 2555908
  17.7 3.7 %collective-permute-start.1 = (bf16[128,1792]{1,0:T(8,128)(2,1)S(1)}, bf16[128,1792]{1,0:T(8,128)(2,1)S(1)}, u32[]{:S(2)}, u32[]{:S(2)}) collective-permute-start(bf16[128,1792]{1,0:T(8,128)(2,1)S(1)} %pad_maximum_fusion.1), channel_id=1, source_target_pairs={{0,1},{1,0},{2,3},{3,2},{4,5},{5,4},{6,7},{7,6},{8,9},{9,8},{10,11... | collective-permute-start | bytes 1376264 | tf_op jit(solution)/shard_map/ppermute | solution.py:45
  21.4 0.8 copy-start.3
  25.3 15.6 %copy-start.6 = (s32[128]{0:T(128)S(1)}, s32[128]{0:T(128)}, u32[]{:S(2)}) copy-start(s32[128]{0:T(128)} %slice.172) | copy-start | bytes 1540
  25.3 22.5 %collective-permute-start.2 = (f32[1544,128]{1,0:T(8,128)}, f32[1544,128]{1,0:T(8,128)}, u32[]{:S(2)}, u32[]{:S(2)}) collective-permute-start(f32[1544,128]{1,0:T(8,128)} %pad_maximum_fusion), channel_id=1, source_target_pairs={{0,2},{1,3},{2,4},{3,5},{4,6},{5,7},{6,8},{7,9},{8,10},{9,11},{10,... | collective-permute-start | bytes 2371592 | tf_op jit(solution)/shard_map/ppermute | solution.py:62
  31.7 10.5 %copy-start.4 = (f32[128,128]{1,0:T(8,128)S(1)}, f32[128,128]{1,0:T(8,128)}, u32[]{:S(2)}) copy-start(f32[128,128]{1,0:T(8,128)} %fusion.68) | copy-start | bytes 196612
  49.0 11.6 %collective-permute-start.3 = (bf16[1544,128]{1,0:T(8,128)(2,1)S(1)}, bf16[1544,128]{1,0:T(8,128)(2,1)S(1)}, u32[]{:S(2)}, u32[]{:S(2)}) collective-permute-start(bf16[1544,128]{1,0:T(8,128)(2,1)S(1)} %convert_element_type.88), channel_id=1, source_target_pairs={{0,2},{1,3},{2,4},{3,5},{4,6},{5,7},{6,8},{7,9},{8,10},{9,11},{10,... | collective-permute-start | bytes 1185800 | tf_op jit(solution)/shard_map/ppermute | solution.py:64
  60.9 22.4 %collective-permute-start.4 = (bf16[24,64,128]{2,1,0:T(8,128)(2,1)S(1)}, bf16[24,64,128]{2,1,0:T(8,128)(2,1)S(1)}, u32[]{:S(2)}, u32[]{:S(2)}) collective-permute-start(bf16[24,64,128]{2,1,0:T(8,128)(2,1)S(1)} %fusion.53), channel_id=1, source_target_pairs={{0,4},{1,5},{2,6},{3,7},{4,8},{5,9},{6,10},{7,11},{8,12},{9,13},{1... | collective-permute-start | bytes 1179656 | tf_op jit(solution)/shard_map/ppermute | solution.py:67
  83.6 6.0 %collective-permute-start.5 = (bf16[24,64,128]{2,1,0:T(8,128)(2,1)S(1)}, bf16[24,64,128]{2,1,0:T(8,128)(2,1)S(1)}, u32[]{:S(2)}, u32[]{:S(2)}) collective-permute-start(bf16[24,64,128]{2,1,0:T(8,128)(2,1)S(1)} %get-tuple-element.29), channel_id=1, source_target_pairs={{0,1},{1,0},{2,3},{3,2},{4,5},{5,4},{6,7},{7,6},{8,9},{9,8},{10,11... | collective-permute-start | bytes 1179656 | tf_op jit(solution)/shard_map/ppermute | solution.py:70
  89.6 0.7 copy-start.7

commit v12 on v11

--- a/solution.py
+++ b/solution.py
@@ -45,11 +45,13 @@
     got = lax.ppermute(
         jnp.concatenate([theirs_x.reshape(rows, width), bs, pieces], axis=1), "ctx", swap
     )
-    got_x = got[:, :width].reshape(scaled.shape[0], half, scaled.shape[2])
+    got_x = got[:, :width]
     got_b = got[:, width : width + bs.shape[1]]
     spare = got[:3, width + bs.shape[1] : width + bs.shape[1] + heads].astype(jnp.float32)
     got_decay = (spare[0] + spare[1]) + spare[2]
-    got_local = jnp.einsum("shp,sn->hpn", got_x, got_b, preferred_element_type=jnp.float32)
+    got_local = jnp.einsum("sk,sn->kn", got_x, got_b, preferred_element_type=jnp.float32).reshape(
+        (half,) + rest
+    )
     decay_hi = lax.dynamic_slice_in_dim(jnp.where(low, got_decay, decay), core * half, half, 0)
     decay_lo = lax.dynamic_slice_in_dim(jnp.where(low, decay, got_decay), core * half, half, 0)
     local_lo = jnp.where(low, mine, got_local)

time: 93.8 us -> 91.2 us (0.972)
  the two profiles are of different devices: /device:TPU:191 before, /device:TPU:183 now
where the time goes in v12:
time: 91.2 us; the launch traced here: 90.1 us
  starting transfers between devices  28.2 us (31%)
  waiting for transfers between devices  27.9 us (31%)
  local copies, waits for them, and re-layouts  17.4 us (19%)
  other arithmetic  9.02 us (10%)
  matrix products  7.21 us (8%)
    ppermute x1, waiting for transfers between devices, chain_carry(): lax.ppermute(local_ab.astype(jnp.bfloat16), 'ctx', two).astype(jnp.float32)  14 us
    ppermute x1, starting transfers between devices, chain_carry(): lax.ppermute(local_ab.astype(jnp.bfloat16), 'ctx', two).astype(jnp.float32)  7.34 us
    ppermute x1, waiting for transfers between devices, chain_carry(): lax.ppermute(first_hop.astype(jnp.bfloat16), 'ctx', one).astype(jnp.float32)  6.76 us
    ppermute x1, waiting for transfers between devices, chain_carry(): first_hop = lax.ppermute(sent, 'ctx', one)  6.62 us
    transpose x7, local copies, waits for them, and re-layouts, body(): step_late[:, part_start:part_start + group].T[:, None, :]  6.39 us
    ppermute x1, starting transfers between devices, chain_carry(): first_hop = lax.ppermute(sent, 'ctx', one)  5.2 us
    ppermute x1, starting transfers between devices, chain_carry(): got_end = lax.ppermute(jnp.where(low, onward, carry_half), 'ctx', swap)  5.19 us
    ppermute x1, starting transfers between devices, shifted(): return lax.ppermute(block, axis, route)  4.55 us
  transfers between devices with their start and end apart: 6, of which 4 were waited for; matrix products, arithmetic and copies ran while one was open for 24% of the time, Pallas kernels for 0%

profile of v12, /device:TPU:183, one launch (start us, length us, event | category | flops | bytes accessed | tf_op | source)
XLA Modules:
  0.0 90.1 jit_solution(15676625355420878137)
XLA Ops:
  0.0 1.0 %slice.173 = bf16[16,3328]{1,0:T(8,128)(2,1)S(1)} slice(bf16[128,3328]{1,0:T(8,128)(2,1)} %param.11), slice={[112:128], [0:3328]} | slice | bytes 212992 | tf_op jit(solution)/shard_map/slice | solution.py:95
  1.0 4.5 %collective-permute-start = (bf16[16,3328]{1,0:T(8,128)(2,1)S(1)}, bf16[16,3328]{1,0:T(8,128)(2,1)S(1)}, u32[]{:S(2)}, u32[]{:S(2)}) collective-permute-start(bf16[16,3328]{1,0:T(8,128)(2,1)S(1)} %slice.173), channel_id=1, source_target_pairs={{0,1},{1,2},{2,3},{3,4},{4,5},{5,6},{6,7},{7,8},{8,9},{9,10},{10,1... | collective-permute-start | bytes 319496 | tf_op jit(solution)/shard_map/ppermute | solution.py:10
  5.6 0.8 select_reduce_fusion
  7.0 1.3 %compare_convert_fusion.1 = (f32[128]{0:T(128)S(1)}, f32[128]{0:T(128)S(1)}, pred[128]{0:T(512)(128)(4,1)S(1)}, pred[128]{0:T(512)(128)(4,1)S(1)}, pred[128]{0:T(512)(128)(4,1)S(1)}) fusion(s32[]{:T(128)} %bitcast.2, s32[144]{0:T(256)S(1)} %compare_select_fusion.1, s32[]{:T(128)} %bitcast.4), kind=kLoop, calls=%fused_computation.130 | loop fusion | flops 896 | bytes 3464 | tf_op jit(solution)/shard_map/convert_element_type | solution.py:109
  8.9 0.8 copy.65
  9.8 1.1 %slice_reduce_fusion.3 = (f32[3328]{0:T(1024)S(1)}, f32[3328]{0:T(1024)S(1)}, f32[3328]{0:T(1024)S(1)}, f32[3328]{0:T(1024)S(1)}) fusion(f32[4,3328]{1,0:T(4,128)} %param.14), kind=kLoop, calls=%fused_computation.124 | loop fusion | bytes 106496 | tf_op jit(solution)/shard_map/slice | solution.py:97
  10.9 0.7 negate_multiply_fusion
  12.8 1.6 %multiply_convert_fusion = bf16[128,3328]{1,0:T(8,128)(2,1)S(1)} fusion(bf16[128,3328]{1,0:T(8,128)(2,1)S(1)} %copy-done, bf16[144,3328]{1,0:T(8,128)(2,1)S(1)} %constant_dynamic-update-slice_fusion, f32[3328]{0:T(1024)S(1)} %get-tuple-element.27, f32[3328]{0:T(1024)S(1)} %get-tuple-element.28, f32[3328]{0:T(1024)S(1)} %get-tuple-element.26, ...), kind=kLoop, calls=%fused_computation.2 | loop fusion | flops 8519680 | bytes 4326784 | tf_op jit(solution)/shard_map/convert_element_type | solution.py:102
  14.4 0.9 copy-done.1
  16.3 1.9 %collective-permute-start.1 = (bf16[128,1792]{1,0:T(8,128)(2,1)S(1)}, bf16[128,1792]{1,0:T(8,128)(2,1)S(1)}, u32[]{:S(2)}, u32[]{:S(2)}) collective-permute-start(bf16[128,1792]{1,0:T(8,128)(2,1)S(1)} %pad_maximum_fusion.1), channel_id=1, source_target_pairs={{0,1},{1,0},{2,3},{3,2},{4,5},{5,4},{6,7},{7,6},{8,9},{9,8},{10,11... | collective-permute-start | bytes 1376264 | tf_op jit(solution)/shard_map/ppermute | solution.py:45
  19.7 1.5 %fusion.70 = f32[128,128]{1,0:T(8,128)} fusion(bf16[128,3328]{1,0:T(8,128)(2,1)} %copy-done.1), kind=kOutput, calls=%fused_computation.116 | convolution fusion | flops 4194304 | bytes 131072 | tf_op jit(solution)/shard_map/dot_general | solution.py:114
  22.3 1.0 %select_add_fusion = (f32[24,64,128]{2,1,0:T(8,128)S(1)}, f32[24,64,128]{2,1,0:T(8,128)S(1)}) fusion(f32[24,64,128]{2,1,0:T(8,128)S(1)} %bitcast.93, f32[24]{0:T(128)S(1)} %get-tuple-element.33, pred[]{:T(512)S(6)} %eq.46, bf16[128,3328]{1,0:T(8,128)(2,1)} %copy-done.1, bf16[128,48,64]{0,2,1:T(8,128)(2,1)S(1)} %fusion), kind=kOutput, calls=%fused_computation.28 | convolution fusion | flops 51314688 | bytes 3179616 | tf_op jit(solution)/shard_map/shp,sn->hpn/dot_general | solution.py:38
  23.3 1.0 %pad_maximum_fusion = f32[1544,128]{1,0:T(8,128)} fusion(f32[8,128]{1,0:T(8,128)S(1)} %pad_bitcast_fusion, f32[1536,128]{1,0:T(8,128)S(1)} %bitcast.108), kind=kLoop, calls=%fused_computation.19 | loop fusion | flops 197632 | bytes 1581056 | tf_op jit(solution)/shard_map/concatenate | solution.py:17
  24.2 5.2 %collective-permute-start.2 = (f32[1544,128]{1,0:T(8,128)}, f32[1544,128]{1,0:T(8,128)S(1)}, u32[]{:S(2)}, u32[]{:S(2)}) collective-permute-start(f32[1544,128]{1,0:T(8,128)} %pad_maximum_fusion), channel_id=1, source_target_pairs={{0,2},{1,3},{2,4},{3,5},{4,6},{5,7},{6,8},{7,9},{8,10},{9,11},{10,... | collective-permute-start | bytes 2371592 | tf_op jit(solution)/shard_map/ppermute | solution.py:64
  29.4 0.9 %slice_bitcast_fusion = (f32[8,128]{0,1:T(8,128)}, f32[8,128]{0,1:T(8,128)}, f32[8,128]{0,1:T(8,128)}, f32[8,128]{0,1:T(8,128)}, f32[8,128]{0,1:T(8,128)}, /*ind...) fusion(f32[128,48]{1,0:T(8,128)S(1)} %get-tuple-element.23, ...), kind=kLoop, calls=%fused_computation.91 | loop fusion | bytes 98304 | tf_op jit(solution)/shard_map/transpose | solution.py:124
  30.4 0.9 %copy.85 = f32[8,128]{1,0:T(8,128)S(1)} copy(f32[8,128]{0,1:T(8,128)} %get-tuple-element.50) | data formatting | bytes 8192 | tf_op jit(solution)/shard_map/transpose | solution.py:124
  31.3 0.9 %copy.82 = f32[8,128]{1,0:T(8,128)S(1)} copy(f32[8,128]{0,1:T(8,128)} %get-tuple-element.51) | data formatting | bytes 8192 | tf_op jit(solution)/shard_map/transpose | solution.py:124
  32.2 0.9 %copy.79 = f32[8,128]{1,0:T(8,128)S(1)} copy(f32[8,128]{0,1:T(8,128)} %get-tuple-element.52) | data formatting | bytes 8192 | tf_op jit(solution)/shard_map/transpose | solution.py:124
  33.1 0.9 %copy.76 = f32[8,128]{1,0:T(8,128)S(1)} copy(f32[8,128]{0,1:T(8,128)} %get-tuple-element.53) | data formatting | bytes 8192 | tf_op jit(solution)/shard_map/transpose | solution.py:124
  34.0 0.9 %copy.73 = f32[8,128]{1,0:T(8,128)S(1)} copy(f32[8,128]{0,1:T(8,128)} %get-tuple-element.54) | data formatting | bytes 8192 | tf_op jit(solution)/shard_map/transpose | solution.py:124
  34.9 0.9 %copy.70 = f32[8,128]{1,0:T(8,128)S(1)} copy(f32[8,128]{0,1:T(8,128)} %get-tuple-element.55) | data formatting | bytes 8192 | tf_op jit(solution)/shard_map/transpose | solution.py:124
  35.8 0.9 %copy.68 = f32[8,128]{1,0:T(8,128)S(1)} copy(f32[8,128]{0,1:T(8,128)} %get-tuple-element.70) | data formatting | bytes 8192 | tf_op jit(solution)/shard_map/transpose | solution.py:120
  36.8 0.9 %copy.71 = f32[8,128]{1,0:T(8,128)S(1)} copy(f32[8,128]{0,1:T(8,128)} %get-tuple-element.71) | data formatting | bytes 8192 | tf_op jit(solution)/shard_map/transpose | solution.py:120
  38.0 1.2 %fusion.7 = f32[128,48,64]{0,2,1:T(8,128)S(1)} fusion(bf16[128,48,64]{0,2,1:T(8,128)(2,1)S(1)} %bitcast.97, f32[8,128]{1,0:T(8,128)S(1)} %copy.70, f32[8,128]{1,0:T(8,128)S(1)} %copy.68, f32[128,128]{1,0:T(8,128)} %fusion.70, pred[128,128]{1,0:T(8,128)(4,1)S(1)} %fusion.60), kind=kOutput, calls=%fused_computation.18 | convolution fusion | flops 17563648 | bytes 1142784 | tf_op jit(solution)/shard_map/hts,shp->thp/dot_general | solution.py:127
  39.6 6.6 %collective-permute-done.2 = f32[1544,128]{1,0:T(8,128)S(1)} collective-permute-done((f32[1544,128]{1,0:T(8,128)}, f32[1544,128]{1,0:T(8,128)S(1)}, u32[]{:S(2)}, u32[]{:S(2)}) %collective-permute-start.2) | collective-permute-done | bytes 790560 | tf_op jit(solution)/shard_map/ppermute | solution.py:64
  46.3 4.0 %collective-permute-start.3 = (bf16[1544,128]{1,0:T(8,128)(2,1)S(1)}, bf16[1544,128]{1,0:T(8,128)(2,1)S(1)}, u32[]{:S(2)}, u32[]{:S(2)}) collective-permute-start(bf16[1544,128]{1,0:T(8,128)(2,1)S(1)} %convert_element_type.88), channel_id=1, source_target_pairs={{0,2},{1,3},{2,4},{3,5},{4,6},{5,7},{6,8},{7,9},{8,10},{9,11},{10,... | collective-permute-start | bytes 1185800 | tf_op jit(solution)/shard_map/ppermute | solution.py:66
  50.7 6.8 %collective-permute-done.3 = bf16[1544,128]{1,0:T(8,128)(2,1)S(1)} collective-permute-done((bf16[1544,128]{1,0:T(8,128)(2,1)S(1)}, bf16[1544,128]{1,0:T(8,128)(2,1)S(1)}, u32[]{:S(2)}, u32[]{:S(2)}) %collective-permute-start.3) | collective-permute-done | bytes 395296 | tf_op jit(solution)/shard_map/ppermute | solution.py:66
  57.7 7.3 %collective-permute-start.4 = (bf16[24,64,128]{2,1,0:T(8,128)(2,1)S(1)}, bf16[24,64,128]{2,1,0:T(8,128)(2,1)S(1)}, u32[]{:S(2)}, u32[]{:S(2)}) collective-permute-start(bf16[24,64,128]{2,1,0:T(8,128)(2,1)S(1)} %fusion.55), channel_id=1, source_target_pairs={{0,4},{1,5},{2,6},{3,7},{4,8},{5,9},{6,10},{7,11},{8,12},{9,13},{1... | collective-permute-start | bytes 1179656 | tf_op jit(solution)/shard_map/ppermute | solution.py:69
  65.5 14.0 %collective-permute-done.4 = bf16[24,64,128]{2,1,0:T(8,128)(2,1)S(1)} collective-permute-done((bf16[24,64,128]{2,1,0:T(8,128)(2,1)S(1)}, bf16[24,64,128]{2,1,0:T(8,128)(2,1)S(1)}, u32[]{:S(2)}, u32[]{:S(2)}) %collective-permute-start.4) | collective-permute-done | bytes 393248 | tf_op jit(solution)/shard_map/ppermute | solution.py:69
  79.8 5.2 %collective-permute-start.5 = (bf16[24,64,128]{2,1,0:T(8,128)(2,1)S(1)}, bf16[24,64,128]{2,1,0:T(8,128)(2,1)S(1)}, u32[]{:S(2)}, u32[]{:S(2)}) collective-permute-start(bf16[24,64,128]{2,1,0:T(8,128)(2,1)S(1)} %get-tuple-element.29), channel_id=1, source_target_pairs={{0,1},{1,0},{2,3},{3,2},{4,5},{5,4},{6,7},{7,6},{8,9},{9,8},{10,11... | collective-permute-start | bytes 1179656 | tf_op jit(solution)/shard_map/ppermute | solution.py:72
  87.1 1.4 %multiply_reduce_fusion = (f32[128,48]{0,1:T(8,128)S(1)}, f32[128,48,64]{0,2,1:T(8,128)S(1)}) fusion(bf16[128,48,64]{0,2,1:T(8,128)(2,1)S(1)} %bitcast.103, f32[48]{0:T(128)S(1)} %copy-done.7, f32[128,48,64]{0,2,1:T(8,128)S(1)} %fusion.2, bf16[24,64,128]{2,1,0:T(8,128)(2,1)S(1)} %get-tuple-element.39, bf16[24,64,128]{2,1,0:T(8,128)(2,1)S(1)} %get-tuple-element.38, ...), kind=kOutput, calls=%fused_computation.6 | convolution fusion | flops 104982528 | bytes 4800704 | tf_op jit(solution)/shard_map/hpn,tn->thp/dot_general | solution.py:139
  89.0 1.2 %copy.87 = bf16[128,3072]{1,0:T(8,128)(2,1)} copy(bf16[128,3072]{0,1:T(8,128)(2,1)S(1)} %bitcast.109) | data formatting | bytes 1572864 | tf_op jit(solution)/shard_map/reshape | solution.py:147
  (67 shorter events, 10.5 us)
Async XLA Ops:
  0.0 12.7 %copy-start = (bf16[128,3328]{1,0:T(8,128)(2,1)S(1)}, bf16[128,3328]{1,0:T(8,128)(2,1)}, u32[]{:S(2)}) copy-start(bf16[128,3328]{1,0:T(8,128)(2,1)} %param.11) | copy-start | bytes 2555908
  0.0 12.8 %copy-start.5 = (f32[3328]{0:T(1024)S(1)}, f32[3328]{0:T(1024)}, u32[]{:S(2)}) copy-start(f32[3328]{0:T(1024)} %param.15) | copy-start | bytes 39940
  1.0 11.7 %collective-permute-start = (bf16[16,3328]{1,0:T(8,128)(2,1)S(1)}, bf16[16,3328]{1,0:T(8,128)(2,1)S(1)}, u32[]{:S(2)}, u32[]{:S(2)}) collective-permute-start(bf16[16,3328]{1,0:T(8,128)(2,1)S(1)} %slice.173), channel_id=1, source_target_pairs={{0,1},{1,2},{2,3},{3,4},{4,5},{5,6},{6,7},{7,8},{8,9},{9,10},{10,1... | collective-permute-start | bytes 319496 | tf_op jit(solution)/shard_map/ppermute | solution.py:10
  14.4 0.9 %copy-start.1 = (bf16[128,3328]{1,0:T(8,128)(2,1)}, bf16[128,3328]{1,0:T(8,128)(2,1)S(1)}, u32[]{:S(2)}) copy-start(bf16[128,3328]{1,0:T(8,128)(2,1)S(1)} %multiply_convert_fusion) | copy-start | bytes 2555908
  16.0 2.3 %copy-start.6 = (f32[3072]{0:T(1024)S(1)}, f32[3072]{0:T(1024)}, u32[]{:S(2)}) copy-start(f32[3072]{0:T(1024)} %param.19) | copy-start | bytes 36868
  16.3 4.9 %collective-permute-start.1 = (bf16[128,1792]{1,0:T(8,128)(2,1)S(1)}, bf16[128,1792]{1,0:T(8,128)(2,1)S(1)}, u32[]{:S(2)}, u32[]{:S(2)}) collective-permute-start(bf16[128,1792]{1,0:T(8,128)(2,1)S(1)} %pad_maximum_fusion.1), channel_id=1, source_target_pairs={{0,1},{1,0},{2,3},{3,2},{4,5},{5,4},{6,7},{7,6},{8,9},{9,8},{10,11... | collective-permute-start | bytes 1376264 | tf_op jit(solution)/shard_map/ppermute | solution.py:45
  24.2 22.0 %collective-permute-start.2 = (f32[1544,128]{1,0:T(8,128)}, f32[1544,128]{1,0:T(8,128)S(1)}, u32[]{:S(2)}, u32[]{:S(2)}) collective-permute-start(f32[1544,128]{1,0:T(8,128)} %pad_maximum_fusion), channel_id=1, source_target_pairs={{0,2},{1,3},{2,4},{3,5},{4,6},{5,7},{6,8},{7,9},{8,10},{9,11},{10,... | collective-permute-start | bytes 2371592 | tf_op jit(solution)/shard_map/ppermute | solution.py:64
  30.4 8.9 %copy-start.4 = (f32[128,128]{1,0:T(8,128)S(1)}, f32[128,128]{1,0:T(8,128)}, u32[]{:S(2)}) copy-start(f32[128,128]{1,0:T(8,128)} %fusion.70) | copy-start | bytes 196612
  46.3 11.2 %collective-permute-start.3 = (bf16[1544,128]{1,0:T(8,128)(2,1)S(1)}, bf16[1544,128]{1,0:T(8,128)(2,1)S(1)}, u32[]{:S(2)}, u32[]{:S(2)}) collective-permute-start(bf16[1544,128]{1,0:T(8,128)(2,1)S(1)} %convert_element_type.88), channel_id=1, source_target_pairs={{0,2},{1,3},{2,4},{3,5},{4,6},{5,7},{6,8},{7,9},{8,10},{9,11},{10,... | collective-permute-start | bytes 1185800 | tf_op jit(solution)/shard_map/ppermute | solution.py:66
  57.7 21.7 %collective-permute-start.4 = (bf16[24,64,128]{2,1,0:T(8,128)(2,1)S(1)}, bf16[24,64,128]{2,1,0:T(8,128)(2,1)S(1)}, u32[]{:S(2)}, u32[]{:S(2)}) collective-permute-start(bf16[24,64,128]{2,1,0:T(8,128)(2,1)S(1)} %fusion.55), channel_id=1, source_target_pairs={{0,4},{1,5},{2,6},{3,7},{4,8},{5,9},{6,10},{7,11},{8,12},{9,13},{1... | collective-permute-start | bytes 1179656 | tf_op jit(solution)/shard_map/ppermute | solution.py:69
  79.8 6.5 %collective-permute-start.5 = (bf16[24,64,128]{2,1,0:T(8,128)(2,1)S(1)}, bf16[24,64,128]{2,1,0:T(8,128)(2,1)S(1)}, u32[]{:S(2)}, u32[]{:S(2)}) collective-permute-start(bf16[24,64,128]{2,1,0:T(8,128)(2,1)S(1)} %get-tuple-element.29), channel_id=1, source_target_pairs={{0,1},{1,0},{2,3},{3,2},{4,5},{5,4},{6,7},{7,6},{8,9},{9,8},{10,11... | collective-permute-start | bytes 1179656 | tf_op jit(solution)/shard_map/ppermute | solution.py:72
  86.3 0.7 copy-start.3
  86.3 0.7 copy-start.7
  87.1 1.4 %copy-start.2 = (f32[48,64]{1,0:T(8,128)S(1)}, f32[48,64]{1,0:T(8,128)}, u32[]{:S(2)}) copy-start(f32[48,64]{1,0:T(8,128)} %mul.333) | copy-start | bytes 36868

commit v13 on v12

--- a/solution.py
+++ b/solution.py
@@ -32,18 +32,19 @@
     rows = scaled.shape[0]
     width = half * scaled.shape[2]
     swap = [(2 * i + j, 2 * i + 1 - j) for i in range(chips) for j in range(2)]
-    front, back = scaled[:, :half], scaled[:, half:]
+    flat = scaled.reshape(rows, 2 * width)
+    front, back = flat[:, :width], flat[:, width:]
     mine_x = jnp.where(low, front, back)
     theirs_x = jnp.where(low, back, front)
-    mine = jnp.einsum("shp,sn->hpn", mine_x, bs, preferred_element_type=jnp.float32)
-    rest = mine.shape[1:]
+    rest = scaled.shape[2:] + bs.shape[1:]
+    mine = jnp.einsum("sk,sn->kn", mine_x, bs, preferred_element_type=jnp.float32).reshape((half,) + rest)
     top = lax.reduce_precision(decay, exponent_bits=8, mantissa_bits=7)
     middle = lax.reduce_precision(decay - top, exponent_bits=8, mantissa_bits=7)
     bottom = lax.reduce_precision(decay - top - middle, exponent_bits=8, mantissa_bits=7)
     split = jnp.stack([top, middle, bottom]).astype(jnp.bfloat16)
     pieces = jnp.zeros((rows, bs.shape[1]), jnp.bfloat16).at[:3, :heads].set(split)
     got = lax.ppermute(
-        jnp.concatenate([theirs_x.reshape(rows, width), bs, pieces], axis=1), "ctx", swap
+        jnp.concatenate([theirs_x, bs, pieces], axis=1), "ctx", swap
     )
     got_x = got[:, :width]
     got_b = got[:, width : width + bs.shape[1]]

time: 91.2 us -> 94 us (1.031)
  the two profiles are of different devices: /device:TPU:183 before, /device:TPU:189 now
where the time goes in v13:
time: 94 us; the launch traced here: 93 us
  starting transfers between devices  28.2 us (30%)
  waiting for transfers between devices  26.9 us (29%)
  local copies, waits for them, and re-layouts  22 us (23%)
  other arithmetic  9.37 us (10%)
  matrix products  6.11 us (6%)
    ppermute x1, waiting for transfers between devices, chain_carry(): lax.ppermute(local_ab.astype(jnp.bfloat16), 'ctx', two).astype(jnp.float32)  14 us
    ppermute x1, starting transfers between devices, chain_carry(): lax.ppermute(local_ab.astype(jnp.bfloat16), 'ctx', two).astype(jnp.float32)  7.35 us
    ppermute x1, waiting for transfers between devices, chain_carry(): lax.ppermute(first_hop.astype(jnp.bfloat16), 'ctx', one).astype(jnp.float32)  6.75 us
    transpose x7, local copies, waits for them, and re-layouts, body(): step_late[:, part_start:part_start + group].T[:, None, :]  6.5 us
    ppermute x1, waiting for transfers between devices, chain_carry(): first_hop = lax.ppermute(sent, 'ctx', one)  5.58 us
    ppermute x1, starting transfers between devices, chain_carry(): first_hop = lax.ppermute(sent, 'ctx', one)  5.2 us
    ppermute x1, starting transfers between devices, chain_carry(): got_end = lax.ppermute(jnp.where(low, onward, carry_half), 'ctx', swap)  5.19 us
    ppermute x1, starting transfers between devices, shifted(): return lax.ppermute(block, axis, route)  4.55 us
  transfers between devices with their start and end apart: 6, of which 4 were waited for; matrix products, arithmetic and copies ran while one was open for 28% of the time, Pallas kernels for 0%

profile of v13, /device:TPU:189, one launch (start us, length us, event | category | flops | bytes accessed | tf_op | source)
XLA Modules:
  0.0 93.0 jit_solution(12701145379831246502)
XLA Ops:
  0.0 0.9 slice.173
  0.9 4.5 %collective-permute-start = (bf16[16,3328]{1,0:T(8,128)(2,1)S(1)}, bf16[16,3328]{1,0:T(8,128)(2,1)S(1)}, u32[]{:S(2)}, u32[]{:S(2)}) collective-permute-start(bf16[16,3328]{1,0:T(8,128)(2,1)S(1)} %slice.173), channel_id=1, source_target_pairs={{0,1},{1,2},{2,3},{3,4},{4,5},{5,6},{6,7},{7,8},{8,9},{9,10},{10,1... | collective-permute-start | bytes 319496 | tf_op jit(solution)/shard_map/ppermute | solution.py:10
  6.9 1.3 %compare_convert_fusion.1 = (f32[128]{0:T(128)S(1)}, f32[128]{0:T(128)S(1)}, pred[128]{0:T(512)(128)(4,1)S(1)}, pred[128]{0:T(512)(128)(4,1)S(1)}, pred[128]{0:T(512)(128)(4,1)S(1)}) fusion(s32[]{:T(128)} %bitcast.2, s32[144]{0:T(256)S(1)} %compare_select_fusion.1, s32[]{:T(128)} %bitcast.4), kind=kLoop, calls=%fused_computation.127 | loop fusion | flops 896 | bytes 3464 | tf_op jit(solution)/shard_map/convert_element_type | solution.py:110
  8.8 0.8 copy.57
  9.6 1.1 %slice_reduce_fusion.3 = (f32[3328]{0:T(1024)S(1)}, f32[3328]{0:T(1024)S(1)}, f32[3328]{0:T(1024)S(1)}, f32[3328]{0:T(1024)S(1)}) fusion(f32[4,3328]{1,0:T(4,128)} %param.14), kind=kLoop, calls=%fused_computation.121 | loop fusion | bytes 106496 | tf_op jit(solution)/shard_map/slice | solution.py:98
  12.5 1.3 %mul.297 = f32[128,48,64]{0,2,1:T(8,128)} broadcast(f32[128,48]{0,1:T(8,128)S(1)} %copy.58), dimensions={0,1} | broadcast | bytes 1597440 | tf_op jit(solution)/shard_map/mul | solution.py:112
  13.8 1.9 %copy.59 = f32[128,3072]{1,0:T(8,128)S(1)} copy(f32[128,3072]{0,1:T(8,128)} %bitcast.93) | data formatting | bytes 3145728 | tf_op jit(solution)/shard_map/mul | solution.py:112
  15.9 1.0 %copy-done.1 = bf16[128,3328]{1,0:T(8,128)(2,1)S(1)} copy-done((bf16[128,3328]{1,0:T(8,128)(2,1)S(1)}, bf16[128,3328]{1,0:T(8,128)(2,1)}, u32[]{:S(2)}) %copy-start.1) | copy-done | bytes 851992
  16.9 1.6 %multiply_convert_fusion = bf16[128,3328]{1,0:T(8,128)(2,1)S(1)} fusion(bf16[128,3328]{1,0:T(8,128)(2,1)S(1)} %copy-done.1, bf16[144,3328]{1,0:T(8,128)(2,1)S(1)} %constant_dynamic-update-slice_fusion, f32[3328]{0:T(1024)S(1)} %get-tuple-element.27, f32[3328]{0:T(1024)S(1)} %get-tuple-element.28, f32[3328]{0:T(1024)S(1)} %get-tuple-element.26, ...), kind=kLoop, calls=%fused_computation | loop fusion | flops 8519680 | bytes 4326784 | tf_op jit(solution)/shard_map/convert_element_type | solution.py:103
  18.8 1.9 %collective-permute-start.1 = (bf16[128,1792]{1,0:T(8,128)(2,1)S(1)}, bf16[128,1792]{1,0:T(8,128)(2,1)}, u32[]{:S(2)}, u32[]{:S(2)}) collective-permute-start(bf16[128,1792]{1,0:T(8,128)(2,1)S(1)} %pad_maximum_fusion.1), channel_id=1, source_target_pairs={{0,1},{1,0},{2,3},{3,2},{4,5},{5,4},{6,7},{7,6},{8,9},{9,8},{10,11... | collective-permute-start | bytes 1376264 | tf_op jit(solution)/shard_map/ppermute | solution.py:46
  22.2 1.2 %copy.56 = bf16[128,3072]{0,1:T(8,128)(2,1)} copy(bf16[128,3072]{1,0:T(8,128)(2,1)S(1)} %slice.221) | data formatting | bytes 1572864 | tf_op jit(solution)/shard_map/slice | solution.py:104
  25.7 1.3 %fusion.10 = f32[1536,128]{1,0:T(8,128)S(1)} fusion(bf16[128,1792]{1,0:T(8,128)(2,1)} %collective-permute-done.1), kind=kOutput, calls=%fused_computation.35 | convolution fusion | flops 50331648 | bytes 1212416 | tf_op jit(solution)/shard_map/sk,sn->kn/dot_general | solution.py:53
  27.4 0.9 %pad_maximum_fusion = f32[1544,128]{1,0:T(8,128)} fusion(f32[8,128]{1,0:T(8,128)S(1)} %pad_bitcast_fusion, f32[1536,128]{1,0:T(8,128)S(1)} %get-tuple-element.39), kind=kLoop, calls=%fused_computation.17 | loop fusion | flops 197632 | bytes 1581056 | tf_op jit(solution)/shard_map/concatenate | solution.py:17
  28.3 5.2 %collective-permute-start.2 = (f32[1544,128]{1,0:T(8,128)}, f32[1544,128]{1,0:T(8,128)S(1)}, u32[]{:S(2)}, u32[]{:S(2)}) collective-permute-start(f32[1544,128]{1,0:T(8,128)} %pad_maximum_fusion), channel_id=1, source_target_pairs={{0,2},{1,3},{2,4},{3,5},{4,6},{5,7},{6,8},{7,9},{8,10},{9,11},{10,... | collective-permute-start | bytes 2371592 | tf_op jit(solution)/shard_map/ppermute | solution.py:65
  33.5 1.0 %slice_bitcast_fusion = (f32[8,128]{0,1:T(8,128)}, f32[8,128]{0,1:T(8,128)}, f32[8,128]{0,1:T(8,128)}, f32[8,128]{0,1:T(8,128)}, f32[8,128]{0,1:T(8,128)}, /*ind...) fusion(f32[128,48]{1,0:T(8,128)S(1)} %get-tuple-element.23, ...), kind=kLoop, calls=%fused_computation.89 | loop fusion | bytes 98304 | tf_op jit(solution)/shard_map/transpose | solution.py:125
  34.5 1.0 %copy.77 = f32[8,128]{1,0:T(8,128)S(1)} copy(f32[8,128]{0,1:T(8,128)} %get-tuple-element.52) | data formatting | bytes 8192 | tf_op jit(solution)/shard_map/transpose | solution.py:125
  35.5 0.9 copy.74
  36.4 0.9 copy.71
  37.3 0.9 copy.68
  38.2 0.9 copy.65
  39.1 0.9 copy.62
  40.0 0.9 copy.60
  40.9 0.9 copy.63
  41.8 0.9 copy.66
  43.1 1.3 %fusion.5 = f32[128,48,64]{0,2,1:T(8,128)S(1)} fusion(bf16[128,48,64]{0,2,1:T(8,128)(2,1)} %bitcast.94, f32[8,128]{1,0:T(8,128)S(1)} %copy.62, f32[8,128]{1,0:T(8,128)S(1)} %copy.60, f32[128,128]{1,0:T(8,128)} %fusion.67, pred[128,128]{1,0:T(8,128)(4,1)S(1)} %fusion.58), kind=kOutput, calls=%fused_computation.16 | convolution fusion | flops 17563648 | bytes 1142784 | tf_op jit(solution)/shard_map/hts,shp->thp/dot_general | solution.py:128
  44.7 5.6 %collective-permute-done.2 = f32[1544,128]{1,0:T(8,128)S(1)} collective-permute-done((f32[1544,128]{1,0:T(8,128)}, f32[1544,128]{1,0:T(8,128)S(1)}, u32[]{:S(2)}, u32[]{:S(2)}) %collective-permute-start.2) | collective-permute-done | bytes 790560 | tf_op jit(solution)/shard_map/ppermute | solution.py:65
  50.3 4.0 %collective-permute-start.3 = (bf16[1544,128]{1,0:T(8,128)(2,1)S(1)}, bf16[1544,128]{1,0:T(8,128)(2,1)S(1)}, u32[]{:S(2)}, u32[]{:S(2)}) collective-permute-start(bf16[1544,128]{1,0:T(8,128)(2,1)S(1)} %convert_element_type.92), channel_id=1, source_target_pairs={{0,2},{1,3},{2,4},{3,5},{4,6},{5,7},{6,8},{7,9},{8,10},{9,11},{10,... | collective-permute-start | bytes 1185800 | tf_op jit(solution)/shard_map/ppermute | solution.py:67
  54.8 6.8 %collective-permute-done.3 = bf16[1544,128]{1,0:T(8,128)(2,1)S(1)} collective-permute-done((bf16[1544,128]{1,0:T(8,128)(2,1)S(1)}, bf16[1544,128]{1,0:T(8,128)(2,1)S(1)}, u32[]{:S(2)}, u32[]{:S(2)}) %collective-permute-start.3) | collective-permute-done | bytes 395296 | tf_op jit(solution)/shard_map/ppermute | solution.py:67
  61.8 7.3 %collective-permute-start.4 = (bf16[24,64,128]{2,1,0:T(8,128)(2,1)S(1)}, bf16[24,64,128]{2,1,0:T(8,128)(2,1)S(1)}, u32[]{:S(2)}, u32[]{:S(2)}) collective-permute-start(bf16[24,64,128]{2,1,0:T(8,128)(2,1)S(1)} %fusion.53), channel_id=1, source_target_pairs={{0,4},{1,5},{2,6},{3,7},{4,8},{5,9},{6,10},{7,11},{8,12},{9,13},{1... | collective-permute-start | bytes 1179656 | tf_op jit(solution)/shard_map/ppermute | solution.py:70
  69.5 14.0 %collective-permute-done.4 = bf16[24,64,128]{2,1,0:T(8,128)(2,1)S(1)} collective-permute-done((bf16[24,64,128]{2,1,0:T(8,128)(2,1)S(1)}, bf16[24,64,128]{2,1,0:T(8,128)(2,1)S(1)}, u32[]{:S(2)}, u32[]{:S(2)}) %collective-permute-start.4) | collective-permute-done | bytes 393248 | tf_op jit(solution)/shard_map/ppermute | solution.py:70
  83.8 5.2 %collective-permute-start.5 = (bf16[24,64,128]{2,1,0:T(8,128)(2,1)S(1)}, bf16[24,64,128]{2,1,0:T(8,128)(2,1)S(1)}, u32[]{:S(2)}, u32[]{:S(2)}) collective-permute-start(bf16[24,64,128]{2,1,0:T(8,128)(2,1)S(1)} %get-tuple-element.29), channel_id=1, source_target_pairs={{0,1},{1,0},{2,3},{3,2},{4,5},{5,4},{6,7},{7,6},{8,9},{9,8},{10,11... | collective-permute-start | bytes 1179656 | tf_op jit(solution)/shard_map/ppermute | solution.py:73
  91.9 1.2 %copy.79 = bf16[128,3072]{1,0:T(8,128)(2,1)} copy(bf16[128,3072]{0,1:T(8,128)(2,1)S(1)} %bitcast.101) | data formatting | bytes 1572864 | tf_op jit(solution)/shard_map/reshape | solution.py:148
  (72 shorter events, 13.1 us)
Async XLA Ops:
  0.9 14.9 %collective-permute-start = (bf16[16,3328]{1,0:T(8,128)(2,1)S(1)}, bf16[16,3328]{1,0:T(8,128)(2,1)S(1)}, u32[]{:S(2)}, u32[]{:S(2)}) collective-permute-start(bf16[16,3328]{1,0:T(8,128)(2,1)S(1)} %slice.173), channel_id=1, source_target_pairs={{0,1},{1,2},{2,3},{3,4},{4,5},{5,6},{6,7},{7,8},{8,9},{9,10},{10,1... | collective-permute-start | bytes 319496 | tf_op jit(solution)/shard_map/ppermute | solution.py:10
  13.8 2.0 %copy-start = (bf16[128,3328]{1,0:T(8,128)(2,1)S(1)}, bf16[128,3328]{1,0:T(8,128)(2,1)}, u32[]{:S(2)}) copy-start(bf16[128,3328]{1,0:T(8,128)(2,1)} %param.11) | copy-start | bytes 2555908
  15.7 1.2 %copy-start.1 = (bf16[128,3328]{1,0:T(8,128)(2,1)S(1)}, bf16[128,3328]{1,0:T(8,128)(2,1)}, u32[]{:S(2)}) copy-start(bf16[128,3328]{1,0:T(8,128)(2,1)} %param.11) | copy-start | bytes 2555908
  15.7 1.1 %copy-start.6 = (f32[3328]{0:T(1024)S(1)}, f32[3328]{0:T(1024)}, u32[]{:S(2)}) copy-start(f32[3328]{0:T(1024)} %param.15) | copy-start | bytes 39940
  18.7 2.1 %copy-start.7 = (f32[3072]{0:T(1024)S(1)}, f32[3072]{0:T(1024)}, u32[]{:S(2)}) copy-start(f32[3072]{0:T(1024)} %param.19) | copy-start | bytes 36868
  18.8 5.4 %collective-permute-start.1 = (bf16[128,1792]{1,0:T(8,128)(2,1)S(1)}, bf16[128,1792]{1,0:T(8,128)(2,1)}, u32[]{:S(2)}, u32[]{:S(2)}) collective-permute-start(bf16[128,1792]{1,0:T(8,128)(2,1)S(1)} %pad_maximum_fusion.1), channel_id=1, source_target_pairs={{0,1},{1,0},{2,3},{3,2},{4,5},{5,4},{6,7},{7,6},{8,9},{9,8},{10,11... | collective-permute-start | bytes 1376264 | tf_op jit(solution)/shard_map/ppermute | solution.py:46
  28.3 22.0 %collective-permute-start.2 = (f32[1544,128]{1,0:T(8,128)}, f32[1544,128]{1,0:T(8,128)S(1)}, u32[]{:S(2)}, u32[]{:S(2)}) collective-permute-start(f32[1544,128]{1,0:T(8,128)} %pad_maximum_fusion), channel_id=1, source_target_pairs={{0,2},{1,3},{2,4},{3,5},{4,6},{5,7},{6,8},{7,9},{8,10},{9,11},{10,... | collective-permute-start | bytes 2371592 | tf_op jit(solution)/shard_map/ppermute | solution.py:65
  34.5 9.8 %copy-start.2 = (bf16[128,3072]{0,1:T(8,128)(2,1)S(1)}, bf16[128,3072]{0,1:T(8,128)(2,1)}, u32[]{:S(2)}) copy-start(bf16[128,3072]{0,1:T(8,128)(2,1)} %copy.56) | copy-start | bytes 2359300
  34.5 9.8 %copy-start.5 = (f32[128,128]{1,0:T(8,128)S(1)}, f32[128,128]{1,0:T(8,128)}, u32[]{:S(2)}) copy-start(f32[128,128]{1,0:T(8,128)} %fusion.67) | copy-start | bytes 196612
  50.3 11.2 %collective-permute-start.3 = (bf16[1544,128]{1,0:T(8,128)(2,1)S(1)}, bf16[1544,128]{1,0:T(8,128)(2,1)S(1)}, u32[]{:S(2)}, u32[]{:S(2)}) collective-permute-start(bf16[1544,128]{1,0:T(8,128)(2,1)S(1)} %convert_element_type.92), channel_id=1, source_target_pairs={{0,2},{1,3},{2,4},{3,5},{4,6},{5,7},{6,8},{7,9},{8,10},{9,11},{10,... | collective-permute-start | bytes 1185800 | tf_op jit(solution)/shard_map/ppermute | solution.py:67
  61.8 21.8 %collective-permute-start.4 = (bf16[24,64,128]{2,1,0:T(8,128)(2,1)S(1)}, bf16[24,64,128]{2,1,0:T(8,128)(2,1)S(1)}, u32[]{:S(2)}, u32[]{:S(2)}) collective-permute-start(bf16[24,64,128]{2,1,0:T(8,128)(2,1)S(1)} %fusion.53), channel_id=1, source_target_pairs={{0,4},{1,5},{2,6},{3,7},{4,8},{5,9},{6,10},{7,11},{8,12},{9,13},{1... | collective-permute-start | bytes 1179656 | tf_op jit(solution)/shard_map/ppermute | solution.py:70
  83.8 6.5 %collective-permute-start.5 = (bf16[24,64,128]{2,1,0:T(8,128)(2,1)S(1)}, bf16[24,64,128]{2,1,0:T(8,128)(2,1)S(1)}, u32[]{:S(2)}, u32[]{:S(2)}) collective-permute-start(bf16[24,64,128]{2,1,0:T(8,128)(2,1)S(1)} %get-tuple-element.29), channel_id=1, source_target_pairs={{0,1},{1,0},{2,3},{3,2},{4,5},{5,4},{6,7},{7,6},{8,9},{9,8},{10,11... | collective-permute-start | bytes 1179656 | tf_op jit(solution)/shard_map/ppermute | solution.py:73
  89.8 0.8 copy-start.4
  89.8 0.8 copy-start.8
  90.6 0.7 copy-start.3
